TPU v7x, 512 devices: a whole 4x8x8 slice. The times are simulated.
512 devices in a mesh: row: 16 (over y, x_lo), col: 16 (over z, core), ka: 2 (over x_hi).
Axes of the slice: x: 4 (x_hi: 2, x_lo: 2; x = x_hi * 2 + x_lo), y: 8, z: 8, core: 2. Of those that a mesh axis runs over, the one named last changes fastest.
Arguments:
- pair: bfloat16 [512, 512, 128], P('row', ('col', 'ka')), may hold values from -6 to 6
- pair_mask: int32 [512, 512], P('row', ('col', 'ka')), may hold values from 0 to 1, as said below
- w_in: bfloat16 [2, 128, 512], replicated, may hold values from -0.5 to 0.5
- w_gate: bfloat16 [2, 128, 128], replicated, may hold values from -0.5 to 0.5
- w_out: bfloat16 [2, 128, 128], replicated, may hold values from -0.5 to 0.5
Outputs:
- updated: bfloat16 [512, 512, 128], P('row', ('col', 'ka'))
Inputs may be any that keep to these rules, and one draw needn't show every extreme that they name: pair_mask[i, j] = v[i] v[j] for a per-token 0/1 validity v; within each aligned run of 16 tokens the real tokens come first and there is at least one.
All inputs are finite; a program needn't handle non-finite values.
Results may differ from a plain program's by a relative error of at most 0.014.
Values may be sent and summed in bfloat16 or wider, within the bound.
No kernel may reach another device: no remote copies, remote signals or barrier semaphores. Data moves between devices by JAX's collectives and lax.ppermute only.
A program may use at most 64 MiB of HBM per device.

v0:
```python
import jax
import jax.numpy as jnp
from jax import lax
from jax.sharding import PartitionSpec as P


def from_root(value, axis, source):
    kept = jnp.where(lax.axis_index(axis) == source, value, 0).astype(value.dtype)
    return lax.psum(kept, axis)


def layer_norm(value):
    mean = jnp.mean(value, axis=-1, keepdims=True)
    centred = value - mean
    var = jnp.mean(centred * centred, axis=-1, keepdims=True)
    return centred / jnp.sqrt(var + 1e-05)


def prepare(pair, valid, weight_in, weight_gate):
    normed = layer_norm(pair.astype(jnp.float32)).astype(jnp.bfloat16)
    proj = jnp.einsum("ijc,cd->ijd", normed, weight_in, preferred_element_type=jnp.float32)
    width = proj.shape[-1] // 4
    left = (jax.nn.sigmoid(proj[..., :width]) * proj[..., width : 2 * width] * valid).astype(
        jnp.bfloat16
    )
    right = (
        jax.nn.sigmoid(proj[..., 2 * width : 3 * width]) * proj[..., 3 * width :] * valid
    ).astype(jnp.bfloat16)
    gate = jax.nn.sigmoid(
        jnp.einsum("ijc,cd->ijd", normed, weight_gate, preferred_element_type=jnp.float32)
    )
    return (left, right, gate)


def finish(pair, tri, gate, weight_out):
    normed = layer_norm(tri).astype(jnp.bfloat16)
    proj = jnp.einsum("ijc,cd->ijd", normed, weight_out, preferred_element_type=jnp.float32)
    return (pair.astype(jnp.float32) + gate * proj).astype(jnp.bfloat16)


def on_device(pair, pair_mask, w_in, w_gate, w_out):
    valid = pair_mask.astype(jnp.float32)[..., None]
    left, right, gate = prepare(pair, valid, w_in[0], w_gate[0])
    left_rows, right_rows = (
        lax.all_gather(left, "col", axis=1, tiled=True),
        lax.all_gather(right, "col", axis=1, tiled=True),
    )
    right_diag = from_root(right_rows, "row", lax.axis_index("col"))
    partial_value = jnp.einsum(
        "ikc,jkc->ijc", left_rows, right_diag, preferred_element_type=jnp.float32
    )
    tri = lax.psum_scatter(
        partial_value.astype(jnp.bfloat16), "ka", scatter_dimension=1, tiled=True
    ).astype(jnp.float32)
    middle = finish(pair, tri, gate, w_out[0])
    left, right, gate = prepare(middle, valid, w_in[1], w_gate[1])
    left_cols, right_cols = (
        lax.all_gather(left, "row", axis=0, tiled=True),
        lax.all_gather(right, "row", axis=0, tiled=True),
    )
    left_wide = lax.all_gather(left_cols, "ka", axis=1, tiled=True)
    left_diag = from_root(left_wide, "col", lax.axis_index("row"))
    tri = jnp.einsum("kic,kjc->ijc", left_diag, right_cols, preferred_element_type=jnp.float32)
    return finish(middle, tri, gate, w_out[1])


def solution(mesh):
    placed = (P("row", ("col", "ka"), None), P("row", ("col", "ka")), P(), P(), P())
    return jax.shard_map(
        on_device,
        mesh=mesh,
        in_specs=placed,
        out_specs=P("row", ("col", "ka"), None),
        check_vma=False,
    )
```

profile of v0, /device:TPU:1, one launch (start us, length us, event | category | flops | bytes accessed | tf_op | source)
XLA Modules:
  0.0 666.7 jit_solution(9475400611187420991)
XLA Ops:
  6.5 1.0 convert_reduce_fusion.1
  7.7 1.1 fusion.18
  9.8 1.3 fusion.42
  11.2 0.9 fusion.31
  12.9 49.2 %all-gather.6.cloned.1.call-done = bf16[32,256,128]{2,1,0:T(8,128)(2,1)} async-done(((bf16[32,16,128]{2,1,0:T(8,128)(2,1)}), bf16[32,256,128]{2,1,0:T(8,128)(2,1)}) %all-gather.6.cloned.1.call-update) | async-done | bytes 2097168 | tf_op jit(solution)/shard_map/all_gather | solution.py:46
  62.0 1.4 broadcast_select_fusion.1
  63.6 43.2 %all-gather.8.cloned.1.call-done = bf16[32,256,128]{2,1,0:T(8,128)(2,1)} async-done(((bf16[32,16,128]{2,1,0:T(8,128)(2,1)}), bf16[32,256,128]{2,1,0:T(8,128)(2,1)}) %all-gather.8.cloned.1.call-update) | async-done | bytes 2097168 | tf_op jit(solution)/shard_map/all_gather | solution.py:45
  106.8 15.2 %copy.49 = bf16[32,256,128]{0,1,2:T(8,128)(2,1)} copy(bf16[32,256,128]{2,1,0:T(8,128)(2,1)} %all-gather.8.cloned.1.call-done) | data formatting | bytes 4194304 | tf_op jit(solution)/shard_map/all_gather | solution.py:45
  122.0 128.2 %all-reduce.3.cloned.1.call-done = bf16[32,256,128]{2,1,0:T(8,128)(2,1)} async-done(((bf16[32,256,128]{2,1,0:T(8,128)(2,1)}), bf16[32,256,128]{2,1,0:T(8,128)(2,1)}) %all-reduce.3.cloned.1.call-update) | async-done | bytes 2097168 | tf_op jit(solution)/shard_map/psum | solution.py:9
  250.2 3.4 copy.48
  253.6 5.8 fusion
  259.9 37.9 %reduce-scatter.2.cloned.1.call-done = bf16[32,16,128]{0,1,2:T(8,128)(2,1)} async-done(((bf16[32,32,128]{0,1,2:T(8,128)(2,1)}), bf16[32,16,128]{0,1,2:T(8,128)(2,1)}) %reduce-scatter.2.cloned.1.call-update) | async-done | bytes 131088 | tf_op jit(solution)/shard_map/reduce_scatter | solution.py:52
  297.8 1.2 convert_reduce_fusion
  299.0 1.3 fusion.14
  300.3 1.2 fusion.15
  303.2 0.9 fusion.21
  304.2 64.7 %all-gather.12.cloned.1.call-done = bf16[512,16,128]{2,1,0:T(8,128)(2,1)} async-done(((bf16[32,16,128]{2,1,0:T(8,128)(2,1)}), bf16[512,16,128]{2,1,0:T(8,128)(2,1)}) %all-gather.12.cloned.1.call-update) | async-done | bytes 2097168 | tf_op jit(solution)/shard_map/all_gather | solution.py:58
  368.9 5.0 copy.55
  374.7 74.4 %all-gather.14.cloned.1.call-done = bf16[512,32,128]{0,1,2:T(8,128)(2,1)} async-done(((bf16[512,16,128]{0,1,2:T(8,128)(2,1)}), bf16[512,32,128]{0,1,2:T(8,128)(2,1)}) %all-gather.14.cloned.1.call-update) | async-done | bytes 4194320 | tf_op jit(solution)/shard_map/all_gather | solution.py:61
  449.1 2.2 broadcast_select_fusion
  451.7 64.2 %all-gather.10.cloned.1.call-done = bf16[512,16,128]{2,1,0:T(8,128)(2,1)} async-done(((bf16[32,16,128]{2,1,0:T(8,128)(2,1)}), bf16[512,16,128]{2,1,0:T(8,128)(2,1)}) %all-gather.10.cloned.1.call-update) | async-done | bytes 2097168 | tf_op jit(solution)/shard_map/all_gather | solution.py:59
  515.8 3.9 copy.56
  519.8 135.0 %all-reduce.5.cloned.1.call-done = bf16[512,32,128]{0,1,2:T(8,128)(2,1)} async-done(((bf16[512,32,128]{0,1,2:T(8,128)(2,1)}), bf16[512,32,128]{0,1,2:T(8,128)(2,1)}) %all-reduce.5.cloned.1.call-update) | async-done | bytes 4194320 | tf_op jit(solution)/shard_map/psum | solution.py:9
  654.8 3.4 fusion.57
  (52 shorter events, 7.0 us)
Async XLA Ops:
  6.5 55.5 %all-gather.6.cloned.1.call-start = ((), (), s32[]{:S(2)}) async-start(), calls=%async_computation.1 | async-start | bytes 2228224 | tf_op jit(solution)/shard_map/all_gather | solution.py:46
  12.1 94.7 %all-gather.8.cloned.1.call-start = ((), (), s32[]{:S(2)}) async-start(), calls=%async_computation.3 | async-start | bytes 2228224 | tf_op jit(solution)/shard_map/all_gather | solution.py:45
  12.8 237.4 %all-reduce.3.cloned.1.call-start = ((), (), s32[]{:S(2)}) async-start(), calls=%async_computation.2 | async-start | bytes 4194304 | tf_op jit(solution)/shard_map/psum | solution.py:9
  63.5 234.3 %reduce-scatter.2.cloned.1.call-start = ((), (), s32[]{:S(2)}) async-start(), calls=%async_computation.4 | async-start | bytes 1572864 | tf_op jit(solution)/shard_map/reduce_scatter | solution.py:52
  253.6 5.9 copy-start
  253.6 5.9 copy-start.3
  259.5 42.5 %copy-start.2 = (bf16[2,128,128]{2,1,0:T(8,128)(2,1)S(1)}, bf16[2,128,128]{2,1,0:T(8,128)(2,1)}, u32[]{:S(2)}) copy-start(bf16[2,128,128]{2,1,0:T(8,128)(2,1)} %param.9) | copy-start | bytes 196612
  259.5 109.4 %all-gather.12.cloned.1.call-start = ((), (), s32[]{:S(2)}) async-start(), calls=%async_computation.6 | async-start | bytes 2228224 | tf_op jit(solution)/shard_map/all_gather | solution.py:58
  259.9 43.0 %copy-start.1 = (bf16[2,128,512]{2,1,0:T(8,128)(2,1)S(1)}, bf16[2,128,512]{2,1,0:T(8,128)(2,1)}, u32[]{:S(2)}) copy-start(bf16[2,128,512]{2,1,0:T(8,128)(2,1)} %param.7) | copy-start | bytes 786436
  304.1 145.0 %all-gather.14.cloned.1.call-start = ((), (), s32[]{:S(2)}) async-start(), calls=%async_computation.7 | async-start | bytes 6291456 | tf_op jit(solution)/shard_map/all_gather | solution.py:61
  373.9 141.9 %all-gather.10.cloned.1.call-start = ((), (), s32[]{:S(2)}) async-start(), calls=%async_computation.5 | async-start | bytes 2228224 | tf_op jit(solution)/shard_map/all_gather | solution.py:59
  374.7 280.1 %all-reduce.5.cloned.1.call-start = ((), (), s32[]{:S(2)}) async-start(), calls=%async_computation.8 | async-start | bytes 8388608 | tf_op jit(solution)/shard_map/psum | solution.py:9
Sparse Core Ops, SparseCore 0:
  12.2 49.8 all-gather.5
  64.1 42.6 all-gather.7
  109.7 140.4 all-reduce.2
  259.6 38.2 reduce-scatter.1
  304.2 64.6 all-gather.11
  374.0 75.0 all-gather.13
  451.2 64.6 all-gather.9
  518.2 136.5 all-reduce.4
where the time goes:
time: 667 us
  waiting for transfers between devices  598 us (90%)
  local copies, waits for them, and re-layouts  29.2 us (4%)
  between operations  13.7 us (2%)
  matrix products  12.7 us (2%)
  other arithmetic  12.5 us (2%)
    psum x2, waiting for transfers between devices, from_root(): return lax.psum(kept, axis)  263 us
    all_gather x1, waiting for transfers between devices, on_device(): left_wide = lax.all_gather(left_cols, 'ka', axis=1, tiled=True)  74.4 us
    all_gather x1, waiting for transfers between devices, on_device(): lax.all_gather(left, 'row', axis=0, tiled=True)  64.7 us
    all_gather x1, waiting for transfers between devices, on_device(): lax.all_gather(right, 'row', axis=0, tiled=True)  64.2 us
    all_gather x1, waiting for transfers between devices, on_device(): lax.all_gather(right, 'col', axis=1, tiled=True)  49.2 us
    all_gather x1, waiting for transfers between devices, on_device(): lax.all_gather(left, 'col', axis=1, tiled=True)  43.2 us
    reduce_scatter x1, waiting for transfers between devices, on_device(): lax.psum_scatter(partial_value.astype(jnp.bfloat16), 'ka', scatter_dimens...  37.9 us
    all_gather x1, local copies, waits for them, and re-layouts, on_device(): lax.all_gather(left, 'col', axis=1, tiled=True)  15.2 us
  transfers between devices with their start and end apart: 8, of which 8 were waited for; matrix products, arithmetic and copies ran while one was open for 4% of the time, Pallas kernels for 0%

commit v1 on v0

--- a/solution.py
+++ b/solution.py
@@ -2,11 +2,6 @@
 import jax.numpy as jnp
 from jax import lax
 from jax.sharding import PartitionSpec as P
-
-
-def from_root(value, axis, source):
-    kept = jnp.where(lax.axis_index(axis) == source, value, 0).astype(value.dtype)
-    return lax.psum(kept, axis)
 
 
 def layer_norm(value):
@@ -38,14 +33,16 @@
     return (pair.astype(jnp.float32) + gate * proj).astype(jnp.bfloat16)
 
 
-def on_device(pair, pair_mask, w_in, w_gate, w_out):
+def transpose_tiles(value, n):
+    perm = [(r * n + c, c * n + r) for r in range(n) for c in range(n)]
+    return lax.ppermute(value, ("row", "col"), perm)
+
+
+def on_device(n, pair, pair_mask, w_in, w_gate, w_out):
     valid = pair_mask.astype(jnp.float32)[..., None]
     left, right, gate = prepare(pair, valid, w_in[0], w_gate[0])
-    left_rows, right_rows = (
-        lax.all_gather(left, "col", axis=1, tiled=True),
-        lax.all_gather(right, "col", axis=1, tiled=True),
-    )
-    right_diag = from_root(right_rows, "row", lax.axis_index("col"))
+    left_rows = lax.all_gather(left, "col", axis=1, tiled=True)
+    right_diag = lax.all_gather(transpose_tiles(right, n), "row", axis=1, tiled=True)
     partial_value = jnp.einsum(
         "ikc,jkc->ijc", left_rows, right_diag, preferred_element_type=jnp.float32
     )
@@ -54,20 +51,19 @@
     ).astype(jnp.float32)
     middle = finish(pair, tri, gate, w_out[0])
     left, right, gate = prepare(middle, valid, w_in[1], w_gate[1])
-    left_cols, right_cols = (
-        lax.all_gather(left, "row", axis=0, tiled=True),
-        lax.all_gather(right, "row", axis=0, tiled=True),
-    )
-    left_wide = lax.all_gather(left_cols, "ka", axis=1, tiled=True)
-    left_diag = from_root(left_wide, "col", lax.axis_index("row"))
+    right_cols = lax.all_gather(right, "row", axis=0, tiled=True)
+    left_half = lax.all_gather(transpose_tiles(left, n), "col", axis=0, tiled=True)
+    left_diag = lax.all_gather(left_half, "ka", axis=1, tiled=True)
     tri = jnp.einsum("kic,kjc->ijc", left_diag, right_cols, preferred_element_type=jnp.float32)
     return finish(middle, tri, gate, w_out[1])
 
 
 def solution(mesh):
+    n = mesh.shape["row"]
+    assert mesh.shape["col"] == n
     placed = (P("row", ("col", "ka"), None), P("row", ("col", "ka")), P(), P(), P())
     return jax.shard_map(
-        on_device,
+        lambda *a: on_device(n, *a),
         mesh=mesh,
         in_specs=placed,
         out_specs=P("row", ("col", "ka"), None),

time: 667 us -> 424 us (0.64)
  waiting for transfers between devices: 598 us -> 335 us
  local copies, waits for them, and re-layouts: 29.2 us -> 42.3 us
  starting transfers between devices: 0.29 us -> 7.61 us
    psum x2 -> x0, waiting for transfers between devices: 263 us -> none  [from_root(): return lax.psum(kept, axis)]
    all_gather x3 -> x4, local copies, waits for them, and re-layouts: 24.1 us -> 39.3 us  [the longest x1 15.2 us: on_device(): left_rows = lax.all_gather(left, 'col', axis=1, tiled=True)]
    ppermute x0 -> x2, starting transfers between devices: none -> 7.4 us  [transpose_tiles(): return lax.ppermute(value, ('row', 'col'), perm)]
    all_gather x5, waiting for transfers between devices: 296 us -> 289 us  [the longest x1 73.1 us: on_device(): left_diag = lax.all_gather(left_half, 'ka', axis=1, tiled=True)]
  transfers between devices with their start and end apart: 8 -> 8, of which waited for: 8 -> 8; matrix products, arithmetic and copies ran while one was open for 4% -> 6% of each run, Pallas kernels for 0% -> 0%
where the time goes in v1:
time: 424 us; the launch traced here: 423 us
  waiting for transfers between devices  335 us (79%)
  local copies, waits for them, and re-layouts  42.3 us (10%)
  matrix products  16 us (4%)
  between operations  13.6 us (3%)
  other arithmetic  8.84 us (2%)
  starting transfers between devices  7.61 us (2%)
    all_gather x1, waiting for transfers between devices, on_device(): left_diag = lax.all_gather(left_half, 'ka', axis=1, tiled=True)  73.1 us
    all_gather x1, waiting for transfers between devices, on_device(): right_cols = lax.all_gather(right, 'row', axis=0, tiled=True)  59.3 us
    all_gather x1, waiting for transfers between devices, on_device(): lax.all_gather(transpose_tiles(right, n), 'row', axis=1, tiled=True)  57.6 us
    all_gather x1, waiting for transfers between devices, on_device(): lax.all_gather(transpose_tiles(left, n), 'col', axis=0, tiled=True)  53.4 us
    all_gather x1, waiting for transfers between devices, on_device(): left_rows = lax.all_gather(left, 'col', axis=1, tiled=True)  45.1 us
    reduce_scatter x1, waiting for transfers between devices, on_device(): lax.psum_scatter(partial_value.astype(jnp.bfloat16), 'ka', scatter_dimens...  39.5 us
    all_gather x1, local copies, waits for them, and re-layouts, on_device(): left_rows = lax.all_gather(left, 'col', axis=1, tiled=True)  15.2 us
    all_gather x1, local copies, waits for them, and re-layouts, on_device(): lax.all_gather(transpose_tiles(right, n), 'row', axis=1, tiled=True)  15.2 us
  transfers between devices with their start and end apart: 8, of which 8 were waited for; matrix products, arithmetic and copies ran while one was open for 6% of the time, Pallas kernels for 0%

profile of v1, /device:TPU:1, one launch (start us, length us, event | category | flops | bytes accessed | tf_op | source)
XLA Modules:
  0.0 423.1 jit_solution(14155994391619889289)
XLA Ops:
  6.5 1.0 convert_reduce_fusion.1
  7.7 1.1 fusion.18
  9.8 1.3 fusion.42
  12.1 4.5 %collective-permute-start = (bf16[32,16,128]{2,1,0:T(8,128)(2,1)S(1)}, bf16[32,16,128]{2,1,0:T(8,128)(2,1)S(1)}, u32[]{:S(2)}, u32[]{:S(2)}) collective-permute-start(bf16[32,16,128]{2,1,0:T(8,128)(2,1)S(1)} %get-tuple-element.8), channel_id=1, source_target_pairs={{0,0},{2,32},{4,64},{6,96},{8,128},{10,160},{12,192},{14,224},{16,... | collective-permute-start | bytes 393224 | tf_op jit(solution)/shard_map/ppermute | solution.py:38
  16.6 2.6 collective-permute-done
  19.9 45.1 %all-gather.8.cloned.1.call-done = bf16[32,256,128]{2,1,0:T(8,128)(2,1)} async-done(((bf16[32,16,128]{2,1,0:T(8,128)(2,1)}), bf16[32,256,128]{2,1,0:T(8,128)(2,1)}) %all-gather.8.cloned.1.call-update) | async-done | bytes 2097168 | tf_op jit(solution)/shard_map/all_gather | solution.py:44
  65.1 15.2 %copy.49 = bf16[32,256,128]{0,1,2:T(8,128)(2,1)} copy(bf16[32,256,128]{2,1,0:T(8,128)(2,1)} %all-gather.8.cloned.1.call-done) | data formatting | bytes 4194304 | tf_op jit(solution)/shard_map/all_gather | solution.py:44
  80.3 57.6 %all-gather.6.cloned.1.call-done = bf16[32,256,128]{2,1,0:T(8,128)(2,1)} async-done(((bf16[32,16,128]{2,1,0:T(8,128)(2,1)}), bf16[32,256,128]{2,1,0:T(8,128)(2,1)}) %all-gather.6.cloned.1.call-update) | async-done | bytes 2097168 | tf_op jit(solution)/shard_map/all_gather | solution.py:45
  137.9 15.2 %copy.48 = bf16[32,256,128]{0,1,2:T(8,128)(2,1)} copy(bf16[32,256,128]{2,1,0:T(8,128)(2,1)} %all-gather.6.cloned.1.call-done) | data formatting | bytes 4194304 | tf_op jit(solution)/shard_map/all_gather | solution.py:45
  153.2 9.2 %fusion = bf16[32,32,128]{0,1,2:T(8,128)(2,1)} fusion(bf16[32,256,128]{0,1,2:T(8,128)(2,1)} %copy.48, bf16[32,256,128]{0,1,2:T(8,128)(2,1)} %copy.49), kind=kOutput, calls=%fused_computation.1 | convolution fusion | flops 67239936 | bytes 4456448 | tf_op jit(solution)/shard_map/ikc,jkc->ijc/dot_general | solution.py:46
  162.8 39.5 %reduce-scatter.2.cloned.1.call-done = bf16[32,16,128]{0,1,2:T(8,128)(2,1)} async-done(((bf16[32,32,128]{0,1,2:T(8,128)(2,1)}), bf16[32,16,128]{0,1,2:T(8,128)(2,1)}) %reduce-scatter.2.cloned.1.call-update) | async-done | bytes 131088 | tf_op jit(solution)/shard_map/reduce_scatter | solution.py:49
  202.3 1.2 convert_reduce_fusion
  203.5 1.3 fusion.14
  204.8 1.2 fusion.15
  207.7 0.8 fusion.21
  208.5 2.9 collective-permute-start.1
  211.4 3.4 collective-permute-done.1
  216.1 53.4 %all-gather.12.cloned.1.call-done = bf16[512,16,128]{2,1,0:T(8,128)(2,1)} async-done(((bf16[32,16,128]{2,1,0:T(8,128)(2,1)}), bf16[512,16,128]{2,1,0:T(8,128)(2,1)}) %all-gather.12.cloned.1.call-update) | async-done | bytes 2097168 | tf_op jit(solution)/shard_map/all_gather | solution.py:55
  269.5 4.9 %copy.55 = bf16[512,16,128]{0,1,2:T(8,128)(2,1)} copy(bf16[512,16,128]{2,1,0:T(8,128)(2,1)} %all-gather.12.cloned.1.call-done) | data formatting | bytes 4194304 | tf_op jit(solution)/shard_map/all_gather | solution.py:55
  274.8 59.3 %all-gather.10.cloned.1.call-done = bf16[512,16,128]{2,1,0:T(8,128)(2,1)} async-done(((bf16[32,16,128]{2,1,0:T(8,128)(2,1)}), bf16[512,16,128]{2,1,0:T(8,128)(2,1)}) %all-gather.10.cloned.1.call-update) | async-done | bytes 2097168 | tf_op jit(solution)/shard_map/all_gather | solution.py:54
  334.1 3.9 copy.56
  338.0 73.1 %all-gather.14.cloned.1.call-done = bf16[512,32,128]{0,1,2:T(8,128)(2,1)} async-done(((bf16[512,16,128]{0,1,2:T(8,128)(2,1)}), bf16[512,32,128]{0,1,2:T(8,128)(2,1)}) %all-gather.14.cloned.1.call-update) | async-done | bytes 4194320 | tf_op jit(solution)/shard_map/all_gather | solution.py:56
  411.1 3.4 fusion.57
  415.4 0.8 fusion.13
  (52 shorter events, 7.3 us)
Async XLA Ops:
  6.5 58.5 %all-gather.8.cloned.1.call-start = ((), (), s32[]{:S(2)}) async-start(), calls=%async_computation.2 | async-start | bytes 2228224 | tf_op jit(solution)/shard_map/all_gather | solution.py:44
  12.0 125.9 %all-gather.6.cloned.1.call-start = ((), (), s32[]{:S(2)}) async-start(), calls=%async_computation.1 | async-start | bytes 2228224 | tf_op jit(solution)/shard_map/all_gather | solution.py:45
  12.1 7.1 %collective-permute-start = (bf16[32,16,128]{2,1,0:T(8,128)(2,1)S(1)}, bf16[32,16,128]{2,1,0:T(8,128)(2,1)S(1)}, u32[]{:S(2)}, u32[]{:S(2)}) collective-permute-start(bf16[32,16,128]{2,1,0:T(8,128)(2,1)S(1)} %get-tuple-element.8), channel_id=1, source_target_pairs={{0,0},{2,32},{4,64},{6,96},{8,128},{10,160},{12,192},{14,224},{16,... | collective-permute-start | bytes 393224 | tf_op jit(solution)/shard_map/ppermute | solution.py:38
  19.2 0.7 copy-start.3
  19.9 182.4 %reduce-scatter.2.cloned.1.call-start = ((), (), s32[]{:S(2)}) async-start(), calls=%async_computation.3 | async-start | bytes 1572864 | tf_op jit(solution)/shard_map/reduce_scatter | solution.py:49
  153.2 9.3 %copy-start = (bf16[32,16,128]{2,1,0:T(8,128)(2,1)S(1)}, bf16[32,16,128]{2,1,0:T(8,128)(2,1)}, u32[]{:S(2)}) copy-start(bf16[32,16,128]{2,1,0:T(8,128)(2,1)} %param.5) | copy-start | bytes 393220
  153.2 9.3 %copy-start.5 = (bf16[2,128,128]{2,1,0:T(8,128)(2,1)S(1)}, bf16[2,128,128]{2,1,0:T(8,128)(2,1)}, u32[]{:S(2)}) copy-start(bf16[2,128,128]{2,1,0:T(8,128)(2,1)} %param.8) | copy-start | bytes 196612
  162.3 44.1 %copy-start.4 = (bf16[2,128,128]{2,1,0:T(8,128)(2,1)S(1)}, bf16[2,128,128]{2,1,0:T(8,128)(2,1)}, u32[]{:S(2)}) copy-start(bf16[2,128,128]{2,1,0:T(8,128)(2,1)} %param.9) | copy-start | bytes 196612
  162.3 45.0 %copy-start.1 = (bf16[2,128,512]{2,1,0:T(8,128)(2,1)S(1)}, bf16[2,128,512]{2,1,0:T(8,128)(2,1)}, u32[]{:S(2)}) copy-start(bf16[2,128,512]{2,1,0:T(8,128)(2,1)} %param.7) | copy-start | bytes 786436
  162.4 107.2 %all-gather.12.cloned.1.call-start = ((), (), s32[]{:S(2)}) async-start(), calls=%async_computation.5 | async-start | bytes 2228224 | tf_op jit(solution)/shard_map/all_gather | solution.py:55
  208.5 6.3 %collective-permute-start.1 = (bf16[32,16,128]{2,1,0:T(8,128)(2,1)S(1)}, bf16[32,16,128]{2,1,0:T(8,128)(2,1)S(1)}, u32[]{:S(2)}, u32[]{:S(2)}) collective-permute-start(bf16[32,16,128]{2,1,0:T(8,128)(2,1)S(1)} %get-tuple-element.5), channel_id=1, source_target_pairs={{0,0},{2,32},{4,64},{6,96},{8,128},{10,160},{12,192},{14,224},{16,... | collective-permute-start | bytes 393224 | tf_op jit(solution)/shard_map/ppermute | solution.py:38
  214.8 0.6 copy-start.2
  215.5 118.6 %all-gather.10.cloned.1.call-start = ((), (), s32[]{:S(2)}) async-start(), calls=%async_computation.4 | async-start | bytes 2228224 | tf_op jit(solution)/shard_map/all_gather | solution.py:54
  216.1 195.1 %all-gather.14.cloned.1.call-start = ((), (), s32[]{:S(2)}) async-start(), calls=%async_computation.6 | async-start | bytes 6291456 | tf_op jit(solution)/shard_map/all_gather | solution.py:56
Sparse Core Ops, SparseCore 0:
  12.1 52.8 all-gather.7
  67.1 70.8 all-gather.5
  162.5 39.7 reduce-scatter.1
  215.6 53.8 all-gather.11
  271.5 62.6 all-gather.9
  336.1 75.0 all-gather.13

commit v2 on v1

--- a/solution.py
+++ b/solution.py
@@ -38,11 +38,18 @@
     return lax.ppermute(value, ("row", "col"), perm)
 
 
+def gather_a2a(value, axis_name, n, axis):
+    copies = jnp.broadcast_to(value[None], (n,) + value.shape)
+    got = lax.all_to_all(copies, axis_name, 0, 0, tiled=False)
+    got = jnp.moveaxis(got, 0, axis)
+    return got.reshape(value.shape[:axis] + (n * value.shape[axis],) + value.shape[axis + 1 :])
+
+
 def on_device(n, pair, pair_mask, w_in, w_gate, w_out):
     valid = pair_mask.astype(jnp.float32)[..., None]
     left, right, gate = prepare(pair, valid, w_in[0], w_gate[0])
     left_rows = lax.all_gather(left, "col", axis=1, tiled=True)
-    right_diag = lax.all_gather(transpose_tiles(right, n), "row", axis=1, tiled=True)
+    right_diag = gather_a2a(transpose_tiles(right, n), "row", n, 1)
     partial_value = jnp.einsum(
         "ikc,jkc->ijc", left_rows, right_diag, preferred_element_type=jnp.float32
     )
@@ -51,7 +58,7 @@
     ).astype(jnp.float32)
     middle = finish(pair, tri, gate, w_out[0])
     left, right, gate = prepare(middle, valid, w_in[1], w_gate[1])
-    right_cols = lax.all_gather(right, "row", axis=0, tiled=True)
+    right_cols = gather_a2a(right, "row", n, 0)
     left_half = lax.all_gather(transpose_tiles(left, n), "col", axis=0, tiled=True)
     left_diag = lax.all_gather(left_half, "ka", axis=1, tiled=True)
     tri = jnp.einsum("kic,kjc->ijc", left_diag, right_cols, preferred_element_type=jnp.float32)

time: 424 us -> 299 us (0.71)
  waiting for transfers between devices: 335 us -> 193 us
  starting transfers between devices: 7.61 us -> 36.2 us
  local copies, waits for them, and re-layouts: 42.3 us -> 34.9 us
    all_gather x2 -> x0, waiting for transfers between devices: 117 us -> none  [the longest x1 59.3 us: on_device(): right_cols = lax.all_gather(right, 'row', axis=0, tiled=True)]
    all_to_all x0 -> x2, waiting for transfers between devices: none -> 56.1 us  [gather_a2a(): got = lax.all_to_all(copies, axis_name, 0, 0, tiled=False)]
    all_gather x1, waiting for transfers between devices: 73.1 us -> 21.9 us  [on_device(): left_diag = lax.all_gather(left_half, 'ka', axis=1, tiled=True)]
    all_to_all x0 -> x2, starting transfers between devices: none -> 28.7 us  [gather_a2a(): got = lax.all_to_all(copies, axis_name, 0, 0, tiled=False)]
    all_gather x1, waiting for transfers between devices: 45.1 us -> 25.5 us  [on_device(): left_rows = lax.all_gather(left, 'col', axis=1, tiled=True)]
    all_gather x2 -> x0, local copies, waits for them, and re-layouts: 19.1 us -> none  [the longest x1 15.2 us: on_device(): lax.all_gather(transpose_tiles(right, n), 'row', axis=1, tiled=True)]
    reduce_scatter x1, waiting for transfers between devices: 39.5 us -> 29.2 us  [on_device(): lax.psum_scatter(partial_value.astype(jnp.bfloat16), 'ka', scatter_dimens...]
    reshape x0 -> x2, local copies, waits for them, and re-layouts: none -> 6.94 us  [gather_a2a(): got.reshape(value.shape[:axis] + (n * value.shape[axis],) + value.shape[a...]
  transfers between devices with their start and end apart: 8 -> 8, of which waited for: 8 -> 8; matrix products, arithmetic and copies ran while one was open for 6% -> 8% of each run, Pallas kernels for 0% -> 0%
where the time goes in v2:
time: 299 us
  waiting for transfers between devices  193 us (65%)
  starting transfers between devices  36.2 us (12%)
  local copies, waits for them, and re-layouts  34.9 us (12%)
  matrix products  13.3 us (4%)
  between operations  13.3 us (4%)
  other arithmetic  8.18 us (3%)
    all_to_all x2, waiting for transfers between devices, gather_a2a(): got = lax.all_to_all(copies, axis_name, 0, 0, tiled=False)  56.1 us
    all_gather x1, waiting for transfers between devices, on_device(): lax.all_gather(transpose_tiles(left, n), 'col', axis=0, tiled=True)  54 us
    reduce_scatter x1, waiting for transfers between devices, on_device(): lax.psum_scatter(partial_value.astype(jnp.bfloat16), 'ka', scatter_dimens...  29.2 us
    all_to_all x2, starting transfers between devices, gather_a2a(): got = lax.all_to_all(copies, axis_name, 0, 0, tiled=False)  28.7 us
    all_gather x1, waiting for transfers between devices, on_device(): left_rows = lax.all_gather(left, 'col', axis=1, tiled=True)  25.5 us
    all_gather x1, waiting for transfers between devices, on_device(): left_diag = lax.all_gather(left_half, 'ka', axis=1, tiled=True)  21.9 us
    all_gather x1, local copies, waits for them, and re-layouts, on_device(): left_rows = lax.all_gather(left, 'col', axis=1, tiled=True)  15.3 us
    ppermute x2, starting transfers between devices, transpose_tiles(): return lax.ppermute(value, ('row', 'col'), perm)  7.43 us
  transfers between devices with their start and end apart: 8, of which 8 were waited for; matrix products, arithmetic and copies ran while one was open for 8% of the time, Pallas kernels for 0%

profile of v2, /device:TPU:1, one launch (start us, length us, event | category | flops | bytes accessed | tf_op | source)
XLA Modules:
  0.0 298.7 jit_solution(10571291877747777106)
XLA Ops:
  9.8 1.3 fusion.42
  12.0 4.5 %collective-permute-start = (bf16[32,16,128]{2,1,0:T(8,128)(2,1)S(1)}, bf16[32,16,128]{2,1,0:T(8,128)(2,1)S(1)}, u32[]{:S(2)}, u32[]{:S(2)}) collective-permute-start(bf16[32,16,128]{2,1,0:T(8,128)(2,1)S(1)} %get-tuple-element.8), channel_id=1, source_target_pairs={{0,0},{2,32},{4,64},{6,96},{8,128},{10,160},{12,192},{14,224},{16,... | collective-permute-start | bytes 393224 | tf_op jit(solution)/shard_map/ppermute | solution.py:38
  16.5 2.6 collective-permute-done
  19.1 1.7 broadcast_in_dim.4
  20.8 21.2 %all-to-all-start = ((bf16[16,32,16,128]{3,2,1,0:T(8,128)(2,1)}), bf16[16,32,16,128]{3,2,1,0:T(8,128)(2,1)S(1)}, u32[]{:S(2)}, u32[]{:S(2)}) async-start(bf16[16,32,16,128]{3,2,1,0:T(8,128)(2,1)} %broadcast_in_dim.4), calls=%async_computation | async-start | bytes 4194304 | tf_op jit(solution)/shard_map/all_to_all | solution.py:43
  42.1 25.5 %all-gather.4.cloned.1.call-done = bf16[32,256,128]{2,1,0:T(8,128)(2,1)} async-done(((bf16[32,16,128]{2,1,0:T(8,128)(2,1)}), bf16[32,256,128]{2,1,0:T(8,128)(2,1)}) %all-gather.4.cloned.1.call-update) | async-done | bytes 2097168 | tf_op jit(solution)/shard_map/all_gather | solution.py:51
  67.6 15.3 %copy.63 = bf16[32,256,128]{0,1,2:T(8,128)(2,1)} copy(bf16[32,256,128]{2,1,0:T(8,128)(2,1)} %all-gather.4.cloned.1.call-done) | data formatting | bytes 4194304 | tf_op jit(solution)/shard_map/all_gather | solution.py:51
  82.9 7.7 %all-to-all-done = bf16[16,32,16,128]{3,2,1,0:T(8,128)(2,1)S(1)} async-done(((bf16[16,32,16,128]{3,2,1,0:T(8,128)(2,1)}), bf16[16,32,16,128]{3,2,1,0:T(8,128)(2,1)S(1)}, u32[]{:S(2)}, u32[]{:S(2)}) %all-to-all-start) | async-done | bytes 2097184 | tf_op jit(solution)/shard_map/all_to_all | solution.py:43
  90.5 2.0 copy.61
  92.5 3.4 %copy.62 = bf16[32,256,128]{1,0,2:T(8,128)(2,1)S(1)} copy(bf16[32,256,128]{2,1,0:T(8,128)(2,1)} %bitcast.41) | data formatting | bytes 4194304 | tf_op jit(solution)/shard_map/reshape | solution.py:45
  95.9 5.8 %fusion = bf16[32,32,128]{0,1,2:T(8,128)(2,1)} fusion(bf16[32,256,128]{1,0,2:T(8,128)(2,1)S(1)} %copy.62, bf16[32,256,128]{0,1,2:T(8,128)(2,1)} %copy.63), kind=kOutput, calls=%fused_computation.1 | convolution fusion | flops 67239936 | bytes 4456448 | tf_op jit(solution)/shard_map/ikc,jkc->ijc/dot_general | solution.py:53
  102.2 29.2 %reduce-scatter.2.cloned.1.call-done = bf16[32,16,128]{0,1,2:T(8,128)(2,1)} async-done(((bf16[32,32,128]{0,1,2:T(8,128)(2,1)}), bf16[32,16,128]{0,1,2:T(8,128)(2,1)}) %reduce-scatter.2.cloned.1.call-update) | async-done | bytes 131088 | tf_op jit(solution)/shard_map/reduce_scatter | solution.py:56
  131.4 1.2 convert_reduce_fusion
  132.6 1.3 fusion.14
  137.0 2.9 collective-permute-start.1
  139.9 3.3 %collective-permute-done.1 = bf16[32,16,128]{2,1,0:T(8,128)(2,1)S(1)} collective-permute-done((bf16[32,16,128]{2,1,0:T(8,128)(2,1)S(1)}, bf16[32,16,128]{2,1,0:T(8,128)(2,1)S(1)}, u32[]{:S(2)}, u32[]{:S(2)}) %collective-permute-start.1) | collective-permute-done | bytes 131104 | tf_op jit(solution)/shard_map/ppermute | solution.py:38
  144.0 54.0 %all-gather.6.cloned.1.call-done = bf16[512,16,128]{2,1,0:T(8,128)(2,1)} async-done(((bf16[32,16,128]{2,1,0:T(8,128)(2,1)}), bf16[512,16,128]{2,1,0:T(8,128)(2,1)}) %all-gather.6.cloned.1.call-update) | async-done | bytes 2097168 | tf_op jit(solution)/shard_map/all_gather | solution.py:62
  198.0 4.9 %copy.69 = bf16[512,16,128]{0,1,2:T(8,128)(2,1)} copy(bf16[512,16,128]{2,1,0:T(8,128)(2,1)} %all-gather.6.cloned.1.call-done) | data formatting | bytes 4194304 | tf_op jit(solution)/shard_map/all_gather | solution.py:62
  203.0 1.7 broadcast_in_dim.5
  204.8 7.5 %all-to-all-start.1 = ((bf16[16,32,16,128]{3,2,1,0:T(8,128)(2,1)}), bf16[16,32,16,128]{3,2,1,0:T(8,128)(2,1)S(1)}, u32[]{:S(2)}, u32[]{:S(2)}) async-start(bf16[16,32,16,128]{3,2,1,0:T(8,128)(2,1)} %broadcast_in_dim.5), calls=%async_computation.2 | async-start | bytes 4194304 | tf_op jit(solution)/shard_map/all_to_all | solution.py:43
  212.6 48.5 %all-to-all-done.1 = bf16[16,32,16,128]{3,2,1,0:T(8,128)(2,1)S(1)} async-done(((bf16[16,32,16,128]{3,2,1,0:T(8,128)(2,1)}), bf16[16,32,16,128]{3,2,1,0:T(8,128)(2,1)S(1)}, u32[]{:S(2)}, u32[]{:S(2)}) %all-to-all-start.1) | async-done | bytes 2097184 | tf_op jit(solution)/shard_map/all_to_all | solution.py:43
  261.0 3.5 %copy.70 = bf16[512,16,128]{0,1,2:T(8,128)(2,1)} copy(bf16[512,16,128]{2,1,0:T(8,128)(2,1)S(1)} %bitcast.40) | data formatting | bytes 4194304 | tf_op jit(solution)/shard_map/reshape | solution.py:45
  264.6 21.9 %all-gather.8.cloned.1.call-done = bf16[512,32,128]{0,1,2:T(8,128)(2,1)} async-done(((bf16[512,16,128]{0,1,2:T(8,128)(2,1)}), bf16[512,32,128]{0,1,2:T(8,128)(2,1)}) %all-gather.8.cloned.1.call-update) | async-done | bytes 4194320 | tf_op jit(solution)/shard_map/all_gather | solution.py:63
  286.4 4.0 %fusion.57 = (f32[32,16]{0,1:T(8,128)S(1)}, f32[32,16,128]{0,1,2:T(8,128)S(1)}) fusion(bf16[512,16,128]{0,1,2:T(8,128)(2,1)} %copy.70, bf16[512,32,128]{0,1,2:T(8,128)(2,1)} %all-gather.8.cloned.1.call-done), kind=kOutput, calls=%fused_computation.85 | convolution fusion | flops 67173888 | bytes 6555648 | tf_op jit(solution)/shard_map/kic,kjc->ijc/dot_general | solution.py:64
  (51 shorter events, 10.4 us)
Async XLA Ops:
  6.5 61.1 %all-gather.4.cloned.1.call-start = ((), (), s32[]{:S(2)}) async-start(), calls=%async_computation.3 | async-start | bytes 2228224 | tf_op jit(solution)/shard_map/all_gather | solution.py:51
  12.0 7.1 %collective-permute-start = (bf16[32,16,128]{2,1,0:T(8,128)(2,1)S(1)}, bf16[32,16,128]{2,1,0:T(8,128)(2,1)S(1)}, u32[]{:S(2)}, u32[]{:S(2)}) collective-permute-start(bf16[32,16,128]{2,1,0:T(8,128)(2,1)S(1)} %get-tuple-element.8), channel_id=1, source_target_pairs={{0,0},{2,32},{4,64},{6,96},{8,128},{10,160},{12,192},{14,224},{16,... | collective-permute-start | bytes 393224 | tf_op jit(solution)/shard_map/ppermute | solution.py:38
  20.8 69.7 %all-to-all-start = ((bf16[16,32,16,128]{3,2,1,0:T(8,128)(2,1)}), bf16[16,32,16,128]{3,2,1,0:T(8,128)(2,1)S(1)}, u32[]{:S(2)}, u32[]{:S(2)}) async-start(bf16[16,32,16,128]{3,2,1,0:T(8,128)(2,1)} %broadcast_in_dim.4), calls=%async_computation | async-start | bytes 4194304 | tf_op jit(solution)/shard_map/all_to_all | solution.py:43
  42.1 89.3 %reduce-scatter.2.cloned.1.call-start = ((), (), s32[]{:S(2)}) async-start(), calls=%async_computation.4 | async-start | bytes 1572864 | tf_op jit(solution)/shard_map/reduce_scatter | solution.py:56
  95.9 5.9 %copy-start = (bf16[32,16,128]{2,1,0:T(8,128)(2,1)S(1)}, bf16[32,16,128]{2,1,0:T(8,128)(2,1)}, u32[]{:S(2)}) copy-start(bf16[32,16,128]{2,1,0:T(8,128)(2,1)} %param.5) | copy-start | bytes 393220
  95.9 5.9 %copy-start.4 = (bf16[2,128,128]{2,1,0:T(8,128)(2,1)S(1)}, bf16[2,128,128]{2,1,0:T(8,128)(2,1)}, u32[]{:S(2)}) copy-start(bf16[2,128,128]{2,1,0:T(8,128)(2,1)} %param.8) | copy-start | bytes 196612
  101.8 33.8 %copy-start.3 = (bf16[2,128,128]{2,1,0:T(8,128)(2,1)S(1)}, bf16[2,128,128]{2,1,0:T(8,128)(2,1)}, u32[]{:S(2)}) copy-start(bf16[2,128,128]{2,1,0:T(8,128)(2,1)} %param.9) | copy-start | bytes 196612
  101.8 96.3 %all-gather.6.cloned.1.call-start = ((), (), s32[]{:S(2)}) async-start(), calls=%async_computation.5 | async-start | bytes 2228224 | tf_op jit(solution)/shard_map/all_gather | solution.py:62
  102.2 34.2 %copy-start.1 = (bf16[2,128,512]{2,1,0:T(8,128)(2,1)S(1)}, bf16[2,128,512]{2,1,0:T(8,128)(2,1)}, u32[]{:S(2)}) copy-start(bf16[2,128,512]{2,1,0:T(8,128)(2,1)} %param.7) | copy-start | bytes 786436
  137.0 6.3 %collective-permute-start.1 = (bf16[32,16,128]{2,1,0:T(8,128)(2,1)S(1)}, bf16[32,16,128]{2,1,0:T(8,128)(2,1)S(1)}, u32[]{:S(2)}, u32[]{:S(2)}) collective-permute-start(bf16[32,16,128]{2,1,0:T(8,128)(2,1)S(1)} %get-tuple-element.5), channel_id=1, source_target_pairs={{0,0},{2,32},{4,64},{6,96},{8,128},{10,160},{12,192},{14,224},{16,... | collective-permute-start | bytes 393224 | tf_op jit(solution)/shard_map/ppermute | solution.py:38
  143.3 0.7 copy-start.2
  143.9 142.5 %all-gather.8.cloned.1.call-start = ((), (), s32[]{:S(2)}) async-start(), calls=%async_computation.6 | async-start | bytes 6291456 | tf_op jit(solution)/shard_map/all_gather | solution.py:63
  204.8 56.3 %all-to-all-start.1 = ((bf16[16,32,16,128]{3,2,1,0:T(8,128)(2,1)}), bf16[16,32,16,128]{3,2,1,0:T(8,128)(2,1)S(1)}, u32[]{:S(2)}, u32[]{:S(2)}) async-start(bf16[16,32,16,128]{3,2,1,0:T(8,128)(2,1)} %broadcast_in_dim.5), calls=%async_computation.2 | async-start | bytes 4194304 | tf_op jit(solution)/shard_map/all_to_all | solution.py:43
Sparse Core Ops, SparseCore 0:
  16.6 50.9 all-gather.3
  101.9 29.4 reduce-scatter.1
  144.1 53.9 all-gather.5
  203.1 83.2 all-gather.7

commit v3 on v2

--- a/solution.py
+++ b/solution.py
@@ -45,6 +45,15 @@
     return got.reshape(value.shape[:axis] + (n * value.shape[axis],) + value.shape[axis + 1 :])
 
 
+def sum_over_ka(partial_value):
+    half = partial_value.shape[1] // 2
+    me = lax.axis_index("ka")
+    mine = lax.dynamic_slice_in_dim(partial_value, me * half, half, axis=1)
+    theirs = lax.dynamic_slice_in_dim(partial_value, (1 - me) * half, half, axis=1)
+    got = lax.ppermute(theirs.astype(jnp.bfloat16), "ka", [(0, 1), (1, 0)])
+    return mine + got.astype(jnp.float32)
+
+
 def on_device(n, pair, pair_mask, w_in, w_gate, w_out):
     valid = pair_mask.astype(jnp.float32)[..., None]
     left, right, gate = prepare(pair, valid, w_in[0], w_gate[0])
@@ -53,9 +62,7 @@
     partial_value = jnp.einsum(
         "ikc,jkc->ijc", left_rows, right_diag, preferred_element_type=jnp.float32
     )
-    tri = lax.psum_scatter(
-        partial_value.astype(jnp.bfloat16), "ka", scatter_dimension=1, tiled=True
-    ).astype(jnp.float32)
+    tri = sum_over_ka(partial_value)
     middle = finish(pair, tri, gate, w_out[0])
     left, right, gate = prepare(middle, valid, w_in[1], w_gate[1])
     right_cols = gather_a2a(right, "row", n, 0)

time: 299 us -> 285 us (0.953)
  waiting for transfers between devices: 193 us -> 175 us
  starting transfers between devices: 36.2 us -> 44.1 us
  other arithmetic: 8.18 us -> 5.13 us
    reduce_scatter x1 -> x0, waiting for transfers between devices: 29.2 us -> none  [on_device(): lax.psum_scatter(partial_value.astype(jnp.bfloat16), 'ka', scatter_dimens...]
    ppermute x0 -> x1, waiting for transfers between devices: none -> 8.67 us  [sum_over_ka(): got = lax.ppermute(theirs.astype(jnp.bfloat16), 'ka', [(0, 1), (1, 0)])]
    ppermute x0 -> x1, starting transfers between devices: none -> 4.88 us  [sum_over_ka(): got = lax.ppermute(theirs.astype(jnp.bfloat16), 'ka', [(0, 1), (1, 0)])]
    all_gather x1, waiting for transfers between devices: 54 us -> 57.4 us  [on_device(): lax.all_gather(transpose_tiles(left, n), 'col', axis=0, tiled=True)]
    ppermute x2, starting transfers between devices: 7.43 us -> 10.5 us  [transpose_tiles(): return lax.ppermute(value, ('row', 'col'), perm)]
where the time goes in v3:
time: 285 us
  waiting for transfers between devices  175 us (61%)
  starting transfers between devices  44.1 us (15%)
  local copies, waits for them, and re-layouts  35.1 us (12%)
  between operations  13.3 us (5%)
  matrix products  12.1 us (4%)
  other arithmetic  5.13 us (2%)
    all_gather x1, waiting for transfers between devices, on_device(): lax.all_gather(transpose_tiles(left, n), 'col', axis=0, tiled=True)  57.4 us
    all_to_all x2, waiting for transfers between devices, gather_a2a(): got = lax.all_to_all(copies, axis_name, 0, 0, tiled=False)  56.1 us
    all_to_all x2, starting transfers between devices, gather_a2a(): got = lax.all_to_all(copies, axis_name, 0, 0, tiled=False)  28.7 us
    all_gather x1, waiting for transfers between devices, on_device(): left_rows = lax.all_gather(left, 'col', axis=1, tiled=True)  25.5 us
    all_gather x1, waiting for transfers between devices, on_device(): left_diag = lax.all_gather(left_half, 'ka', axis=1, tiled=True)  21.9 us
    all_gather x1, local copies, waits for them, and re-layouts, on_device(): left_rows = lax.all_gather(left, 'col', axis=1, tiled=True)  15.3 us
    ppermute x2, starting transfers between devices, transpose_tiles(): return lax.ppermute(value, ('row', 'col'), perm)  10.5 us
    ppermute x1, waiting for transfers between devices, sum_over_ka(): got = lax.ppermute(theirs.astype(jnp.bfloat16), 'ka', [(0, 1), (1, 0)])  8.67 us
  transfers between devices with their start and end apart: 8, of which 8 were waited for; matrix products, arithmetic and copies ran while one was open for 8% of the time, Pallas kernels for 0%

profile of v3, /device:TPU:1, one launch (start us, length us, event | category | flops | bytes accessed | tf_op | source)
XLA Modules:
  0.0 284.6 jit_solution(6736398770562295000)
XLA Ops:
  7.7 1.1 fusion.15
  9.8 1.3 fusion.39
  12.0 4.5 %collective-permute-start = (bf16[32,16,128]{2,1,0:T(8,128)(2,1)S(1)}, bf16[32,16,128]{2,1,0:T(8,128)(2,1)S(1)}, u32[]{:S(2)}, u32[]{:S(2)}) collective-permute-start(bf16[32,16,128]{2,1,0:T(8,128)(2,1)S(1)} %get-tuple-element.8), channel_id=1, source_target_pairs={{0,0},{2,32},{4,64},{6,96},{8,128},{10,160},{12,192},{14,224},{16,... | collective-permute-start | bytes 393224 | tf_op jit(solution)/shard_map/ppermute | solution.py:38
  16.5 2.6 collective-permute-done
  19.1 1.7 broadcast_in_dim.4
  20.8 21.2 %all-to-all-start = ((bf16[16,32,16,128]{3,2,1,0:T(8,128)(2,1)}), bf16[16,32,16,128]{3,2,1,0:T(8,128)(2,1)S(1)}, u32[]{:S(2)}, u32[]{:S(2)}) async-start(bf16[16,32,16,128]{3,2,1,0:T(8,128)(2,1)} %broadcast_in_dim.4), calls=%async_computation | async-start | bytes 4194304 | tf_op jit(solution)/shard_map/all_to_all | solution.py:43
  42.1 25.5 %all-gather.4.cloned.1.call-done = bf16[32,256,128]{2,1,0:T(8,128)(2,1)} async-done(((bf16[32,16,128]{2,1,0:T(8,128)(2,1)}), bf16[32,256,128]{2,1,0:T(8,128)(2,1)}) %all-gather.4.cloned.1.call-update) | async-done | bytes 2097168 | tf_op jit(solution)/shard_map/all_gather | solution.py:60
  67.6 15.3 %copy.63 = bf16[32,256,128]{0,1,2:T(8,128)(2,1)} copy(bf16[32,256,128]{2,1,0:T(8,128)(2,1)} %all-gather.4.cloned.1.call-done) | data formatting | bytes 4194304 | tf_op jit(solution)/shard_map/all_gather | solution.py:60
  82.9 7.6 %all-to-all-done = bf16[16,32,16,128]{3,2,1,0:T(8,128)(2,1)S(1)} async-done(((bf16[16,32,16,128]{3,2,1,0:T(8,128)(2,1)}), bf16[16,32,16,128]{3,2,1,0:T(8,128)(2,1)S(1)}, u32[]{:S(2)}, u32[]{:S(2)}) %all-to-all-start) | async-done | bytes 2097184 | tf_op jit(solution)/shard_map/all_to_all | solution.py:43
  90.5 2.0 copy.61
  92.5 3.4 %copy.62 = bf16[32,256,128]{1,0,2:T(8,128)(2,1)S(1)} copy(bf16[32,256,128]{2,1,0:T(8,128)(2,1)} %bitcast.49) | data formatting | bytes 4194304 | tf_op jit(solution)/shard_map/reshape | solution.py:45
  95.9 4.6 %fusion.55 = f32[128,32,32]{2,1,0:T(8,128)S(1)} fusion(bf16[32,256,128]{1,0,2:T(8,128)(2,1)S(1)} %copy.62, bf16[32,256,128]{0,1,2:T(8,128)(2,1)} %copy.63), kind=kOutput, calls=%fused_computation.84 | convolution fusion | flops 67108864 | bytes 4718592 | tf_op jit(solution)/shard_map/ikc,jkc->ijc/dot_general | solution.py:62
  100.7 4.9 %collective-permute-start.1 = (bf16[32,16,128]{0,1,2:T(8,128)(2,1)S(1)}, bf16[32,16,128]{0,1,2:T(8,128)(2,1)S(1)}, u32[]{:S(2)}, u32[]{:S(2)}) collective-permute-start(bf16[32,16,128]{0,1,2:T(8,128)(2,1)S(1)} %fusion.11), channel_id=1, source_target_pairs={{0,1},{1,0},{2,3},{3,2},{4,5},{5,4},{6,7},{7,6},{8,9},{9,8},{10,11... | collective-permute-start | bytes 393224 | tf_op jit(solution)/shard_map/ppermute | solution.py:53
  106.0 8.7 %collective-permute-done.1 = bf16[32,16,128]{0,1,2:T(8,128)(2,1)S(1)} collective-permute-done((bf16[32,16,128]{0,1,2:T(8,128)(2,1)S(1)}, bf16[32,16,128]{0,1,2:T(8,128)(2,1)S(1)}, u32[]{:S(2)}, u32[]{:S(2)}) %collective-permute-start.1) | collective-permute-done | bytes 131104 | tf_op jit(solution)/shard_map/ppermute | solution.py:53
  117.2 6.0 %collective-permute-start.2 = (bf16[32,16,128]{2,1,0:T(8,128)(2,1)S(1)}, bf16[32,16,128]{2,1,0:T(8,128)(2,1)S(1)}, u32[]{:S(2)}, u32[]{:S(2)}) collective-permute-start(bf16[32,16,128]{2,1,0:T(8,128)(2,1)S(1)} %get-tuple-element.5), channel_id=1, source_target_pairs={{0,0},{2,32},{4,64},{6,96},{8,128},{10,160},{12,192},{14,224},{16,... | collective-permute-start | bytes 393224 | tf_op jit(solution)/shard_map/ppermute | solution.py:38
  123.2 2.6 collective-permute-done.2
  126.6 57.4 %all-gather.6.cloned.1.call-done = bf16[512,16,128]{2,1,0:T(8,128)(2,1)} async-done(((bf16[32,16,128]{2,1,0:T(8,128)(2,1)}), bf16[512,16,128]{2,1,0:T(8,128)(2,1)}) %all-gather.6.cloned.1.call-update) | async-done | bytes 2097168 | tf_op jit(solution)/shard_map/all_gather | solution.py:69
  184.0 4.9 %copy.69 = bf16[512,16,128]{0,1,2:T(8,128)(2,1)} copy(bf16[512,16,128]{2,1,0:T(8,128)(2,1)} %all-gather.6.cloned.1.call-done) | data formatting | bytes 4194304 | tf_op jit(solution)/shard_map/all_gather | solution.py:69
  188.9 1.7 broadcast_in_dim.5
  190.7 7.5 %all-to-all-start.1 = ((bf16[16,32,16,128]{3,2,1,0:T(8,128)(2,1)}), bf16[16,32,16,128]{3,2,1,0:T(8,128)(2,1)S(1)}, u32[]{:S(2)}, u32[]{:S(2)}) async-start(bf16[16,32,16,128]{3,2,1,0:T(8,128)(2,1)} %broadcast_in_dim.5), calls=%async_computation.1 | async-start | bytes 4194304 | tf_op jit(solution)/shard_map/all_to_all | solution.py:43
  198.5 48.5 %all-to-all-done.1 = bf16[16,32,16,128]{3,2,1,0:T(8,128)(2,1)S(1)} async-done(((bf16[16,32,16,128]{3,2,1,0:T(8,128)(2,1)}), bf16[16,32,16,128]{3,2,1,0:T(8,128)(2,1)S(1)}, u32[]{:S(2)}, u32[]{:S(2)}) %all-to-all-start.1) | async-done | bytes 2097184 | tf_op jit(solution)/shard_map/all_to_all | solution.py:43
  246.9 3.5 %copy.70 = bf16[512,16,128]{0,1,2:T(8,128)(2,1)} copy(bf16[512,16,128]{2,1,0:T(8,128)(2,1)S(1)} %bitcast.48) | data formatting | bytes 4194304 | tf_op jit(solution)/shard_map/reshape | solution.py:45
  250.5 21.9 %all-gather.8.cloned.1.call-done = bf16[512,32,128]{0,1,2:T(8,128)(2,1)} async-done(((bf16[512,16,128]{0,1,2:T(8,128)(2,1)}), bf16[512,32,128]{0,1,2:T(8,128)(2,1)}) %all-gather.8.cloned.1.call-update) | async-done | bytes 4194320 | tf_op jit(solution)/shard_map/all_gather | solution.py:70
  272.3 4.0 %fusion.54 = (f32[32,16]{0,1:T(8,128)S(1)}, f32[32,16,128]{0,1,2:T(8,128)S(1)}) fusion(bf16[512,16,128]{0,1,2:T(8,128)(2,1)} %copy.70, bf16[512,32,128]{0,1,2:T(8,128)(2,1)} %all-gather.8.cloned.1.call-done), kind=kOutput, calls=%fused_computation.83 | convolution fusion | flops 67173888 | bytes 6555648 | tf_op jit(solution)/shard_map/kic,kjc->ijc/dot_general | solution.py:71
  (51 shorter events, 8.7 us)
Async XLA Ops:
  6.5 61.1 %all-gather.4.cloned.1.call-start = ((), (), s32[]{:S(2)}) async-start(), calls=%async_computation.2 | async-start | bytes 2228224 | tf_op jit(solution)/shard_map/all_gather | solution.py:60
  12.0 7.1 %collective-permute-start = (bf16[32,16,128]{2,1,0:T(8,128)(2,1)S(1)}, bf16[32,16,128]{2,1,0:T(8,128)(2,1)S(1)}, u32[]{:S(2)}, u32[]{:S(2)}) collective-permute-start(bf16[32,16,128]{2,1,0:T(8,128)(2,1)S(1)} %get-tuple-element.8), channel_id=1, source_target_pairs={{0,0},{2,32},{4,64},{6,96},{8,128},{10,160},{12,192},{14,224},{16,... | collective-permute-start | bytes 393224 | tf_op jit(solution)/shard_map/ppermute | solution.py:38
  20.8 69.7 %all-to-all-start = ((bf16[16,32,16,128]{3,2,1,0:T(8,128)(2,1)}), bf16[16,32,16,128]{3,2,1,0:T(8,128)(2,1)S(1)}, u32[]{:S(2)}, u32[]{:S(2)}) async-start(bf16[16,32,16,128]{3,2,1,0:T(8,128)(2,1)} %broadcast_in_dim.4), calls=%async_computation | async-start | bytes 4194304 | tf_op jit(solution)/shard_map/all_to_all | solution.py:43
  42.1 141.9 %all-gather.6.cloned.1.call-start = ((), (), s32[]{:S(2)}) async-start(), calls=%async_computation.3 | async-start | bytes 2228224 | tf_op jit(solution)/shard_map/all_gather | solution.py:69
  95.9 9.7 %copy-start = (bf16[32,16,128]{2,1,0:T(8,128)(2,1)S(1)}, bf16[32,16,128]{2,1,0:T(8,128)(2,1)}, u32[]{:S(2)}) copy-start(bf16[32,16,128]{2,1,0:T(8,128)(2,1)} %param.5) | copy-start | bytes 393220
  95.9 9.7 %copy-start.4 = (bf16[2,128,128]{2,1,0:T(8,128)(2,1)S(1)}, bf16[2,128,128]{2,1,0:T(8,128)(2,1)}, u32[]{:S(2)}) copy-start(bf16[2,128,128]{2,1,0:T(8,128)(2,1)} %param.8) | copy-start | bytes 196612
  100.7 13.9 %collective-permute-start.1 = (bf16[32,16,128]{0,1,2:T(8,128)(2,1)S(1)}, bf16[32,16,128]{0,1,2:T(8,128)(2,1)S(1)}, u32[]{:S(2)}, u32[]{:S(2)}) collective-permute-start(bf16[32,16,128]{0,1,2:T(8,128)(2,1)S(1)} %fusion.11), channel_id=1, source_target_pairs={{0,1},{1,0},{2,3},{3,2},{4,5},{5,4},{6,7},{7,6},{8,9},{9,8},{10,11... | collective-permute-start | bytes 393224 | tf_op jit(solution)/shard_map/ppermute | solution.py:53
  114.8 1.0 copy-start.3
  115.1 1.6 copy-start.1
  117.2 8.6 %collective-permute-start.2 = (bf16[32,16,128]{2,1,0:T(8,128)(2,1)S(1)}, bf16[32,16,128]{2,1,0:T(8,128)(2,1)S(1)}, u32[]{:S(2)}, u32[]{:S(2)}) collective-permute-start(bf16[32,16,128]{2,1,0:T(8,128)(2,1)S(1)} %get-tuple-element.5), channel_id=1, source_target_pairs={{0,0},{2,32},{4,64},{6,96},{8,128},{10,160},{12,192},{14,224},{16,... | collective-permute-start | bytes 393224 | tf_op jit(solution)/shard_map/ppermute | solution.py:38
  125.8 0.7 copy-start.2
  126.5 145.8 %all-gather.8.cloned.1.call-start = ((), (), s32[]{:S(2)}) async-start(), calls=%async_computation.4 | async-start | bytes 6291456 | tf_op jit(solution)/shard_map/all_gather | solution.py:70
  190.7 56.3 %all-to-all-start.1 = ((bf16[16,32,16,128]{3,2,1,0:T(8,128)(2,1)}), bf16[16,32,16,128]{3,2,1,0:T(8,128)(2,1)S(1)}, u32[]{:S(2)}, u32[]{:S(2)}) async-start(bf16[16,32,16,128]{3,2,1,0:T(8,128)(2,1)} %broadcast_in_dim.5), calls=%async_computation.1 | async-start | bytes 4194304 | tf_op jit(solution)/shard_map/all_to_all | solution.py:43
Sparse Core Ops, SparseCore 0:
  16.6 50.9 all-gather.3
  126.6 57.2 all-gather.5
  189.1 83.2 all-gather.7

commit v4 on v3

--- a/solution.py
+++ b/solution.py
@@ -54,6 +54,14 @@
     return mine + got.astype(jnp.float32)
 
 
+def split_rows_over_ka(value):
+    rows, cols = value.shape[0], value.shape[1]
+    halves = value.reshape((2, rows // 2) + value.shape[1:])
+    got = lax.all_to_all(halves, "ka", 0, 0, tiled=False)
+    got = jnp.moveaxis(got, 0, 1)
+    return got.reshape((rows // 2, 2 * cols) + value.shape[2:])
+
+
 def on_device(n, pair, pair_mask, w_in, w_gate, w_out):
     valid = pair_mask.astype(jnp.float32)[..., None]
     left, right, gate = prepare(pair, valid, w_in[0], w_gate[0])
@@ -65,10 +73,13 @@
     tri = sum_over_ka(partial_value)
     middle = finish(pair, tri, gate, w_out[0])
     left, right, gate = prepare(middle, valid, w_in[1], w_gate[1])
-    right_cols = gather_a2a(right, "row", n, 0)
-    left_half = lax.all_gather(transpose_tiles(left, n), "col", axis=0, tiled=True)
-    left_diag = lax.all_gather(left_half, "ka", axis=1, tiled=True)
-    tri = jnp.einsum("kic,kjc->ijc", left_diag, right_cols, preferred_element_type=jnp.float32)
+    left_h, right_h = split_rows_over_ka(left), split_rows_over_ka(right)
+    right_cols = gather_a2a(right_h, "row", n, 0)
+    left_cols = lax.all_gather(transpose_tiles(left_h, n), "col", axis=0, tiled=True)
+    partial_value = jnp.einsum(
+        "kic,kjc->ijc", left_cols, right_cols, preferred_element_type=jnp.float32
+    )
+    tri = sum_over_ka(partial_value)
     return finish(middle, tri, gate, w_out[1])
 
 

time: 285 us -> 302 us (1.060)
  blocking collectives: 0 us -> 17.8 us
  waiting for transfers between devices: 175 us -> 169 us
  starting transfers between devices: 44.1 us -> 49.9 us
    all_gather x2 -> x1, waiting for transfers between devices: 79.3 us -> 35.2 us  [on_device(): lax.all_gather(transpose_tiles(left_h, n), 'col', axis=0, tiled=True)]
    all_to_all x2, waiting for transfers between devices: 56.1 us -> 83.1 us  [gather_a2a(): got = lax.all_to_all(copies, axis_name, 0, 0, tiled=False)]
    all_to_all x0 -> x2, blocking collectives: none -> 17.8 us  [split_rows_over_ka(): got = lax.all_to_all(halves, 'ka', 0, 0, tiled=False)]
    ppermute x1 -> x2, waiting for transfers between devices: 8.67 us -> 22.9 us  [sum_over_ka(): got = lax.ppermute(theirs.astype(jnp.bfloat16), 'ka', [(0, 1), (1, 0)])]
    all_gather x1 -> x0, local copies, waits for them, and re-layouts: 4.95 us -> none  [on_device(): lax.all_gather(transpose_tiles(left, n), 'col', axis=0, tiled=True)]
    all_to_all x2, starting transfers between devices: 28.7 us -> 32.2 us  [gather_a2a(): got = lax.all_to_all(copies, axis_name, 0, 0, tiled=False)]
    ppermute x1 -> x2, starting transfers between devices: 4.88 us -> 6.91 us  [sum_over_ka(): got = lax.ppermute(theirs.astype(jnp.bfloat16), 'ka', [(0, 1), (1, 0)])]
  transfers between devices with their start and end apart: 8 -> 8, of which waited for: 8 -> 7; matrix products, arithmetic and copies ran while one was open for 8% -> 8% of each run, Pallas kernels for 0% -> 0%
where the time goes in v4:
time: 302 us
  waiting for transfers between devices  169 us (56%)
  starting transfers between devices  49.9 us (17%)
  local copies, waits for them, and re-layouts  32.7 us (11%)
  blocking collectives  17.8 us (6%)
  between operations  13.7 us (5%)
  matrix products  12.7 us (4%)
  other arithmetic  5.4 us (2%)
    all_to_all x2, waiting for transfers between devices, gather_a2a(): got = lax.all_to_all(copies, axis_name, 0, 0, tiled=False)  83.1 us
    all_gather x1, waiting for transfers between devices, on_device(): lax.all_gather(transpose_tiles(left_h, n), 'col', axis=0, tiled=True)  35.2 us
    all_to_all x2, starting transfers between devices, gather_a2a(): got = lax.all_to_all(copies, axis_name, 0, 0, tiled=False)  32.2 us
    all_gather x1, waiting for transfers between devices, on_device(): left_rows = lax.all_gather(left, 'col', axis=1, tiled=True)  25.5 us
    ppermute x2, waiting for transfers between devices, sum_over_ka(): got = lax.ppermute(theirs.astype(jnp.bfloat16), 'ka', [(0, 1), (1, 0)])  22.9 us
    all_to_all x2, blocking collectives, split_rows_over_ka(): got = lax.all_to_all(halves, 'ka', 0, 0, tiled=False)  17.8 us
    all_gather x1, local copies, waits for them, and re-layouts, on_device(): left_rows = lax.all_gather(left, 'col', axis=1, tiled=True)  15.3 us
    ppermute x2, starting transfers between devices, transpose_tiles(): return lax.ppermute(value, ('row', 'col'), perm)  10.7 us
  transfers between devices with their start and end apart: 8, of which 7 were waited for; matrix products, arithmetic and copies ran while one was open for 8% of the time, Pallas kernels for 0%

profile of v4, /device:TPU:1, one launch (start us, length us, event | category | flops | bytes accessed | tf_op | source)
XLA Modules:
  0.0 301.6 jit_solution(12850776835299335418)
XLA Ops:
  12.0 4.5 %collective-permute-start = (bf16[32,16,128]{2,1,0:T(8,128)(2,1)S(1)}, bf16[32,16,128]{2,1,0:T(8,128)(2,1)S(1)}, u32[]{:S(2)}, u32[]{:S(2)}) collective-permute-start(bf16[32,16,128]{2,1,0:T(8,128)(2,1)S(1)} %get-tuple-element.8), channel_id=1, source_target_pairs={{0,0},{2,32},{4,64},{6,96},{8,128},{10,160},{12,192},{14,224},{16,... | collective-permute-start | bytes 393224 | tf_op jit(solution)/shard_map/ppermute | solution.py:38
  16.5 2.6 collective-permute-done
  19.1 1.7 broadcast_in_dim.6
  20.8 21.2 %all-to-all-start = ((bf16[16,32,16,128]{3,2,1,0:T(8,128)(2,1)}), bf16[16,32,16,128]{3,2,1,0:T(8,128)(2,1)S(1)}, u32[]{:S(2)}, u32[]{:S(2)}) async-start(bf16[16,32,16,128]{3,2,1,0:T(8,128)(2,1)} %broadcast_in_dim.6), calls=%async_computation | async-start | bytes 4194304 | tf_op jit(solution)/shard_map/all_to_all | solution.py:43
  42.1 25.5 %all-gather.3.cloned.1.call-done = bf16[32,256,128]{2,1,0:T(8,128)(2,1)} async-done(((bf16[32,16,128]{2,1,0:T(8,128)(2,1)}), bf16[32,256,128]{2,1,0:T(8,128)(2,1)}) %all-gather.3.cloned.1.call-update) | async-done | bytes 2097168 | tf_op jit(solution)/shard_map/all_gather | solution.py:68
  67.6 15.3 %copy.68 = bf16[32,256,128]{0,1,2:T(8,128)(2,1)} copy(bf16[32,256,128]{2,1,0:T(8,128)(2,1)} %all-gather.3.cloned.1.call-done) | data formatting | bytes 4194304 | tf_op jit(solution)/shard_map/all_gather | solution.py:68
  82.9 7.7 %all-to-all-done = bf16[16,32,16,128]{3,2,1,0:T(8,128)(2,1)S(1)} async-done(((bf16[16,32,16,128]{3,2,1,0:T(8,128)(2,1)}), bf16[16,32,16,128]{3,2,1,0:T(8,128)(2,1)S(1)}, u32[]{:S(2)}, u32[]{:S(2)}) %all-to-all-start) | async-done | bytes 2097184 | tf_op jit(solution)/shard_map/all_to_all | solution.py:43
  90.5 2.0 copy.66
  92.5 3.4 %copy.67 = bf16[32,256,128]{1,0,2:T(8,128)(2,1)S(1)} copy(bf16[32,256,128]{2,1,0:T(8,128)(2,1)} %bitcast.65) | data formatting | bytes 4194304 | tf_op jit(solution)/shard_map/reshape | solution.py:45
  95.9 4.6 %fusion.56 = f32[128,32,32]{2,1,0:T(8,128)S(1)} fusion(bf16[32,256,128]{1,0,2:T(8,128)(2,1)S(1)} %copy.67, bf16[32,256,128]{0,1,2:T(8,128)(2,1)} %copy.68), kind=kOutput, calls=%fused_computation.86 | convolution fusion | flops 67108864 | bytes 4718592 | tf_op jit(solution)/shard_map/ikc,jkc->ijc/dot_general | solution.py:70
  100.7 4.9 %collective-permute-start.1 = (bf16[32,16,128]{0,1,2:T(8,128)(2,1)S(1)}, bf16[32,16,128]{0,1,2:T(8,128)(2,1)S(1)}, u32[]{:S(2)}, u32[]{:S(2)}) collective-permute-start(bf16[32,16,128]{0,1,2:T(8,128)(2,1)S(1)} %fusion.11), channel_id=1, source_target_pairs={{0,1},{1,0},{2,3},{3,2},{4,5},{5,4},{6,7},{7,6},{8,9},{9,8},{10,11... | collective-permute-start | bytes 393224 | tf_op jit(solution)/shard_map/ppermute | solution.py:53
  106.0 8.7 %collective-permute-done.1 = bf16[32,16,128]{0,1,2:T(8,128)(2,1)S(1)} collective-permute-done((bf16[32,16,128]{0,1,2:T(8,128)(2,1)S(1)}, bf16[32,16,128]{0,1,2:T(8,128)(2,1)S(1)}, u32[]{:S(2)}, u32[]{:S(2)}) %collective-permute-start.1) | collective-permute-done | bytes 131104 | tf_op jit(solution)/shard_map/ppermute | solution.py:53
  117.2 9.5 %all_to_all.20 = bf16[2,16,16,128]{3,2,1,0:T(8,128)(2,1)S(1)} all-to-all(bf16[2,16,16,128]{3,2,1,0:T(8,128)(2,1)S(1)} %bitcast.69), channel_id=1, replica_groups=mesh['row'=16,'col'=16,'ka'=2] {'ka'}, dimensions={0} | all-to-all | bytes 262144 | tf_op jit(solution)/shard_map/all_to_all | solution.py:60
  127.2 6.2 %collective-permute-start.2 = (bf16[16,32,128]{1,0,2:T(8,128)(2,1)S(1)}, bf16[16,32,128]{1,0,2:T(8,128)(2,1)S(1)}, u32[]{:S(2)}, u32[]{:S(2)}) collective-permute-start(bf16[16,32,128]{1,0,2:T(8,128)(2,1)S(1)} %copy.76), channel_id=1, source_target_pairs={{0,0},{2,32},{4,64},{6,96},{8,128},{10,160},{12,192},{14,224},{16,... | collective-permute-start | bytes 393224 | tf_op jit(solution)/shard_map/ppermute | solution.py:38
  133.4 8.3 %all_to_all.21 = bf16[2,16,16,128]{3,2,1,0:T(8,128)(2,1)S(1)} all-to-all(bf16[2,16,16,128]{3,2,1,0:T(8,128)(2,1)S(1)} %bitcast.68), channel_id=1, replica_groups=mesh['row'=16,'col'=16,'ka'=2] {'ka'}, dimensions={0} | all-to-all | bytes 262144 | tf_op jit(solution)/shard_map/all_to_all | solution.py:60
  141.7 1.8 broadcast_in_dim.8
  143.5 11.0 %all-to-all-start.2 = ((bf16[16,16,32,128]{3,2,1,0:T(8,128)(2,1)}), bf16[16,16,32,128]{3,2,1,0:T(8,128)(2,1)S(1)}, u32[]{:S(2)}, u32[]{:S(2)}) async-start(bf16[16,16,32,128]{3,2,1,0:T(8,128)(2,1)} %broadcast_in_dim.8), calls=%async_computation.2 | async-start | bytes 4194304 | tf_op jit(solution)/shard_map/all_to_all | solution.py:43
  155.4 75.5 %all-to-all-done.2 = bf16[16,16,32,128]{3,2,1,0:T(8,128)(2,1)S(1)} async-done(((bf16[16,16,32,128]{3,2,1,0:T(8,128)(2,1)}), bf16[16,16,32,128]{3,2,1,0:T(8,128)(2,1)S(1)}, u32[]{:S(2)}, u32[]{:S(2)}) %all-to-all-start.2) | async-done | bytes 2097184 | tf_op jit(solution)/shard_map/all_to_all | solution.py:43
  230.9 1.4 copy-done
  232.3 3.9 %copy.77 = bf16[256,32,128]{0,1,2:T(8,128)(2,1)S(1)} copy(bf16[256,32,128]{2,1,0:T(8,128)(2,1)} %bitcast.64) | data formatting | bytes 4194304 | tf_op jit(solution)/shard_map/reshape | solution.py:45
  236.2 35.2 %all-gather.5.cloned.1.call-done = bf16[256,32,128]{1,0,2:T(8,128)(2,1)} async-done(((bf16[16,32,128]{1,0,2:T(8,128)(2,1)}), bf16[256,32,128]{1,0,2:T(8,128)(2,1)}) %all-gather.5.cloned.1.call-update) | async-done | bytes 2097168 | tf_op jit(solution)/shard_map/all_gather | solution.py:78
  271.4 4.6 %fusion.57 = f32[128,32,32]{2,1,0:T(8,128)S(1)} fusion(bf16[256,32,128]{0,1,2:T(8,128)(2,1)S(1)} %copy.77, bf16[256,32,128]{1,0,2:T(8,128)(2,1)} %all-gather.5.cloned.1.call-done), kind=kOutput, calls=%fused_computation.87 | convolution fusion | flops 67108864 | bytes 4718592 | tf_op jit(solution)/shard_map/kic,kjc->ijc/dot_general | solution.py:79
  276.2 2.0 collective-permute-start.3
  278.6 14.2 %collective-permute-done.3 = bf16[32,16,128]{0,1,2:T(8,128)(2,1)S(1)} collective-permute-done((bf16[32,16,128]{0,1,2:T(8,128)(2,1)S(1)}, bf16[32,16,128]{0,1,2:T(8,128)(2,1)S(1)}, u32[]{:S(2)}, u32[]{:S(2)}) %collective-permute-start.3) | collective-permute-done | bytes 131104 | tf_op jit(solution)/shard_map/ppermute | solution.py:53
  (60 shorter events, 12.2 us)
Async XLA Ops:
  6.5 61.1 %all-gather.3.cloned.1.call-start = ((), (), s32[]{:S(2)}) async-start(), calls=%async_computation.4 | async-start | bytes 2228224 | tf_op jit(solution)/shard_map/all_gather | solution.py:68
  12.0 7.1 %collective-permute-start = (bf16[32,16,128]{2,1,0:T(8,128)(2,1)S(1)}, bf16[32,16,128]{2,1,0:T(8,128)(2,1)S(1)}, u32[]{:S(2)}, u32[]{:S(2)}) collective-permute-start(bf16[32,16,128]{2,1,0:T(8,128)(2,1)S(1)} %get-tuple-element.8), channel_id=1, source_target_pairs={{0,0},{2,32},{4,64},{6,96},{8,128},{10,160},{12,192},{14,224},{16,... | collective-permute-start | bytes 393224 | tf_op jit(solution)/shard_map/ppermute | solution.py:38
  20.8 69.7 %all-to-all-start = ((bf16[16,32,16,128]{3,2,1,0:T(8,128)(2,1)}), bf16[16,32,16,128]{3,2,1,0:T(8,128)(2,1)S(1)}, u32[]{:S(2)}, u32[]{:S(2)}) async-start(bf16[16,32,16,128]{3,2,1,0:T(8,128)(2,1)} %broadcast_in_dim.6), calls=%async_computation | async-start | bytes 4194304 | tf_op jit(solution)/shard_map/all_to_all | solution.py:43
  95.9 9.7 %copy-start.1 = (bf16[32,16,128]{2,1,0:T(8,128)(2,1)S(1)}, bf16[32,16,128]{2,1,0:T(8,128)(2,1)}, u32[]{:S(2)}) copy-start(bf16[32,16,128]{2,1,0:T(8,128)(2,1)} %param.5) | copy-start | bytes 393220
  95.9 9.7 %copy-start.5 = (bf16[2,128,128]{2,1,0:T(8,128)(2,1)S(1)}, bf16[2,128,128]{2,1,0:T(8,128)(2,1)}, u32[]{:S(2)}) copy-start(bf16[2,128,128]{2,1,0:T(8,128)(2,1)} %param.8) | copy-start | bytes 196612
  100.7 13.9 %collective-permute-start.1 = (bf16[32,16,128]{0,1,2:T(8,128)(2,1)S(1)}, bf16[32,16,128]{0,1,2:T(8,128)(2,1)S(1)}, u32[]{:S(2)}, u32[]{:S(2)}) collective-permute-start(bf16[32,16,128]{0,1,2:T(8,128)(2,1)S(1)} %fusion.11), channel_id=1, source_target_pairs={{0,1},{1,0},{2,3},{3,2},{4,5},{5,4},{6,7},{7,6},{8,9},{9,8},{10,11... | collective-permute-start | bytes 393224 | tf_op jit(solution)/shard_map/ppermute | solution.py:53
  114.8 1.0 copy-start.4
  115.1 1.6 copy-start.3
  127.2 27.3 %collective-permute-start.2 = (bf16[16,32,128]{1,0,2:T(8,128)(2,1)S(1)}, bf16[16,32,128]{1,0,2:T(8,128)(2,1)S(1)}, u32[]{:S(2)}, u32[]{:S(2)}) collective-permute-start(bf16[16,32,128]{1,0,2:T(8,128)(2,1)S(1)} %copy.76), channel_id=1, source_target_pairs={{0,0},{2,32},{4,64},{6,96},{8,128},{10,160},{12,192},{14,224},{16,... | collective-permute-start | bytes 393224 | tf_op jit(solution)/shard_map/ppermute | solution.py:38
  143.5 87.4 %all-to-all-start.2 = ((bf16[16,16,32,128]{3,2,1,0:T(8,128)(2,1)}), bf16[16,16,32,128]{3,2,1,0:T(8,128)(2,1)S(1)}, u32[]{:S(2)}, u32[]{:S(2)}) async-start(bf16[16,16,32,128]{3,2,1,0:T(8,128)(2,1)} %broadcast_in_dim.8), calls=%async_computation.2 | async-start | bytes 4194304 | tf_op jit(solution)/shard_map/all_to_all | solution.py:43
  154.5 116.9 %all-gather.5.cloned.1.call-start = ((), (), s32[]{:S(2)}) async-start(), calls=%async_computation.5 | async-start | bytes 8912896 | tf_op jit(solution)/shard_map/all_gather | solution.py:78
  154.6 0.8 copy-start.2
  230.9 1.4 copy-start
  236.2 42.0 %copy-start.6 = (bf16[2,128,128]{2,1,0:T(8,128)(2,1)S(1)}, bf16[2,128,128]{2,1,0:T(8,128)(2,1)}, u32[]{:S(2)}) copy-start(bf16[2,128,128]{2,1,0:T(8,128)(2,1)} %param.8) | copy-start | bytes 196612
  276.2 16.6 %collective-permute-start.3 = (bf16[32,16,128]{0,1,2:T(8,128)(2,1)S(1)}, bf16[32,16,128]{0,1,2:T(8,128)(2,1)S(1)}, u32[]{:S(2)}, u32[]{:S(2)}) collective-permute-start(bf16[32,16,128]{0,1,2:T(8,128)(2,1)S(1)} %fusion.12), channel_id=1, source_target_pairs={{0,1},{1,0},{2,3},{3,2},{4,5},{5,4},{6,7},{7,6},{8,9},{9,8},{10,11... | collective-permute-start | bytes 393224 | tf_op jit(solution)/shard_map/ppermute | solution.py:53
Sparse Core Ops, SparseCore 0:
  16.6 50.9 all-gather.2
  157.4 114.0 all-gather.4

commit v5 on v3

--- a/solution.py
+++ b/solution.py
@@ -54,6 +54,14 @@
     return mine + got.astype(jnp.float32)
 
 
+def join_over_ka(value):
+    me = lax.axis_index("ka")
+    got = lax.ppermute(value, "ka", [(0, 1), (1, 0)])
+    return jnp.where(
+        me == 0, jnp.concatenate([value, got], axis=1), jnp.concatenate([got, value], axis=1)
+    )
+
+
 def on_device(n, pair, pair_mask, w_in, w_gate, w_out):
     valid = pair_mask.astype(jnp.float32)[..., None]
     left, right, gate = prepare(pair, valid, w_in[0], w_gate[0])
@@ -66,8 +74,8 @@
     middle = finish(pair, tri, gate, w_out[0])
     left, right, gate = prepare(middle, valid, w_in[1], w_gate[1])
     right_cols = gather_a2a(right, "row", n, 0)
-    left_half = lax.all_gather(transpose_tiles(left, n), "col", axis=0, tiled=True)
-    left_diag = lax.all_gather(left_half, "ka", axis=1, tiled=True)
+    left_tile = join_over_ka(transpose_tiles(left, n))
+    left_diag = lax.all_gather(left_tile, "col", axis=0, tiled=True)
     tri = jnp.einsum("kic,kjc->ijc", left_diag, right_cols, preferred_element_type=jnp.float32)
     return finish(middle, tri, gate, w_out[1])
 

time: 285 us -> 248 us (0.87)
  waiting for transfers between devices: 175 us -> 100 us
  local copies, waits for them, and re-layouts: 35.1 us -> 54.2 us
  starting transfers between devices: 44.1 us -> 56.2 us
  matrix products: 12.1 us -> 15.1 us
    all_gather x2 -> x1, waiting for transfers between devices: 79.3 us -> 0.02 us  [on_device(): left_diag = lax.all_gather(left_tile, 'col', axis=0, tiled=True)]
    all_gather x1, local copies, waits for them, and re-layouts: 4.95 us -> 23.1 us  [on_device(): left_diag = lax.all_gather(left_tile, 'col', axis=0, tiled=True)]
    all_to_all x2, starting transfers between devices: 28.7 us -> 38.5 us  [gather_a2a(): got = lax.all_to_all(copies, axis_name, 0, 0, tiled=False)]
    ppermute x0 -> x1, starting transfers between devices: none -> 3.73 us  [join_over_ka(): got = lax.ppermute(value, 'ka', [(0, 1), (1, 0)])]
    ppermute x0 -> x1, waiting for transfers between devices: none -> 3.47 us  [join_over_ka(): got = lax.ppermute(value, 'ka', [(0, 1), (1, 0)])]
    dot_general x1, matrix products: 4.03 us -> 7.05 us  [on_device(): jnp.einsum('kic,kjc->ijc', left_diag, right_cols, preferred_element_type=...]
  transfers between devices with their start and end apart: 8 -> 8, of which waited for: 8 -> 7; matrix products, arithmetic and copies ran while one was open for 8% -> 9% of each run, Pallas kernels for 0% -> 0%
where the time goes in v5:
time: 248 us; the launch traced here: 246 us
  waiting for transfers between devices  100 us (40%)
  starting transfers between devices  56.2 us (23%)
  local copies, waits for them, and re-layouts  54.2 us (22%)
  matrix products  15.1 us (6%)
  between operations  13.7 us (6%)
  other arithmetic  5.97 us (2%)
    all_to_all x2, waiting for transfers between devices, gather_a2a(): got = lax.all_to_all(copies, axis_name, 0, 0, tiled=False)  55.5 us
    all_to_all x2, starting transfers between devices, gather_a2a(): got = lax.all_to_all(copies, axis_name, 0, 0, tiled=False)  38.5 us
    all_gather x1, waiting for transfers between devices, on_device(): left_rows = lax.all_gather(left, 'col', axis=1, tiled=True)  25.5 us
    all_gather x1, local copies, waits for them, and re-layouts, on_device(): left_diag = lax.all_gather(left_tile, 'col', axis=0, tiled=True)  23.1 us
    all_gather x1, local copies, waits for them, and re-layouts, on_device(): left_rows = lax.all_gather(left, 'col', axis=1, tiled=True)  15.2 us
    ppermute x1, waiting for transfers between devices, sum_over_ka(): got = lax.ppermute(theirs.astype(jnp.bfloat16), 'ka', [(0, 1), (1, 0)])  9.96 us
    ppermute x2, starting transfers between devices, transpose_tiles(): return lax.ppermute(value, ('row', 'col'), perm)  9.72 us
    reshape x2, local copies, waits for them, and re-layouts, gather_a2a(): got.reshape(value.shape[:axis] + (n * value.shape[axis],) + value.shape[a...  7.31 us
  transfers between devices with their start and end apart: 8, of which 7 were waited for; matrix products, arithmetic and copies ran while one was open for 9% of the time, Pallas kernels for 0%

profile of v5, /device:TPU:1, one launch (start us, length us, event | category | flops | bytes accessed | tf_op | source)
XLA Modules:
  0.0 245.6 jit_solution(1125124166623002917)
XLA Ops:
  9.8 1.3 fusion.39
  12.0 4.5 %collective-permute-start = (bf16[32,16,128]{2,1,0:T(8,128)(2,1)S(1)}, bf16[32,16,128]{2,1,0:T(8,128)(2,1)S(1)}, u32[]{:S(2)}, u32[]{:S(2)}) collective-permute-start(bf16[32,16,128]{2,1,0:T(8,128)(2,1)S(1)} %get-tuple-element.8), channel_id=1, source_target_pairs={{0,0},{2,32},{4,64},{6,96},{8,128},{10,160},{12,192},{14,224},{16,... | collective-permute-start | bytes 393224 | tf_op jit(solution)/shard_map/ppermute | solution.py:38
  16.5 2.6 %collective-permute-done = bf16[32,16,128]{2,1,0:T(8,128)(2,1)S(1)} collective-permute-done((bf16[32,16,128]{2,1,0:T(8,128)(2,1)S(1)}, bf16[32,16,128]{2,1,0:T(8,128)(2,1)S(1)}, u32[]{:S(2)}, u32[]{:S(2)}) %collective-permute-start) | collective-permute-done | bytes 131104 | tf_op jit(solution)/shard_map/ppermute | solution.py:38
  19.1 1.7 broadcast_in_dim.4
  20.8 21.2 %all-to-all-start = ((bf16[16,32,16,128]{3,2,1,0:T(8,128)(2,1)}), bf16[16,32,16,128]{3,2,1,0:T(8,128)(2,1)S(1)}, u32[]{:S(2)}, u32[]{:S(2)}) async-start(bf16[16,32,16,128]{3,2,1,0:T(8,128)(2,1)} %broadcast_in_dim.4), calls=%async_computation | async-start | bytes 4194304 | tf_op jit(solution)/shard_map/all_to_all | solution.py:43
  42.1 25.5 %all-gather.3.cloned.1.call-done = bf16[32,256,128]{2,1,0:T(8,128)(2,1)} async-done(((bf16[32,16,128]{2,1,0:T(8,128)(2,1)}), bf16[32,256,128]{2,1,0:T(8,128)(2,1)}) %all-gather.3.cloned.1.call-update) | async-done | bytes 2097168 | tf_op jit(solution)/shard_map/all_gather | solution.py:68
  67.6 15.2 %copy.63 = bf16[32,256,128]{0,1,2:T(8,128)(2,1)} copy(bf16[32,256,128]{2,1,0:T(8,128)(2,1)} %all-gather.3.cloned.1.call-done) | data formatting | bytes 4194304 | tf_op jit(solution)/shard_map/all_gather | solution.py:68
  82.8 8.2 %all-to-all-done = bf16[16,32,16,128]{3,2,1,0:T(8,128)(2,1)S(1)} async-done(((bf16[16,32,16,128]{3,2,1,0:T(8,128)(2,1)}), bf16[16,32,16,128]{3,2,1,0:T(8,128)(2,1)S(1)}, u32[]{:S(2)}, u32[]{:S(2)}) %all-to-all-start) | async-done | bytes 2097184 | tf_op jit(solution)/shard_map/all_to_all | solution.py:43
  91.1 2.0 copy.61
  93.1 3.4 %copy.62 = bf16[32,256,128]{1,0,2:T(8,128)(2,1)S(1)} copy(bf16[32,256,128]{2,1,0:T(8,128)(2,1)} %bitcast.49) | data formatting | bytes 4194304 | tf_op jit(solution)/shard_map/reshape | solution.py:45
  96.5 4.6 %fusion.55 = f32[128,32,32]{2,1,0:T(8,128)S(1)} fusion(bf16[32,256,128]{1,0,2:T(8,128)(2,1)S(1)} %copy.62, bf16[32,256,128]{0,1,2:T(8,128)(2,1)} %copy.63), kind=kOutput, calls=%fused_computation.85 | convolution fusion | flops 67108864 | bytes 4718592 | tf_op jit(solution)/shard_map/ikc,jkc->ijc/dot_general | solution.py:70
  101.3 4.3 %collective-permute-start.1 = (bf16[32,16,128]{0,1,2:T(8,128)(2,1)S(1)}, bf16[32,16,128]{0,1,2:T(8,128)(2,1)S(1)}, u32[]{:S(2)}, u32[]{:S(2)}) collective-permute-start(bf16[32,16,128]{0,1,2:T(8,128)(2,1)S(1)} %fusion.11), channel_id=1, source_target_pairs={{0,1},{1,0},{2,3},{3,2},{4,5},{5,4},{6,7},{7,6},{8,9},{9,8},{10,11... | collective-permute-start | bytes 393224 | tf_op jit(solution)/shard_map/ppermute | solution.py:53
  105.9 10.0 %collective-permute-done.1 = bf16[32,16,128]{0,1,2:T(8,128)(2,1)S(1)} collective-permute-done((bf16[32,16,128]{0,1,2:T(8,128)(2,1)S(1)}, bf16[32,16,128]{0,1,2:T(8,128)(2,1)S(1)}, u32[]{:S(2)}, u32[]{:S(2)}) %collective-permute-start.1) | collective-permute-done | bytes 131104 | tf_op jit(solution)/shard_map/ppermute | solution.py:53
  118.4 5.2 %collective-permute-start.2 = (bf16[32,16,128]{2,1,0:T(8,128)(2,1)S(1)}, bf16[32,16,128]{2,1,0:T(8,128)(2,1)S(1)}, u32[]{:S(2)}, u32[]{:S(2)}) collective-permute-start(bf16[32,16,128]{2,1,0:T(8,128)(2,1)S(1)} %get-tuple-element.5), channel_id=1, source_target_pairs={{0,0},{2,32},{4,64},{6,96},{8,128},{10,160},{12,192},{14,224},{16,... | collective-permute-start | bytes 393224 | tf_op jit(solution)/shard_map/ppermute | solution.py:38
  123.7 3.3 %collective-permute-done.2 = bf16[32,16,128]{2,1,0:T(8,128)(2,1)S(1)} collective-permute-done((bf16[32,16,128]{2,1,0:T(8,128)(2,1)S(1)}, bf16[32,16,128]{2,1,0:T(8,128)(2,1)S(1)}, u32[]{:S(2)}, u32[]{:S(2)}) %collective-permute-start.2) | collective-permute-done | bytes 131104 | tf_op jit(solution)/shard_map/ppermute | solution.py:38
  127.0 3.7 %collective-permute-start.3 = (bf16[32,16,128]{2,1,0:T(8,128)(2,1)S(1)}, bf16[32,16,128]{2,1,0:T(8,128)(2,1)S(1)}, u32[]{:S(2)}, u32[]{:S(2)}) collective-permute-start(bf16[32,16,128]{2,1,0:T(8,128)(2,1)S(1)} %collective-permute-done.2), channel_id=1, source_target_pairs={{0,1},{1,0},{2,3},{3,2},{4,5},{5,4},{6,7},{7,6},{8,9},{9,8},{10,11... | collective-permute-start | bytes 393224 | tf_op jit(solution)/shard_map/ppermute | solution.py:59
  130.7 3.5 %collective-permute-done.3 = bf16[32,16,128]{2,1,0:T(8,128)(2,1)S(1)} collective-permute-done((bf16[32,16,128]{2,1,0:T(8,128)(2,1)S(1)}, bf16[32,16,128]{2,1,0:T(8,128)(2,1)S(1)}, u32[]{:S(2)}, u32[]{:S(2)}) %collective-permute-start.3) | collective-permute-done | bytes 131104 | tf_op jit(solution)/shard_map/ppermute | solution.py:59
  135.1 1.8 broadcast_in_dim.5
  136.8 17.2 %all-to-all-start.1 = ((bf16[16,32,16,128]{3,2,1,0:T(8,128)(2,1)}), bf16[16,32,16,128]{3,2,1,0:T(8,128)(2,1)S(1)}, u32[]{:S(2)}, u32[]{:S(2)}) async-start(bf16[16,32,16,128]{3,2,1,0:T(8,128)(2,1)} %broadcast_in_dim.5), calls=%async_computation.1 | async-start | bytes 4194304 | tf_op jit(solution)/shard_map/all_to_all | solution.py:43
  154.4 47.2 %all-to-all-done.1 = bf16[16,32,16,128]{3,2,1,0:T(8,128)(2,1)S(1)} async-done(((bf16[16,32,16,128]{3,2,1,0:T(8,128)(2,1)}), bf16[16,32,16,128]{3,2,1,0:T(8,128)(2,1)S(1)}, u32[]{:S(2)}, u32[]{:S(2)}) %all-to-all-start.1) | async-done | bytes 2097184 | tf_op jit(solution)/shard_map/all_to_all | solution.py:43
  201.7 1.3 copy-done
  203.0 3.9 %copy.69 = bf16[512,16,128]{0,1,2:T(8,128)(2,1)S(1)} copy(bf16[512,16,128]{2,1,0:T(8,128)(2,1)} %bitcast.48) | data formatting | bytes 4194304 | tf_op jit(solution)/shard_map/reshape | solution.py:45
  207.0 23.1 %copy.70 = bf16[512,32,128]{1,0,2:T(8,128)(2,1)} copy(bf16[512,32,128]{2,1,0:T(8,128)(2,1)} %all-gather.5.cloned.1.call-done) | data formatting | bytes 8388608 | tf_op jit(solution)/shard_map/all_gather | solution.py:78
  230.0 7.0 %fusion.54 = (f32[32,16]{0,1:T(8,128)S(1)}, f32[32,16,128]{0,1,2:T(8,128)S(1)}) fusion(bf16[512,16,128]{0,1,2:T(8,128)(2,1)S(1)} %copy.69, bf16[512,32,128]{1,0,2:T(8,128)(2,1)} %copy.70), kind=kOutput, calls=%fused_computation.84 | convolution fusion | flops 67173888 | bytes 6555648 | tf_op jit(solution)/shard_map/kic,kjc->ijc/dot_general | solution.py:79
  (51 shorter events, 10.0 us)
Async XLA Ops:
  6.5 61.1 %all-gather.3.cloned.1.call-start = ((), (), s32[]{:S(2)}) async-start(), calls=%async_computation.2 | async-start | bytes 2228224 | tf_op jit(solution)/shard_map/all_gather | solution.py:68
  12.0 7.1 %collective-permute-start = (bf16[32,16,128]{2,1,0:T(8,128)(2,1)S(1)}, bf16[32,16,128]{2,1,0:T(8,128)(2,1)S(1)}, u32[]{:S(2)}, u32[]{:S(2)}) collective-permute-start(bf16[32,16,128]{2,1,0:T(8,128)(2,1)S(1)} %get-tuple-element.8), channel_id=1, source_target_pairs={{0,0},{2,32},{4,64},{6,96},{8,128},{10,160},{12,192},{14,224},{16,... | collective-permute-start | bytes 393224 | tf_op jit(solution)/shard_map/ppermute | solution.py:38
  20.8 70.2 %all-to-all-start = ((bf16[16,32,16,128]{3,2,1,0:T(8,128)(2,1)}), bf16[16,32,16,128]{3,2,1,0:T(8,128)(2,1)S(1)}, u32[]{:S(2)}, u32[]{:S(2)}) async-start(bf16[16,32,16,128]{3,2,1,0:T(8,128)(2,1)} %broadcast_in_dim.4), calls=%async_computation | async-start | bytes 4194304 | tf_op jit(solution)/shard_map/all_to_all | solution.py:43
  42.1 164.9 %all-gather.5.cloned.1.call-start = ((), (), s32[]{:S(2)}) async-start(), calls=%async_computation.3 | async-start | bytes 4456448 | tf_op jit(solution)/shard_map/all_gather | solution.py:78
  96.5 9.1 %copy-start.1 = (bf16[32,16,128]{2,1,0:T(8,128)(2,1)S(1)}, bf16[32,16,128]{2,1,0:T(8,128)(2,1)}, u32[]{:S(2)}) copy-start(bf16[32,16,128]{2,1,0:T(8,128)(2,1)} %param.5) | copy-start | bytes 393220
  96.5 9.1 %copy-start.4 = (bf16[2,128,128]{2,1,0:T(8,128)(2,1)S(1)}, bf16[2,128,128]{2,1,0:T(8,128)(2,1)}, u32[]{:S(2)}) copy-start(bf16[2,128,128]{2,1,0:T(8,128)(2,1)} %param.8) | copy-start | bytes 196612
  101.3 14.6 %collective-permute-start.1 = (bf16[32,16,128]{0,1,2:T(8,128)(2,1)S(1)}, bf16[32,16,128]{0,1,2:T(8,128)(2,1)S(1)}, u32[]{:S(2)}, u32[]{:S(2)}) collective-permute-start(bf16[32,16,128]{0,1,2:T(8,128)(2,1)S(1)} %fusion.11), channel_id=1, source_target_pairs={{0,1},{1,0},{2,3},{3,2},{4,5},{5,4},{6,7},{7,6},{8,9},{9,8},{10,11... | collective-permute-start | bytes 393224 | tf_op jit(solution)/shard_map/ppermute | solution.py:53
  116.1 1.0 copy-start.3
  116.3 1.6 copy-start.2
  118.4 8.6 %collective-permute-start.2 = (bf16[32,16,128]{2,1,0:T(8,128)(2,1)S(1)}, bf16[32,16,128]{2,1,0:T(8,128)(2,1)S(1)}, u32[]{:S(2)}, u32[]{:S(2)}) collective-permute-start(bf16[32,16,128]{2,1,0:T(8,128)(2,1)S(1)} %get-tuple-element.5), channel_id=1, source_target_pairs={{0,0},{2,32},{4,64},{6,96},{8,128},{10,160},{12,192},{14,224},{16,... | collective-permute-start | bytes 393224 | tf_op jit(solution)/shard_map/ppermute | solution.py:38
  127.0 7.2 %collective-permute-start.3 = (bf16[32,16,128]{2,1,0:T(8,128)(2,1)S(1)}, bf16[32,16,128]{2,1,0:T(8,128)(2,1)S(1)}, u32[]{:S(2)}, u32[]{:S(2)}) collective-permute-start(bf16[32,16,128]{2,1,0:T(8,128)(2,1)S(1)} %collective-permute-done.2), channel_id=1, source_target_pairs={{0,1},{1,0},{2,3},{3,2},{4,5},{5,4},{6,7},{7,6},{8,9},{9,8},{10,11... | collective-permute-start | bytes 393224 | tf_op jit(solution)/shard_map/ppermute | solution.py:59
  136.8 64.8 %all-to-all-start.1 = ((bf16[16,32,16,128]{3,2,1,0:T(8,128)(2,1)}), bf16[16,32,16,128]{3,2,1,0:T(8,128)(2,1)S(1)}, u32[]{:S(2)}, u32[]{:S(2)}) async-start(bf16[16,32,16,128]{3,2,1,0:T(8,128)(2,1)} %broadcast_in_dim.5), calls=%async_computation.1 | async-start | bytes 4194304 | tf_op jit(solution)/shard_map/all_to_all | solution.py:43
  201.7 1.4 copy-start
Sparse Core Ops, SparseCore 0:
  16.6 50.9 all-gather.2
  135.2 59.6 all-gather.4

commit v6 on v5

--- a/solution.py
+++ b/solution.py
@@ -76,7 +76,9 @@
     right_cols = gather_a2a(right, "row", n, 0)
     left_tile = join_over_ka(transpose_tiles(left, n))
     left_diag = lax.all_gather(left_tile, "col", axis=0, tiled=True)
-    tri = jnp.einsum("kic,kjc->ijc", left_diag, right_cols, preferred_element_type=jnp.float32)
+    tri = jnp.sum(
+        left_diag[:, :, None].astype(jnp.float32) * right_cols[:, None].astype(jnp.float32), axis=0
+    )
     return finish(middle, tri, gate, w_out[1])
 
 

time: 248 us -> 233 us (0.940)
  local copies, waits for them, and re-layouts: 54.2 us -> 26.3 us
  other arithmetic: 5.97 us -> 23.6 us
  matrix products: 15.1 us -> 10.5 us
    all_gather x1 -> x0, local copies, waits for them, and re-layouts: 23.1 us -> none  [on_device(): left_diag = lax.all_gather(left_tile, 'col', axis=0, tiled=True)]
    reduce_sum x2 -> x3, other arithmetic: 1.22 us -> 13.2 us  [layer_norm(): mean = jnp.mean(value, axis=-1, keepdims=True)]
    dot_general x1 -> x0, matrix products: 7.05 us -> none  [on_device(): jnp.einsum('kic,kjc->ijc', left_diag, right_cols, preferred_element_type=...]
    convert_element_type x0 -> x2, other arithmetic: none -> 5.81 us  [the longest x1 3.52 us: on_device(): left_diag[:, :, None].astype(jnp.float32)]
    reshape x2 -> x1, local copies, waits for them, and re-layouts: 7.31 us -> 4.61 us  [gather_a2a(): got.reshape(value.shape[:axis] + (n * value.shape[axis],) + value.shape[a...]
where the time goes in v6:
time: 233 us; the launch traced here: 231 us
  waiting for transfers between devices  100 us (43%)
  starting transfers between devices  56.5 us (24%)
  local copies, waits for them, and re-layouts  26.3 us (11%)
  other arithmetic  23.6 us (10%)
  between operations  13.7 us (6%)
  matrix products  10.5 us (5%)
    all_to_all x2, waiting for transfers between devices, gather_a2a(): got = lax.all_to_all(copies, axis_name, 0, 0, tiled=False)  55.5 us
    all_to_all x2, starting transfers between devices, gather_a2a(): got = lax.all_to_all(copies, axis_name, 0, 0, tiled=False)  38.7 us
    all_gather x1, waiting for transfers between devices, on_device(): left_rows = lax.all_gather(left, 'col', axis=1, tiled=True)  25.5 us
    all_gather x1, local copies, waits for them, and re-layouts, on_device(): left_rows = lax.all_gather(left, 'col', axis=1, tiled=True)  15.3 us
    reduce_sum x3, other arithmetic, layer_norm(): mean = jnp.mean(value, axis=-1, keepdims=True)  13.2 us
    ppermute x1, waiting for transfers between devices, sum_over_ka(): got = lax.ppermute(theirs.astype(jnp.bfloat16), 'ka', [(0, 1), (1, 0)])  9.99 us
    ppermute x2, starting transfers between devices, transpose_tiles(): return lax.ppermute(value, ('row', 'col'), perm)  9.72 us
    ppermute x2, waiting for transfers between devices, transpose_tiles(): return lax.ppermute(value, ('row', 'col'), perm)  5.81 us
  transfers between devices with their start and end apart: 8, of which 7 were waited for; matrix products, arithmetic and copies ran while one was open for 9% of the time, Pallas kernels for 0%

profile of v6, /device:TPU:1, one launch (start us, length us, event | category | flops | bytes accessed | tf_op | source)
XLA Modules:
  0.0 230.8 jit_solution(264574278774812957)
XLA Ops:
  9.6 1.3 fusion.39
  11.7 4.5 %collective-permute-start = (bf16[32,16,128]{2,1,0:T(8,128)(2,1)S(1)}, bf16[32,16,128]{2,1,0:T(8,128)(2,1)S(1)}, u32[]{:S(2)}, u32[]{:S(2)}) collective-permute-start(bf16[32,16,128]{2,1,0:T(8,128)(2,1)S(1)} %get-tuple-element.10), channel_id=1, source_target_pairs={{0,0},{2,32},{4,64},{6,96},{8,128},{10,160},{12,192},{14,224},{16,... | collective-permute-start | bytes 393224 | tf_op jit(solution)/shard_map/ppermute | solution.py:38
  16.2 2.6 %collective-permute-done = bf16[32,16,128]{2,1,0:T(8,128)(2,1)S(1)} collective-permute-done((bf16[32,16,128]{2,1,0:T(8,128)(2,1)S(1)}, bf16[32,16,128]{2,1,0:T(8,128)(2,1)S(1)}, u32[]{:S(2)}, u32[]{:S(2)}) %collective-permute-start) | collective-permute-done | bytes 131104 | tf_op jit(solution)/shard_map/ppermute | solution.py:38
  18.9 1.7 broadcast_in_dim.4
  20.6 21.2 %all-to-all-start = ((bf16[16,32,16,128]{3,2,1,0:T(8,128)(2,1)}), bf16[16,32,16,128]{3,2,1,0:T(8,128)(2,1)S(1)}, u32[]{:S(2)}, u32[]{:S(2)}) async-start(bf16[16,32,16,128]{3,2,1,0:T(8,128)(2,1)} %broadcast_in_dim.4), calls=%async_computation | async-start | bytes 4194304 | tf_op jit(solution)/shard_map/all_to_all | solution.py:43
  41.9 25.5 %all-gather.3.cloned.1.call-done = bf16[32,256,128]{2,1,0:T(8,128)(2,1)} async-done(((bf16[32,16,128]{2,1,0:T(8,128)(2,1)}), bf16[32,256,128]{2,1,0:T(8,128)(2,1)}) %all-gather.3.cloned.1.call-update) | async-done | bytes 2097168 | tf_op jit(solution)/shard_map/all_gather | solution.py:68
  67.3 15.3 %copy.41 = bf16[32,256,128]{0,1,2:T(8,128)(2,1)} copy(bf16[32,256,128]{2,1,0:T(8,128)(2,1)} %all-gather.3.cloned.1.call-done) | data formatting | bytes 4194304 | tf_op jit(solution)/shard_map/all_gather | solution.py:68
  82.6 8.2 %all-to-all-done = bf16[16,32,16,128]{3,2,1,0:T(8,128)(2,1)S(1)} async-done(((bf16[16,32,16,128]{3,2,1,0:T(8,128)(2,1)}), bf16[16,32,16,128]{3,2,1,0:T(8,128)(2,1)S(1)}, u32[]{:S(2)}, u32[]{:S(2)}) %all-to-all-start) | async-done | bytes 2097184 | tf_op jit(solution)/shard_map/all_to_all | solution.py:43
  90.8 1.9 copy.39
  92.7 4.6 %copy.40 = bf16[32,256,128]{1,0,2:T(8,128)(2,1)} copy(bf16[32,256,128]{2,1,0:T(8,128)(2,1)} %bitcast.45) | data formatting | bytes 4194304 | tf_op jit(solution)/shard_map/reshape | solution.py:45
  97.3 5.3 %fusion.56 = f32[128,32,32]{2,1,0:T(8,128)S(1)} fusion(bf16[32,256,128]{1,0,2:T(8,128)(2,1)} %copy.40, bf16[32,256,128]{0,1,2:T(8,128)(2,1)} %copy.41), kind=kOutput, calls=%fused_computation.87 | convolution fusion | flops 67108864 | bytes 4718592 | tf_op jit(solution)/shard_map/ikc,jkc->ijc/dot_general | solution.py:70
  102.8 4.2 %collective-permute-start.1 = (bf16[32,16,128]{0,1,2:T(8,128)(2,1)S(1)}, bf16[32,16,128]{0,1,2:T(8,128)(2,1)S(1)}, u32[]{:S(2)}, u32[]{:S(2)}) collective-permute-start(bf16[32,16,128]{0,1,2:T(8,128)(2,1)S(1)} %fusion.11), channel_id=1, source_target_pairs={{0,1},{1,0},{2,3},{3,2},{4,5},{5,4},{6,7},{7,6},{8,9},{9,8},{10,11... | collective-permute-start | bytes 393224 | tf_op jit(solution)/shard_map/ppermute | solution.py:53
  107.4 10.0 %collective-permute-done.1 = bf16[32,16,128]{0,1,2:T(8,128)(2,1)S(1)} collective-permute-done((bf16[32,16,128]{0,1,2:T(8,128)(2,1)S(1)}, bf16[32,16,128]{0,1,2:T(8,128)(2,1)S(1)}, u32[]{:S(2)}, u32[]{:S(2)}) %collective-permute-start.1) | collective-permute-done | bytes 131104 | tf_op jit(solution)/shard_map/ppermute | solution.py:53
  120.1 1.3 fusion.37
  121.6 5.2 %collective-permute-start.2 = (bf16[32,16,128]{2,1,0:T(8,128)(2,1)S(1)}, bf16[32,16,128]{2,1,0:T(8,128)(2,1)S(1)}, u32[]{:S(2)}, u32[]{:S(2)}) collective-permute-start(bf16[32,16,128]{2,1,0:T(8,128)(2,1)S(1)} %get-tuple-element.7), channel_id=1, source_target_pairs={{0,0},{2,32},{4,64},{6,96},{8,128},{10,160},{12,192},{14,224},{16,... | collective-permute-start | bytes 393224 | tf_op jit(solution)/shard_map/ppermute | solution.py:38
  126.8 3.2 %collective-permute-done.2 = bf16[32,16,128]{2,1,0:T(8,128)(2,1)S(1)} collective-permute-done((bf16[32,16,128]{2,1,0:T(8,128)(2,1)S(1)}, bf16[32,16,128]{2,1,0:T(8,128)(2,1)S(1)}, u32[]{:S(2)}, u32[]{:S(2)}) %collective-permute-start.2) | collective-permute-done | bytes 131104 | tf_op jit(solution)/shard_map/ppermute | solution.py:38
  130.0 3.8 %collective-permute-start.3 = (bf16[32,16,128]{2,1,0:T(8,128)(2,1)S(1)}, bf16[32,16,128]{2,1,0:T(8,128)(2,1)S(1)}, u32[]{:S(2)}, u32[]{:S(2)}) collective-permute-start(bf16[32,16,128]{2,1,0:T(8,128)(2,1)S(1)} %collective-permute-done.2), channel_id=1, source_target_pairs={{0,1},{1,0},{2,3},{3,2},{4,5},{5,4},{6,7},{7,6},{8,9},{9,8},{10,11... | collective-permute-start | bytes 393224 | tf_op jit(solution)/shard_map/ppermute | solution.py:59
  133.8 3.4 %collective-permute-done.3 = bf16[32,16,128]{2,1,0:T(8,128)(2,1)S(1)} collective-permute-done((bf16[32,16,128]{2,1,0:T(8,128)(2,1)S(1)}, bf16[32,16,128]{2,1,0:T(8,128)(2,1)S(1)}, u32[]{:S(2)}, u32[]{:S(2)}) %collective-permute-start.3) | collective-permute-done | bytes 131104 | tf_op jit(solution)/shard_map/ppermute | solution.py:59
  138.1 1.7 broadcast_in_dim.5
  139.8 17.5 %all-to-all-start.1 = ((bf16[16,32,16,128]{3,2,1,0:T(8,128)(2,1)}), bf16[16,32,16,128]{3,2,1,0:T(8,128)(2,1)S(1)}, u32[]{:S(2)}, u32[]{:S(2)}) async-start(bf16[16,32,16,128]{3,2,1,0:T(8,128)(2,1)} %broadcast_in_dim.5), calls=%async_computation.1 | async-start | bytes 4194304 | tf_op jit(solution)/shard_map/all_to_all | solution.py:43
  157.7 47.2 %all-to-all-done.1 = bf16[16,32,16,128]{3,2,1,0:T(8,128)(2,1)S(1)} async-done(((bf16[16,32,16,128]{3,2,1,0:T(8,128)(2,1)}), bf16[16,32,16,128]{3,2,1,0:T(8,128)(2,1)S(1)}, u32[]{:S(2)}, u32[]{:S(2)}) %all-to-all-start.1) | async-done | bytes 2097184 | tf_op jit(solution)/shard_map/all_to_all | solution.py:43
  204.9 2.3 convert.1
  207.2 3.5 %convert_element_type.78 = f32[512,32,128]{2,1,0:T(8,128)S(1)} convert(bf16[512,32,128]{2,1,0:T(8,128)(2,1)} %all-gather.5.cloned.1.call-done) | non-fusion elementwise | flops 2097152 | bytes 12582912 | tf_op jit(solution)/shard_map/convert_element_type | solution.py:80
  210.8 12.0 %multiply_reduce_fusion = (f32[32,16]{1,0:T(8,128)S(1)}, f32[32,16,128]{2,1,0:T(8,128)S(1)}) fusion(f32[512,16,128]{2,1,0:T(8,128)S(1)} %copy-done, f32[512,32,128]{2,1,0:T(8,128)S(1)} %convert_element_type.78), kind=kLoop, calls=%fused_computation | loop fusion | flops 100597248 | bytes 12847104 | tf_op jit(solution)/shard_map/reduce_sum | solution.py:8
  (53 shorter events, 9.7 us)
Async XLA Ops:
  6.5 60.8 %all-gather.3.cloned.1.call-start = ((), (), s32[]{:S(2)}) async-start(), calls=%async_computation.2 | async-start | bytes 2228224 | tf_op jit(solution)/shard_map/all_gather | solution.py:68
  8.8 3.0 %copy-start.4 = (f32[32,16]{1,0:T(8,128)}, f32[32,16]{1,0:T(8,128)S(1)}, u32[]{:S(2)}) copy-start(f32[32,16]{1,0:T(8,128)S(1)} %add_sqrt_fusion.3) | copy-start | bytes 6148
  9.6 11.0 %copy-start.2 = (f32[32,16]{1,0:T(8,128)}, f32[32,16]{1,0:T(8,128)S(1)}, u32[]{:S(2)}) copy-start(f32[32,16]{1,0:T(8,128)S(1)} %copy.38) | copy-start | bytes 6148
  11.7 7.1 %collective-permute-start = (bf16[32,16,128]{2,1,0:T(8,128)(2,1)S(1)}, bf16[32,16,128]{2,1,0:T(8,128)(2,1)S(1)}, u32[]{:S(2)}, u32[]{:S(2)}) collective-permute-start(bf16[32,16,128]{2,1,0:T(8,128)(2,1)S(1)} %get-tuple-element.10), channel_id=1, source_target_pairs={{0,0},{2,32},{4,64},{6,96},{8,128},{10,160},{12,192},{14,224},{16,... | collective-permute-start | bytes 393224 | tf_op jit(solution)/shard_map/ppermute | solution.py:38
  20.6 70.2 %all-to-all-start = ((bf16[16,32,16,128]{3,2,1,0:T(8,128)(2,1)}), bf16[16,32,16,128]{3,2,1,0:T(8,128)(2,1)S(1)}, u32[]{:S(2)}, u32[]{:S(2)}) async-start(bf16[16,32,16,128]{3,2,1,0:T(8,128)(2,1)} %broadcast_in_dim.4), calls=%async_computation | async-start | bytes 4194304 | tf_op jit(solution)/shard_map/all_to_all | solution.py:43
  41.8 165.4 %all-gather.5.cloned.1.call-start = ((), (), s32[]{:S(2)}) async-start(), calls=%async_computation.3 | async-start | bytes 4456448 | tf_op jit(solution)/shard_map/all_gather | solution.py:78
  97.3 9.7 %copy-start.1 = (bf16[32,16,128]{2,1,0:T(8,128)(2,1)S(1)}, bf16[32,16,128]{2,1,0:T(8,128)(2,1)}, u32[]{:S(2)}) copy-start(bf16[32,16,128]{2,1,0:T(8,128)(2,1)} %param.5) | copy-start | bytes 393220
  97.3 9.7 %copy-start.5 = (f32[32,16]{1,0:T(8,128)S(1)}, f32[32,16]{1,0:T(8,128)}, u32[]{:S(2)}) copy-start(f32[32,16]{1,0:T(8,128)} %copy-done.4) | copy-start | bytes 6148
  97.3 9.7 %copy-start.7 = (bf16[2,128,128]{2,1,0:T(8,128)(2,1)S(1)}, bf16[2,128,128]{2,1,0:T(8,128)(2,1)}, u32[]{:S(2)}) copy-start(bf16[2,128,128]{2,1,0:T(8,128)(2,1)} %param.8) | copy-start | bytes 196612
  102.8 14.6 %collective-permute-start.1 = (bf16[32,16,128]{0,1,2:T(8,128)(2,1)S(1)}, bf16[32,16,128]{0,1,2:T(8,128)(2,1)S(1)}, u32[]{:S(2)}, u32[]{:S(2)}) collective-permute-start(bf16[32,16,128]{0,1,2:T(8,128)(2,1)S(1)} %fusion.11), channel_id=1, source_target_pairs={{0,1},{1,0},{2,3},{3,2},{4,5},{5,4},{6,7},{7,6},{8,9},{9,8},{10,11... | collective-permute-start | bytes 393224 | tf_op jit(solution)/shard_map/ppermute | solution.py:53
  118.3 3.1 %copy-start.3 = (f32[32,16]{1,0:T(8,128)S(1)}, f32[32,16]{1,0:T(8,128)}, u32[]{:S(2)}) copy-start(f32[32,16]{1,0:T(8,128)} %copy-done.2) | copy-start | bytes 6148
  121.6 8.4 %collective-permute-start.2 = (bf16[32,16,128]{2,1,0:T(8,128)(2,1)S(1)}, bf16[32,16,128]{2,1,0:T(8,128)(2,1)S(1)}, u32[]{:S(2)}, u32[]{:S(2)}) collective-permute-start(bf16[32,16,128]{2,1,0:T(8,128)(2,1)S(1)} %get-tuple-element.7), channel_id=1, source_target_pairs={{0,0},{2,32},{4,64},{6,96},{8,128},{10,160},{12,192},{14,224},{16,... | collective-permute-start | bytes 393224 | tf_op jit(solution)/shard_map/ppermute | solution.py:38
  130.0 7.2 %collective-permute-start.3 = (bf16[32,16,128]{2,1,0:T(8,128)(2,1)S(1)}, bf16[32,16,128]{2,1,0:T(8,128)(2,1)S(1)}, u32[]{:S(2)}, u32[]{:S(2)}) collective-permute-start(bf16[32,16,128]{2,1,0:T(8,128)(2,1)S(1)} %collective-permute-done.2), channel_id=1, source_target_pairs={{0,1},{1,0},{2,3},{3,2},{4,5},{5,4},{6,7},{7,6},{8,9},{9,8},{10,11... | collective-permute-start | bytes 393224 | tf_op jit(solution)/shard_map/ppermute | solution.py:59
  139.8 17.5 %copy-start.8 = (bf16[2,128,128]{2,1,0:T(8,128)(2,1)S(1)}, bf16[2,128,128]{2,1,0:T(8,128)(2,1)}, u32[]{:S(2)}) copy-start(bf16[2,128,128]{2,1,0:T(8,128)(2,1)} %param.8) | copy-start | bytes 196612
  139.8 65.1 %all-to-all-start.1 = ((bf16[16,32,16,128]{3,2,1,0:T(8,128)(2,1)}), bf16[16,32,16,128]{3,2,1,0:T(8,128)(2,1)S(1)}, u32[]{:S(2)}, u32[]{:S(2)}) async-start(bf16[16,32,16,128]{3,2,1,0:T(8,128)(2,1)} %broadcast_in_dim.5), calls=%async_computation.1 | async-start | bytes 4194304 | tf_op jit(solution)/shard_map/all_to_all | solution.py:43
  207.2 3.5 %copy-start = (f32[512,16,128]{2,1,0:T(8,128)S(1)}, f32[512,16,128]{2,1,0:T(8,128)}, u32[]{:S(2)}) copy-start(f32[512,16,128]{2,1,0:T(8,128)} %convert.1) | copy-start | bytes 12582916
  210.8 12.3 %copy-start.6 = (bf16[2,128,128]{2,1,0:T(8,128)(2,1)S(1)}, bf16[2,128,128]{2,1,0:T(8,128)(2,1)}, u32[]{:S(2)}) copy-start(bf16[2,128,128]{2,1,0:T(8,128)(2,1)} %param.9) | copy-start | bytes 196612
Sparse Core Ops, SparseCore 0:
  16.4 50.9 all-gather.2
  138.2 59.7 all-gather.4

commit v7 on v6

--- a/solution.py
+++ b/solution.py
@@ -65,10 +65,11 @@
 def on_device(n, pair, pair_mask, w_in, w_gate, w_out):
     valid = pair_mask.astype(jnp.float32)[..., None]
     left, right, gate = prepare(pair, valid, w_in[0], w_gate[0])
-    left_rows = lax.all_gather(left, "col", axis=1, tiled=True)
-    right_diag = gather_a2a(transpose_tiles(right, n), "row", n, 1)
-    partial_value = jnp.einsum(
-        "ikc,jkc->ijc", left_rows, right_diag, preferred_element_type=jnp.float32
+    left_rows = lax.all_gather(jnp.swapaxes(left, 0, 1), "col", axis=0, tiled=True)
+    right_diag = gather_a2a(jnp.swapaxes(transpose_tiles(right, n), 0, 1), "row", n, 0)
+    partial_value = jnp.sum(
+        left_rows[:, :, None].astype(jnp.float32) * right_diag[:, None].astype(jnp.float32),
+        axis=0,
     )
     tri = sum_over_ka(partial_value)
     middle = finish(pair, tri, gate, w_out[0])

time: 233 us -> 223 us (0.957)
  local copies, waits for them, and re-layouts: 26.3 us -> 9.84 us
  other arithmetic: 23.6 us -> 35.5 us
  matrix products: 10.5 us -> 3.73 us
    all_gather x1 -> x0, local copies, waits for them, and re-layouts: 15.3 us -> none  [on_device(): left_rows = lax.all_gather(left, 'col', axis=1, tiled=True)]
    reduce_sum x0 -> x1, other arithmetic: none -> 11.3 us  [on_device(): jnp.sum(left_rows[:, :, None].astype(jnp.float32) * right_diag[:, None].a...]
    all_to_all x2, waiting for transfers between devices: 55.5 us -> 66.1 us  [gather_a2a(): got = lax.all_to_all(copies, axis_name, 0, 0, tiled=False)]
    ppermute x1, waiting for transfers between devices: 9.99 us -> 2 us  [sum_over_ka(): got = lax.ppermute(theirs.astype(jnp.bfloat16), 'ka', [(0, 1), (1, 0)])]
    dot_general x1 -> x0, matrix products: 5.27 us -> none  [on_device(): jnp.einsum('ikc,jkc->ijc', left_rows, right_diag, preferred_element_type=...]
    reshape x1 -> x0, local copies, waits for them, and re-layouts: 4.61 us -> none  [gather_a2a(): got.reshape(value.shape[:axis] + (n * value.shape[axis],) + value.shape[a...]
    convert_element_type x1, local copies, waits for them, and re-layouts: 0.5 us -> 4.73 us  [on_device(): left_rows[:, :, None].astype(jnp.float32)]
  transfers between devices with their start and end apart: 8 -> 8, of which waited for: 7 -> 7; matrix products, arithmetic and copies ran while one was open for 9% -> 5% of each run, Pallas kernels for 0% -> 0%
where the time goes in v7:
time: 223 us; the launch traced here: 222 us
  waiting for transfers between devices  102 us (46%)
  starting transfers between devices  57.4 us (26%)
  other arithmetic  35.5 us (16%)
  between operations  13.7 us (6%)
  local copies, waits for them, and re-layouts  9.84 us (4%)
  matrix products  3.73 us (2%)
    all_to_all x2, waiting for transfers between devices, gather_a2a(): got = lax.all_to_all(copies, axis_name, 0, 0, tiled=False)  66.1 us
    all_to_all x2, starting transfers between devices, gather_a2a(): got = lax.all_to_all(copies, axis_name, 0, 0, tiled=False)  37.7 us
    all_gather x1, waiting for transfers between devices, on_device(): lax.all_gather(jnp.swapaxes(left, 0, 1), 'col', axis=0, tiled=True)  25.4 us
    reduce_sum x3, other arithmetic, layer_norm(): mean = jnp.mean(value, axis=-1, keepdims=True)  13.1 us
    reduce_sum x1, other arithmetic, on_device(): jnp.sum(left_rows[:, :, None].astype(jnp.float32) * right_diag[:, None].a...  11.3 us
    ppermute x2, starting transfers between devices, transpose_tiles(): return lax.ppermute(value, ('row', 'col'), perm)  10.7 us
    ppermute x2, waiting for transfers between devices, transpose_tiles(): return lax.ppermute(value, ('row', 'col'), perm)  5.43 us
    ppermute x1, starting transfers between devices, sum_over_ka(): got = lax.ppermute(theirs.astype(jnp.bfloat16), 'ka', [(0, 1), (1, 0)])  4.98 us
  transfers between devices with their start and end apart: 8, of which 7 were waited for; matrix products, arithmetic and copies ran while one was open for 5% of the time, Pallas kernels for 0%

profile of v7, /device:TPU:1, one launch (start us, length us, event | category | flops | bytes accessed | tf_op | source)
XLA Modules:
  0.0 222.3 jit_solution(10849930910078287763)
XLA Ops:
  6.5 1.0 convert_reduce_fusion
  7.6 1.1 fusion.13
  9.5 1.3 fusion.37
  11.7 4.5 %collective-permute-start = (bf16[32,16,128]{2,1,0:T(8,128)(2,1)S(1)}, bf16[32,16,128]{2,1,0:T(8,128)(2,1)S(1)}, u32[]{:S(2)}, u32[]{:S(2)}) collective-permute-start(bf16[32,16,128]{2,1,0:T(8,128)(2,1)S(1)} %get-tuple-element.10), channel_id=1, source_target_pairs={{0,0},{2,32},{4,64},{6,96},{8,128},{10,160},{12,192},{14,224},{16,... | collective-permute-start | bytes 393224 | tf_op jit(solution)/shard_map/ppermute | solution.py:38
  16.2 2.6 %collective-permute-done = bf16[32,16,128]{2,1,0:T(8,128)(2,1)S(1)} collective-permute-done((bf16[32,16,128]{2,1,0:T(8,128)(2,1)S(1)}, bf16[32,16,128]{2,1,0:T(8,128)(2,1)S(1)}, u32[]{:S(2)}, u32[]{:S(2)}) %collective-permute-start) | collective-permute-done | bytes 131104 | tf_op jit(solution)/shard_map/ppermute | solution.py:38
  18.9 1.8 broadcast_in_dim.4
  20.6 21.2 %all-to-all-start = ((bf16[16,16,32,128]{3,2,1,0:T(8,128)(2,1)}), bf16[16,16,32,128]{3,2,1,0:T(8,128)(2,1)S(1)}, u32[]{:S(2)}, u32[]{:S(2)}) async-start(bf16[16,16,32,128]{3,2,1,0:T(8,128)(2,1)} %broadcast_in_dim.4), calls=%async_computation | async-start | bytes 4194304 | tf_op jit(solution)/shard_map/all_to_all | solution.py:43
  41.9 25.4 %all-gather.3.cloned.1.call-done = bf16[256,32,128]{2,0,1:T(8,128)(2,1)} async-done(((bf16[16,32,128]{2,0,1:T(8,128)(2,1)}), bf16[256,32,128]{2,0,1:T(8,128)(2,1)}) %all-gather.3.cloned.1.call-update) | async-done | bytes 2097168 | tf_op jit(solution)/shard_map/all_gather | solution.py:68
  67.3 4.7 %copy.13 = f32[256,32,128]{2,1,0:T(8,128)} copy(bf16[256,32,128]{2,0,1:T(8,128)(2,1)} %all-gather.3.cloned.1.call-done) | data formatting | bytes 6291456 | tf_op jit(solution)/shard_map/convert_element_type | solution.py:71
  72.0 18.3 %all-to-all-done = bf16[16,16,32,128]{3,2,1,0:T(8,128)(2,1)S(1)} async-done(((bf16[16,16,32,128]{3,2,1,0:T(8,128)(2,1)}), bf16[16,16,32,128]{3,2,1,0:T(8,128)(2,1)S(1)}, u32[]{:S(2)}, u32[]{:S(2)}) %all-to-all-start) | async-done | bytes 2097184 | tf_op jit(solution)/shard_map/all_to_all | solution.py:43
  91.0 1.5 copy-done.1
  92.5 11.3 %multiply_reduce_fusion.2 = f32[32,32,128]{2,1,0:T(8,128)S(1)} fusion(f32[256,32,128]{2,1,0:T(8,128)S(1)} %bitcast_convert_fusion, f32[256,32,128]{2,1,0:T(8,128)S(1)} %copy-done.1), kind=kLoop, calls=%fused_computation.2 | loop fusion | flops 66977792 | bytes 8912896 | tf_op jit(solution)/shard_map/reduce_sum | solution.py:70
  103.9 5.0 %collective-permute-start.1 = (bf16[32,16,128]{2,1,0:T(8,128)(2,1)S(1)}, bf16[32,16,128]{2,1,0:T(8,128)(2,1)S(1)}, u32[]{:S(2)}, u32[]{:S(2)}) collective-permute-start(bf16[32,16,128]{2,1,0:T(8,128)(2,1)S(1)} %dynamic-slice_convert_fusion), channel_id=1, source_target_pairs={{0,1},{1,0},{2,3},{3,2},{4,5},{5,4},{6,7},{7,6},{8,9},{9,8},{10,11... | collective-permute-start | bytes 393224 | tf_op jit(solution)/shard_map/ppermute | solution.py:53
  109.2 2.0 collective-permute-done.1
  112.9 6.2 %collective-permute-start.2 = (bf16[32,16,128]{2,1,0:T(8,128)(2,1)S(1)}, bf16[32,16,128]{2,1,0:T(8,128)(2,1)S(1)}, u32[]{:S(2)}, u32[]{:S(2)}) collective-permute-start(bf16[32,16,128]{2,1,0:T(8,128)(2,1)S(1)} %get-tuple-element.7), channel_id=1, source_target_pairs={{0,0},{2,32},{4,64},{6,96},{8,128},{10,160},{12,192},{14,224},{16,... | collective-permute-start | bytes 393224 | tf_op jit(solution)/shard_map/ppermute | solution.py:38
  119.1 2.8 %collective-permute-done.2 = bf16[32,16,128]{2,1,0:T(8,128)(2,1)S(1)} collective-permute-done((bf16[32,16,128]{2,1,0:T(8,128)(2,1)S(1)}, bf16[32,16,128]{2,1,0:T(8,128)(2,1)S(1)}, u32[]{:S(2)}, u32[]{:S(2)}) %collective-permute-start.2) | collective-permute-done | bytes 131104 | tf_op jit(solution)/shard_map/ppermute | solution.py:38
  122.0 4.0 %collective-permute-start.3 = (bf16[32,16,128]{2,1,0:T(8,128)(2,1)S(1)}, bf16[32,16,128]{2,1,0:T(8,128)(2,1)S(1)}, u32[]{:S(2)}, u32[]{:S(2)}) collective-permute-start(bf16[32,16,128]{2,1,0:T(8,128)(2,1)S(1)} %collective-permute-done.2), channel_id=1, source_target_pairs={{0,1},{1,0},{2,3},{3,2},{4,5},{5,4},{6,7},{7,6},{8,9},{9,8},{10,11... | collective-permute-start | bytes 393224 | tf_op jit(solution)/shard_map/ppermute | solution.py:59
  126.0 3.2 %collective-permute-done.3 = bf16[32,16,128]{2,1,0:T(8,128)(2,1)S(1)} collective-permute-done((bf16[32,16,128]{2,1,0:T(8,128)(2,1)S(1)}, bf16[32,16,128]{2,1,0:T(8,128)(2,1)S(1)}, u32[]{:S(2)}, u32[]{:S(2)}) %collective-permute-start.3) | collective-permute-done | bytes 131104 | tf_op jit(solution)/shard_map/ppermute | solution.py:59
  130.0 1.7 broadcast_in_dim.5
  131.8 16.4 %all-to-all-start.1 = ((bf16[16,32,16,128]{3,2,1,0:T(8,128)(2,1)}), bf16[16,32,16,128]{3,2,1,0:T(8,128)(2,1)S(1)}, u32[]{:S(2)}, u32[]{:S(2)}) async-start(bf16[16,32,16,128]{3,2,1,0:T(8,128)(2,1)} %broadcast_in_dim.5), calls=%async_computation.1 | async-start | bytes 4194304 | tf_op jit(solution)/shard_map/all_to_all | solution.py:43
  148.5 47.9 %all-to-all-done.1 = bf16[16,32,16,128]{3,2,1,0:T(8,128)(2,1)S(1)} async-done(((bf16[16,32,16,128]{3,2,1,0:T(8,128)(2,1)}), bf16[16,32,16,128]{3,2,1,0:T(8,128)(2,1)S(1)}, u32[]{:S(2)}, u32[]{:S(2)}) %all-to-all-start.1) | async-done | bytes 2097184 | tf_op jit(solution)/shard_map/all_to_all | solution.py:43
  196.4 2.3 %convert.3 = f32[512,16,128]{2,1,0:T(8,128)} convert(bf16[512,16,128]{2,1,0:T(8,128)(2,1)S(1)} %bitcast.34) | non-fusion elementwise | flops 1048576 | bytes 6291456 | tf_op jit(solution)/shard_map/convert_element_type | solution.py:81
  198.7 3.5 %convert_element_type.92 = f32[512,32,128]{2,1,0:T(8,128)S(1)} convert(bf16[512,32,128]{2,1,0:T(8,128)(2,1)} %all-gather.5.cloned.1.call-done) | non-fusion elementwise | flops 2097152 | bytes 12582912 | tf_op jit(solution)/shard_map/convert_element_type | solution.py:81
  202.2 12.0 %multiply_reduce_fusion = (f32[32,16]{1,0:T(8,128)S(1)}, f32[32,16,128]{2,1,0:T(8,128)S(1)}) fusion(f32[512,16,128]{2,1,0:T(8,128)S(1)} %copy-done, f32[512,32,128]{2,1,0:T(8,128)S(1)} %convert_element_type.92), kind=kLoop, calls=%fused_computation | loop fusion | flops 100597248 | bytes 12847104 | tf_op jit(solution)/shard_map/reduce_sum | solution.py:8
  (41 shorter events, 6.8 us)
Async XLA Ops:
  6.5 60.8 %all-gather.3.cloned.1.call-start = ((), (), s32[]{:S(2)}) async-start(), calls=%async_computation.2 | async-start | bytes 2228224 | tf_op jit(solution)/shard_map/all_gather | solution.py:68
  11.7 7.1 %collective-permute-start = (bf16[32,16,128]{2,1,0:T(8,128)(2,1)S(1)}, bf16[32,16,128]{2,1,0:T(8,128)(2,1)S(1)}, u32[]{:S(2)}, u32[]{:S(2)}) collective-permute-start(bf16[32,16,128]{2,1,0:T(8,128)(2,1)S(1)} %get-tuple-element.10), channel_id=1, source_target_pairs={{0,0},{2,32},{4,64},{6,96},{8,128},{10,160},{12,192},{14,224},{16,... | collective-permute-start | bytes 393224 | tf_op jit(solution)/shard_map/ppermute | solution.py:38
  20.6 69.7 %all-to-all-start = ((bf16[16,16,32,128]{3,2,1,0:T(8,128)(2,1)}), bf16[16,16,32,128]{3,2,1,0:T(8,128)(2,1)S(1)}, u32[]{:S(2)}, u32[]{:S(2)}) async-start(bf16[16,16,32,128]{3,2,1,0:T(8,128)(2,1)} %broadcast_in_dim.4), calls=%async_computation | async-start | bytes 4194304 | tf_op jit(solution)/shard_map/all_to_all | solution.py:43
  41.9 156.9 %all-gather.5.cloned.1.call-start = ((), (), s32[]{:S(2)}) async-start(), calls=%async_computation.3 | async-start | bytes 4456448 | tf_op jit(solution)/shard_map/all_gather | solution.py:79
  90.3 2.2 copy-start.1
  92.5 16.4 %copy-start.2 = (bf16[32,16,128]{2,1,0:T(8,128)(2,1)S(1)}, bf16[32,16,128]{2,1,0:T(8,128)(2,1)}, u32[]{:S(2)}) copy-start(bf16[32,16,128]{2,1,0:T(8,128)(2,1)} %param.5) | copy-start | bytes 393220
  92.5 16.4 %copy-start.4 = (bf16[2,128,128]{2,1,0:T(8,128)(2,1)S(1)}, bf16[2,128,128]{2,1,0:T(8,128)(2,1)}, u32[]{:S(2)}) copy-start(bf16[2,128,128]{2,1,0:T(8,128)(2,1)} %param.8) | copy-start | bytes 196612
  92.5 19.2 %copy-start.5 = (bf16[2,128,128]{2,1,0:T(8,128)(2,1)S(1)}, bf16[2,128,128]{2,1,0:T(8,128)(2,1)}, u32[]{:S(2)}) copy-start(bf16[2,128,128]{2,1,0:T(8,128)(2,1)} %param.9) | copy-start | bytes 196612
  103.8 8.5 %copy-start.3 = (bf16[2,128,512]{2,1,0:T(8,128)(2,1)S(1)}, bf16[2,128,512]{2,1,0:T(8,128)(2,1)}, u32[]{:S(2)}) copy-start(bf16[2,128,512]{2,1,0:T(8,128)(2,1)} %param.7) | copy-start | bytes 786436
  103.9 7.3 %collective-permute-start.1 = (bf16[32,16,128]{2,1,0:T(8,128)(2,1)S(1)}, bf16[32,16,128]{2,1,0:T(8,128)(2,1)S(1)}, u32[]{:S(2)}, u32[]{:S(2)}) collective-permute-start(bf16[32,16,128]{2,1,0:T(8,128)(2,1)S(1)} %dynamic-slice_convert_fusion), channel_id=1, source_target_pairs={{0,1},{1,0},{2,3},{3,2},{4,5},{5,4},{6,7},{7,6},{8,9},{9,8},{10,11... | collective-permute-start | bytes 393224 | tf_op jit(solution)/shard_map/ppermute | solution.py:53
  112.9 9.0 %collective-permute-start.2 = (bf16[32,16,128]{2,1,0:T(8,128)(2,1)S(1)}, bf16[32,16,128]{2,1,0:T(8,128)(2,1)S(1)}, u32[]{:S(2)}, u32[]{:S(2)}) collective-permute-start(bf16[32,16,128]{2,1,0:T(8,128)(2,1)S(1)} %get-tuple-element.7), channel_id=1, source_target_pairs={{0,0},{2,32},{4,64},{6,96},{8,128},{10,160},{12,192},{14,224},{16,... | collective-permute-start | bytes 393224 | tf_op jit(solution)/shard_map/ppermute | solution.py:38
  122.0 7.2 %collective-permute-start.3 = (bf16[32,16,128]{2,1,0:T(8,128)(2,1)S(1)}, bf16[32,16,128]{2,1,0:T(8,128)(2,1)S(1)}, u32[]{:S(2)}, u32[]{:S(2)}) collective-permute-start(bf16[32,16,128]{2,1,0:T(8,128)(2,1)S(1)} %collective-permute-done.2), channel_id=1, source_target_pairs={{0,1},{1,0},{2,3},{3,2},{4,5},{5,4},{6,7},{7,6},{8,9},{9,8},{10,11... | collective-permute-start | bytes 393224 | tf_op jit(solution)/shard_map/ppermute | solution.py:59
  131.8 64.7 %all-to-all-start.1 = ((bf16[16,32,16,128]{3,2,1,0:T(8,128)(2,1)}), bf16[16,32,16,128]{3,2,1,0:T(8,128)(2,1)S(1)}, u32[]{:S(2)}, u32[]{:S(2)}) async-start(bf16[16,32,16,128]{3,2,1,0:T(8,128)(2,1)} %broadcast_in_dim.5), calls=%async_computation.1 | async-start | bytes 4194304 | tf_op jit(solution)/shard_map/all_to_all | solution.py:43
  198.7 3.5 %copy-start = (f32[512,16,128]{2,1,0:T(8,128)S(1)}, f32[512,16,128]{2,1,0:T(8,128)}, u32[]{:S(2)}) copy-start(f32[512,16,128]{2,1,0:T(8,128)} %convert.3) | copy-start | bytes 12582916
Sparse Core Ops, SparseCore 0:
  16.3 50.9 all-gather.2
  130.1 58.6 all-gather.4

commit v8 on v7

--- a/solution.py
+++ b/solution.py
@@ -62,11 +62,31 @@
     )
 
 
+def gather_over_row(value, n):
+    ny = n // 2
+    me = lax.axis_index("row")
+    swapped = lax.ppermute(value, "row", [(r, r ^ 1) for r in range(n)])
+    pair = jnp.where(me % 2 == 0, jnp.stack([value, swapped]), jnp.stack([swapped, value]))
+    fwd = [(r, ((r // 2 + 1) % ny) * 2 + r % 2) for r in range(n)]
+    bwd = [(r, ((r // 2 - 1) % ny) * 2 + r % 2) for r in range(n)]
+    plus, minus, got_plus, got_minus = pair, pair, [], []
+    for step in range(1, ny // 2 + 1):
+        plus = lax.ppermute(plus, "row", fwd)
+        got_plus.append(plus)
+        if step < ny - ny // 2:
+            minus = lax.ppermute(minus, "row", bwd)
+            got_minus.append(minus)
+    stacked = jnp.stack([pair] + got_plus + got_minus[::-1])
+    order = (me // 2 - jnp.arange(ny)) % ny
+    blocks = jnp.take(stacked, order, axis=0)
+    return blocks.reshape((n * value.shape[0],) + value.shape[1:])
+
+
 def on_device(n, pair, pair_mask, w_in, w_gate, w_out):
     valid = pair_mask.astype(jnp.float32)[..., None]
     left, right, gate = prepare(pair, valid, w_in[0], w_gate[0])
     left_rows = lax.all_gather(jnp.swapaxes(left, 0, 1), "col", axis=0, tiled=True)
-    right_diag = gather_a2a(jnp.swapaxes(transpose_tiles(right, n), 0, 1), "row", n, 0)
+    right_diag = gather_over_row(jnp.swapaxes(transpose_tiles(right, n), 0, 1), n)
     partial_value = jnp.sum(
         left_rows[:, :, None].astype(jnp.float32) * right_diag[:, None].astype(jnp.float32),
         axis=0,
@@ -74,7 +94,7 @@
     tri = sum_over_ka(partial_value)
     middle = finish(pair, tri, gate, w_out[0])
     left, right, gate = prepare(middle, valid, w_in[1], w_gate[1])
-    right_cols = gather_a2a(right, "row", n, 0)
+    right_cols = gather_over_row(right, n)
     left_tile = join_over_ka(transpose_tiles(left, n))
     left_diag = lax.all_gather(left_tile, "col", axis=0, tiled=True)
     tri = jnp.sum(

time: 223 us -> 231 us (1.036)
  the two profiles are of different devices: /device:TPU:1 before, /device:TPU:58 now
where the time goes in v8:
time: 231 us
  waiting for transfers between devices  85.5 us (37%)
  starting transfers between devices  67.6 us (29%)
  other arithmetic  40.7 us (18%)
  local copies, waits for them, and re-layouts  19.2 us (8%)
  between operations  13.9 us (6%)
  matrix products  3.72 us (2%)
    ppermute x2, waiting for transfers between devices, transpose_tiles(): return lax.ppermute(value, ('row', 'col'), perm)  29.9 us
    ppermute x8, waiting for transfers between devices, gather_over_row(): plus = lax.ppermute(plus, 'row', fwd)  27.3 us
    ppermute x8, starting transfers between devices, gather_over_row(): plus = lax.ppermute(plus, 'row', fwd)  26.2 us
    ppermute x6, starting transfers between devices, gather_over_row(): minus = lax.ppermute(minus, 'row', bwd)  15.6 us
    reduce_sum x3, other arithmetic, layer_norm(): mean = jnp.mean(value, axis=-1, keepdims=True)  13.1 us
    ppermute x6, waiting for transfers between devices, gather_over_row(): minus = lax.ppermute(minus, 'row', bwd)  11.6 us
    ppermute x2, starting transfers between devices, transpose_tiles(): return lax.ppermute(value, ('row', 'col'), perm)  11.5 us
    reduce_sum x1, other arithmetic, on_device(): jnp.sum(left_rows[:, :, None].astype(jnp.float32) * right_diag[:, None].a...  11.3 us
  transfers between devices with their start and end apart: 22, of which 17 were waited for; matrix products, arithmetic and copies ran while one was open for 11% of the time, Pallas kernels for 0%

profile of v8, /device:TPU:58, one launch (start us, length us, event | category | flops | bytes accessed | tf_op | source)
XLA Modules:
  0.0 230.6 jit_solution(15517181329925368052)
XLA Ops:
  11.8 9.6 %collective-permute-start = (bf16[32,16,128]{2,1,0:T(8,128)(2,1)S(1)}, bf16[32,16,128]{2,1,0:T(8,128)(2,1)S(1)}, u32[]{:S(2)}, u32[]{:S(2)}) collective-permute-start(bf16[32,16,128]{2,1,0:T(8,128)(2,1)S(1)} %get-tuple-element.10), channel_id=1, source_target_pairs={{0,0},{2,32},{4,64},{6,96},{8,128},{10,160},{12,192},{14,224},{16,... | collective-permute-start | bytes 393224 | tf_op jit(solution)/shard_map/ppermute | solution.py:38
  21.3 11.8 %collective-permute-done = bf16[32,16,128]{2,1,0:T(8,128)(2,1)S(1)} collective-permute-done((bf16[32,16,128]{2,1,0:T(8,128)(2,1)S(1)}, bf16[32,16,128]{2,1,0:T(8,128)(2,1)S(1)}, u32[]{:S(2)}, u32[]{:S(2)}) %collective-permute-start) | collective-permute-done | bytes 131104 | tf_op jit(solution)/shard_map/ppermute | solution.py:38
  33.1 3.2 %collective-permute-start.1 = (bf16[16,32,128]{2,0,1:T(8,128)(2,1)S(1)}, bf16[16,32,128]{2,0,1:T(8,128)(2,1)S(1)}, u32[]{:S(2)}, u32[]{:S(2)}) collective-permute-start(bf16[16,32,128]{2,0,1:T(8,128)(2,1)S(1)} %bitcast.77), channel_id=1, source_target_pairs={{0,32},{32,0},{64,96},{96,64},{128,160},{160,128},{192,224},{224,1... | collective-permute-start | bytes 393224 | tf_op jit(solution)/shard_map/ppermute | solution.py:68
  36.4 4.3 %collective-permute-done.1 = bf16[16,32,128]{2,0,1:T(8,128)(2,1)S(1)} collective-permute-done((bf16[16,32,128]{2,0,1:T(8,128)(2,1)S(1)}, bf16[16,32,128]{2,0,1:T(8,128)(2,1)S(1)}, u32[]{:S(2)}, u32[]{:S(2)}) %collective-permute-start.1) | collective-permute-done | bytes 131104 | tf_op jit(solution)/shard_map/ppermute | solution.py:68
  42.6 7.6 %collective-permute-done.2 = bf16[2,16,32,128]{3,1,2,0:T(8,128)(2,1)S(1)} collective-permute-done((bf16[2,16,32,128]{3,1,2,0:T(8,128)(2,1)S(1)}, bf16[2,16,32,128]{3,1,2,0:T(8,128)(2,1)S(1)}, u32[]{:S(2)}, u32[]{:S(2)}) %collective-permute-start.2) | collective-permute-done | bytes 262176 | tf_op jit(solution)/shard_map/ppermute | solution.py:74
  50.2 3.4 %collective-permute-start.3 = (bf16[2,16,32,128]{3,1,2,0:T(8,128)(2,1)S(1)}, bf16[2,16,32,128]{3,1,2,0:T(8,128)(2,1)S(1)}, u32[]{:S(2)}, u32[]{:S(2)}) collective-permute-start(bf16[2,16,32,128]{3,1,2,0:T(8,128)(2,1)S(1)} %collective-permute-done.2), channel_id=1, source_target_pairs={{0,64},{32,96},{64,128},{96,160},{128,192},{160,224},{192,256},{22... | collective-permute-start | bytes 786440 | tf_op jit(solution)/shard_map/ppermute | solution.py:74
  58.8 4.9 %collective-permute-start.4 = (bf16[2,16,32,128]{3,1,2,0:T(8,128)(2,1)S(1)}, bf16[2,16,32,128]{3,1,2,0:T(8,128)(2,1)S(1)}, u32[]{:S(2)}, u32[]{:S(2)}) collective-permute-start(bf16[2,16,32,128]{3,1,2,0:T(8,128)(2,1)S(1)} %collective-permute-done.3), channel_id=1, source_target_pairs={{0,64},{32,96},{64,128},{96,160},{128,192},{160,224},{192,256},{22... | collective-permute-start | bytes 786440 | tf_op jit(solution)/shard_map/ppermute | solution.py:74
  67.6 5.6 %collective-permute-start.5 = (bf16[2,16,32,128]{3,1,2,0:T(8,128)(2,1)S(1)}, bf16[2,16,32,128]{3,1,2,0:T(8,128)(2,1)S(1)}, u32[]{:S(2)}, u32[]{:S(2)}) collective-permute-start(bf16[2,16,32,128]{3,1,2,0:T(8,128)(2,1)S(1)} %collective-permute-done.4), channel_id=1, source_target_pairs={{0,64},{32,96},{64,128},{96,160},{128,192},{160,224},{192,256},{22... | collective-permute-start | bytes 786440 | tf_op jit(solution)/shard_map/ppermute | solution.py:74
  77.8 5.6 %collective-permute-done.8 = bf16[2,16,32,128]{3,1,2,0:T(8,128)(2,1)S(1)} collective-permute-done((bf16[2,16,32,128]{3,1,2,0:T(8,128)(2,1)S(1)}, bf16[2,16,32,128]{3,1,2,0:T(8,128)(2,1)S(1)}, u32[]{:S(2)}, u32[]{:S(2)}) %collective-permute-start.8) | collective-permute-done | bytes 262176 | tf_op jit(solution)/shard_map/ppermute | solution.py:77
  94.2 11.3 %multiply_reduce_fusion.2 = f32[32,32,128]{2,1,0:T(8,128)S(1)} fusion(f32[256,32,128]{2,1,0:T(8,128)S(1)} %copy-done.1, f32[256,32,128]{2,1,0:T(8,128)S(1)} %copy.15), kind=kLoop, calls=%fused_computation.4 | loop fusion | flops 66977792 | bytes 8912896 | tf_op jit(solution)/shard_map/reduce_sum | solution.py:90
  105.6 4.3 %collective-permute-start.9 = (bf16[32,16,128]{2,1,0:T(8,128)(2,1)S(1)}, bf16[32,16,128]{2,1,0:T(8,128)(2,1)S(1)}, u32[]{:S(2)}, u32[]{:S(2)}) collective-permute-start(bf16[32,16,128]{2,1,0:T(8,128)(2,1)S(1)} %dynamic-slice_convert_fusion), channel_id=1, source_target_pairs={{0,1},{1,0},{2,3},{3,2},{4,5},{5,4},{6,7},{7,6},{8,9},{9,8},{10,11... | collective-permute-start | bytes 393224 | tf_op jit(solution)/shard_map/ppermute | solution.py:53
  110.4 3.8 %collective-permute-done.9 = bf16[32,16,128]{2,1,0:T(8,128)(2,1)S(1)} collective-permute-done((bf16[32,16,128]{2,1,0:T(8,128)(2,1)S(1)}, bf16[32,16,128]{2,1,0:T(8,128)(2,1)S(1)}, u32[]{:S(2)}, u32[]{:S(2)}) %collective-permute-start.9) | collective-permute-done | bytes 131104 | tf_op jit(solution)/shard_map/ppermute | solution.py:53
  117.7 18.2 %collective-permute-done.10 = bf16[32,16,128]{2,1,0:T(8,128)(2,1)S(1)} collective-permute-done((bf16[32,16,128]{2,1,0:T(8,128)(2,1)S(1)}, bf16[32,16,128]{2,1,0:T(8,128)(2,1)S(1)}, u32[]{:S(2)}, u32[]{:S(2)}) %collective-permute-start.10) | collective-permute-done | bytes 131104 | tf_op jit(solution)/shard_map/ppermute | solution.py:38
  135.9 4.0 %collective-permute-start.11 = (bf16[32,16,128]{2,1,0:T(8,128)(2,1)S(1)}, bf16[32,16,128]{2,1,0:T(8,128)(2,1)S(1)}, u32[]{:S(2)}, u32[]{:S(2)}) collective-permute-start(bf16[32,16,128]{2,1,0:T(8,128)(2,1)S(1)} %collective-permute-done.10), channel_id=1, source_target_pairs={{0,1},{1,0},{2,3},{3,2},{4,5},{5,4},{6,7},{7,6},{8,9},{9,8},{10,11... | collective-permute-start | bytes 393224 | tf_op jit(solution)/shard_map/ppermute | solution.py:59
  139.9 4.4 %collective-permute-done.11 = bf16[32,16,128]{2,1,0:T(8,128)(2,1)S(1)} collective-permute-done((bf16[32,16,128]{2,1,0:T(8,128)(2,1)S(1)}, bf16[32,16,128]{2,1,0:T(8,128)(2,1)S(1)}, u32[]{:S(2)}, u32[]{:S(2)}) %collective-permute-start.11) | collective-permute-done | bytes 131104 | tf_op jit(solution)/shard_map/ppermute | solution.py:59
  147.9 4.1 %collective-permute-done.12 = bf16[32,16,128]{2,1,0:T(8,128)(2,1)S(1)} collective-permute-done((bf16[32,16,128]{2,1,0:T(8,128)(2,1)S(1)}, bf16[32,16,128]{2,1,0:T(8,128)(2,1)S(1)}, u32[]{:S(2)}, u32[]{:S(2)}) %collective-permute-start.12) | collective-permute-done | bytes 131104 | tf_op jit(solution)/shard_map/ppermute | solution.py:68
  153.9 8.6 %collective-permute-done.13 = bf16[2,32,16,128]{3,2,1,0:T(8,128)(2,1)S(1)} collective-permute-done((bf16[2,32,16,128]{3,2,1,0:T(8,128)(2,1)S(1)}, bf16[2,32,16,128]{3,2,1,0:T(8,128)(2,1)S(1)}, u32[]{:S(2)}, u32[]{:S(2)}) %collective-permute-start.13) | collective-permute-done | bytes 262176 | tf_op jit(solution)/shard_map/ppermute | solution.py:74
  164.6 3.9 %collective-permute-start.17 = (bf16[2,32,16,128]{3,2,1,0:T(8,128)(2,1)S(1)}, bf16[2,32,16,128]{3,2,1,0:T(8,128)(2,1)S(1)}, u32[]{:S(2)}, u32[]{:S(2)}) collective-permute-start(bf16[2,32,16,128]{3,2,1,0:T(8,128)(2,1)S(1)} %maximum_select_fusion.4), channel_id=1, source_target_pairs={{0,448},{32,480},{64,0},{96,32},{128,64},{160,96},{192,128},{224,1... | collective-permute-start | bytes 786440 | tf_op jit(solution)/shard_map/ppermute | solution.py:77
  168.9 4.5 %collective-permute-done.14 = bf16[2,32,16,128]{3,2,1,0:T(8,128)(2,1)S(1)} collective-permute-done((bf16[2,32,16,128]{3,2,1,0:T(8,128)(2,1)S(1)}, bf16[2,32,16,128]{3,2,1,0:T(8,128)(2,1)S(1)}, u32[]{:S(2)}, u32[]{:S(2)}) %collective-permute-start.14) | collective-permute-done | bytes 262176 | tf_op jit(solution)/shard_map/ppermute | solution.py:74
  176.5 3.5 %collective-permute-start.18 = (bf16[2,32,16,128]{3,2,1,0:T(8,128)(2,1)S(1)}, bf16[2,32,16,128]{3,2,1,0:T(8,128)(2,1)S(1)}, u32[]{:S(2)}, u32[]{:S(2)}) collective-permute-start(bf16[2,32,16,128]{3,2,1,0:T(8,128)(2,1)S(1)} %collective-permute-done.17), channel_id=1, source_target_pairs={{0,448},{32,480},{64,0},{96,32},{128,64},{160,96},{192,128},{224,1... | collective-permute-start | bytes 786440 | tf_op jit(solution)/shard_map/ppermute | solution.py:77
  183.5 4.3 %collective-permute-start.16 = (bf16[2,32,16,128]{3,2,1,0:T(8,128)(2,1)S(1)}, bf16[2,32,16,128]{3,2,1,0:T(8,128)(2,1)S(1)}, u32[]{:S(2)}, u32[]{:S(2)}) collective-permute-start(bf16[2,32,16,128]{3,2,1,0:T(8,128)(2,1)S(1)} %collective-permute-done.15), channel_id=1, source_target_pairs={{0,64},{32,96},{64,128},{96,160},{128,192},{160,224},{192,256},{22... | collective-permute-start | bytes 786440 | tf_op jit(solution)/shard_map/ppermute | solution.py:74
  192.5 5.7 %collective-permute-done.19 = bf16[2,32,16,128]{3,2,1,0:T(8,128)(2,1)S(1)} collective-permute-done((bf16[2,32,16,128]{3,2,1,0:T(8,128)(2,1)S(1)}, bf16[2,32,16,128]{3,2,1,0:T(8,128)(2,1)S(1)}, u32[]{:S(2)}, u32[]{:S(2)}) %collective-permute-start.19) | collective-permute-done | bytes 262176 | tf_op jit(solution)/shard_map/ppermute | solution.py:77
  207.0 3.5 %convert_element_type.85 = f32[512,32,128]{2,1,0:T(8,128)S(1)} convert(bf16[512,32,128]{2,1,0:T(8,128)(2,1)} %all-gather.5.cloned.1.call-done) | non-fusion elementwise | flops 2097152 | bytes 12582912 | tf_op jit(solution)/shard_map/convert_element_type | solution.py:101
  210.5 12.0 %multiply_reduce_fusion = (f32[32,16]{1,0:T(8,128)S(1)}, f32[32,16,128]{2,1,0:T(8,128)S(1)}) fusion(f32[512,16,128]{2,1,0:T(8,128)S(1)} %copy-done, f32[512,32,128]{2,1,0:T(8,128)S(1)} %convert_element_type.85), kind=kLoop, calls=%fused_computation.2 | loop fusion | flops 100597248 | bytes 12847104 | tf_op jit(solution)/shard_map/reduce_sum | solution.py:8
  (95 shorter events, 64.7 us)
Async XLA Ops:
  6.5 84.7 %all-gather.3.cloned.1.call-start = ((), (), s32[]{:S(2)}) async-start(), calls=%async_computation | async-start | bytes 2228224 | tf_op jit(solution)/shard_map/all_gather | solution.py:88
  11.7 195.2 %all-gather.5.cloned.1.call-start = ((), (), s32[]{:S(2)}) async-start(), calls=%async_computation.1 | async-start | bytes 4456448 | tf_op jit(solution)/shard_map/all_gather | solution.py:99
  11.8 21.4 %collective-permute-start = (bf16[32,16,128]{2,1,0:T(8,128)(2,1)S(1)}, bf16[32,16,128]{2,1,0:T(8,128)(2,1)S(1)}, u32[]{:S(2)}, u32[]{:S(2)}) collective-permute-start(bf16[32,16,128]{2,1,0:T(8,128)(2,1)S(1)} %get-tuple-element.10), channel_id=1, source_target_pairs={{0,0},{2,32},{4,64},{6,96},{8,128},{10,160},{12,192},{14,224},{16,... | collective-permute-start | bytes 393224 | tf_op jit(solution)/shard_map/ppermute | solution.py:38
  33.1 7.5 %collective-permute-start.1 = (bf16[16,32,128]{2,0,1:T(8,128)(2,1)S(1)}, bf16[16,32,128]{2,0,1:T(8,128)(2,1)S(1)}, u32[]{:S(2)}, u32[]{:S(2)}) collective-permute-start(bf16[16,32,128]{2,0,1:T(8,128)(2,1)S(1)} %bitcast.77), channel_id=1, source_target_pairs={{0,32},{32,0},{64,96},{96,64},{128,160},{160,128},{192,224},{224,1... | collective-permute-start | bytes 393224 | tf_op jit(solution)/shard_map/ppermute | solution.py:68
  40.7 9.5 %collective-permute-start.2 = (bf16[2,16,32,128]{3,1,2,0:T(8,128)(2,1)S(1)}, bf16[2,16,32,128]{3,1,2,0:T(8,128)(2,1)S(1)}, u32[]{:S(2)}, u32[]{:S(2)}) collective-permute-start(bf16[2,16,32,128]{3,1,2,0:T(8,128)(2,1)S(1)} %maximum_select_fusion.1), channel_id=1, source_target_pairs={{0,64},{32,96},{64,128},{96,160},{128,192},{160,224},{192,256},{22... | collective-permute-start | bytes 786440 | tf_op jit(solution)/shard_map/ppermute | solution.py:74
  50.2 8.6 %collective-permute-start.3 = (bf16[2,16,32,128]{3,1,2,0:T(8,128)(2,1)S(1)}, bf16[2,16,32,128]{3,1,2,0:T(8,128)(2,1)S(1)}, u32[]{:S(2)}, u32[]{:S(2)}) collective-permute-start(bf16[2,16,32,128]{3,1,2,0:T(8,128)(2,1)S(1)} %collective-permute-done.2), channel_id=1, source_target_pairs={{0,64},{32,96},{64,128},{96,160},{128,192},{160,224},{192,256},{22... | collective-permute-start | bytes 786440 | tf_op jit(solution)/shard_map/ppermute | solution.py:74
  53.6 10.9 %collective-permute-start.6 = (bf16[2,16,32,128]{3,1,2,0:T(8,128)(2,1)S(1)}, bf16[2,16,32,128]{3,1,2,0:T(8,128)(2,1)S(1)}, u32[]{:S(2)}, u32[]{:S(2)}) collective-permute-start(bf16[2,16,32,128]{3,1,2,0:T(8,128)(2,1)S(1)} %maximum_select_fusion.1), channel_id=1, source_target_pairs={{0,448},{32,480},{64,0},{96,32},{128,64},{160,96},{192,128},{224,1... | collective-permute-start | bytes 786440 | tf_op jit(solution)/shard_map/ppermute | solution.py:77
  58.8 8.8 %collective-permute-start.4 = (bf16[2,16,32,128]{3,1,2,0:T(8,128)(2,1)S(1)}, bf16[2,16,32,128]{3,1,2,0:T(8,128)(2,1)S(1)}, u32[]{:S(2)}, u32[]{:S(2)}) collective-permute-start(bf16[2,16,32,128]{3,1,2,0:T(8,128)(2,1)S(1)} %collective-permute-done.3), channel_id=1, source_target_pairs={{0,64},{32,96},{64,128},{96,160},{128,192},{160,224},{192,256},{22... | collective-permute-start | bytes 786440 | tf_op jit(solution)/shard_map/ppermute | solution.py:74
  64.5 9.5 %collective-permute-start.7 = (bf16[2,16,32,128]{3,1,2,0:T(8,128)(2,1)S(1)}, bf16[2,16,32,128]{3,1,2,0:T(8,128)(2,1)S(1)}, u32[]{:S(2)}, u32[]{:S(2)}) collective-permute-start(bf16[2,16,32,128]{3,1,2,0:T(8,128)(2,1)S(1)} %collective-permute-done.6), channel_id=1, source_target_pairs={{0,448},{32,480},{64,0},{96,32},{128,64},{160,96},{192,128},{224,1... | collective-permute-start | bytes 786440 | tf_op jit(solution)/shard_map/ppermute | solution.py:77
  67.6 9.5 %collective-permute-start.5 = (bf16[2,16,32,128]{3,1,2,0:T(8,128)(2,1)S(1)}, bf16[2,16,32,128]{3,1,2,0:T(8,128)(2,1)S(1)}, u32[]{:S(2)}, u32[]{:S(2)}) collective-permute-start(bf16[2,16,32,128]{3,1,2,0:T(8,128)(2,1)S(1)} %collective-permute-done.4), channel_id=1, source_target_pairs={{0,64},{32,96},{64,128},{96,160},{128,192},{160,224},{192,256},{22... | collective-permute-start | bytes 786440 | tf_op jit(solution)/shard_map/ppermute | solution.py:74
  74.0 9.5 %collective-permute-start.8 = (bf16[2,16,32,128]{3,1,2,0:T(8,128)(2,1)S(1)}, bf16[2,16,32,128]{3,1,2,0:T(8,128)(2,1)S(1)}, u32[]{:S(2)}, u32[]{:S(2)}) collective-permute-start(bf16[2,16,32,128]{3,1,2,0:T(8,128)(2,1)S(1)} %collective-permute-done.7), channel_id=1, source_target_pairs={{0,448},{32,480},{64,0},{96,32},{128,64},{160,96},{192,128},{224,1... | collective-permute-start | bytes 786440 | tf_op jit(solution)/shard_map/ppermute | solution.py:77
  94.2 15.8 %copy-start.2 = (bf16[32,16,128]{2,1,0:T(8,128)(2,1)S(1)}, bf16[32,16,128]{2,1,0:T(8,128)(2,1)}, u32[]{:S(2)}) copy-start(bf16[32,16,128]{2,1,0:T(8,128)(2,1)} %param.5) | copy-start | bytes 393220
  94.2 15.8 %copy-start.4 = (bf16[2,128,128]{2,1,0:T(8,128)(2,1)S(1)}, bf16[2,128,128]{2,1,0:T(8,128)(2,1)}, u32[]{:S(2)}) copy-start(bf16[2,128,128]{2,1,0:T(8,128)(2,1)} %param.8) | copy-start | bytes 196612
  105.6 8.5 %collective-permute-start.9 = (bf16[32,16,128]{2,1,0:T(8,128)(2,1)S(1)}, bf16[32,16,128]{2,1,0:T(8,128)(2,1)S(1)}, u32[]{:S(2)}, u32[]{:S(2)}) collective-permute-start(bf16[32,16,128]{2,1,0:T(8,128)(2,1)S(1)} %dynamic-slice_convert_fusion), channel_id=1, source_target_pairs={{0,1},{1,0},{2,3},{3,2},{4,5},{5,4},{6,7},{7,6},{8,9},{9,8},{10,11... | collective-permute-start | bytes 393224 | tf_op jit(solution)/shard_map/ppermute | solution.py:53
  115.8 20.1 %collective-permute-start.10 = (bf16[32,16,128]{2,1,0:T(8,128)(2,1)S(1)}, bf16[32,16,128]{2,1,0:T(8,128)(2,1)S(1)}, u32[]{:S(2)}, u32[]{:S(2)}) collective-permute-start(bf16[32,16,128]{2,1,0:T(8,128)(2,1)S(1)} %get-tuple-element.7), channel_id=1, source_target_pairs={{0,0},{2,32},{4,64},{6,96},{8,128},{10,160},{12,192},{14,224},{16,... | collective-permute-start | bytes 393224 | tf_op jit(solution)/shard_map/ppermute | solution.py:38
  135.9 8.4 %collective-permute-start.11 = (bf16[32,16,128]{2,1,0:T(8,128)(2,1)S(1)}, bf16[32,16,128]{2,1,0:T(8,128)(2,1)S(1)}, u32[]{:S(2)}, u32[]{:S(2)}) collective-permute-start(bf16[32,16,128]{2,1,0:T(8,128)(2,1)S(1)} %collective-permute-done.10), channel_id=1, source_target_pairs={{0,1},{1,0},{2,3},{3,2},{4,5},{5,4},{6,7},{7,6},{8,9},{9,8},{10,11... | collective-permute-start | bytes 393224 | tf_op jit(solution)/shard_map/ppermute | solution.py:59
  145.1 6.9 %collective-permute-start.12 = (bf16[32,16,128]{2,1,0:T(8,128)(2,1)S(1)}, bf16[32,16,128]{2,1,0:T(8,128)(2,1)S(1)}, u32[]{:S(2)}, u32[]{:S(2)}) collective-permute-start(bf16[32,16,128]{2,1,0:T(8,128)(2,1)S(1)} %get-tuple-element.8), channel_id=1, source_target_pairs={{0,32},{32,0},{64,96},{96,64},{128,160},{160,128},{192,224},{224,1... | collective-permute-start | bytes 393224 | tf_op jit(solution)/shard_map/ppermute | solution.py:68
  152.0 10.5 %collective-permute-start.13 = (bf16[2,32,16,128]{3,2,1,0:T(8,128)(2,1)S(1)}, bf16[2,32,16,128]{3,2,1,0:T(8,128)(2,1)S(1)}, u32[]{:S(2)}, u32[]{:S(2)}) collective-permute-start(bf16[2,32,16,128]{3,2,1,0:T(8,128)(2,1)S(1)} %maximum_select_fusion.4), channel_id=1, source_target_pairs={{0,64},{32,96},{64,128},{96,160},{128,192},{160,224},{192,256},{22... | collective-permute-start | bytes 786440 | tf_op jit(solution)/shard_map/ppermute | solution.py:74
  162.6 10.9 %collective-permute-start.14 = (bf16[2,32,16,128]{3,2,1,0:T(8,128)(2,1)S(1)}, bf16[2,32,16,128]{3,2,1,0:T(8,128)(2,1)S(1)}, u32[]{:S(2)}, u32[]{:S(2)}) collective-permute-start(bf16[2,32,16,128]{3,2,1,0:T(8,128)(2,1)S(1)} %collective-permute-done.13), channel_id=1, source_target_pairs={{0,64},{32,96},{64,128},{96,160},{128,192},{160,224},{192,256},{22... | collective-permute-start | bytes 786440 | tf_op jit(solution)/shard_map/ppermute | solution.py:74
  164.6 11.9 %collective-permute-start.17 = (bf16[2,32,16,128]{3,2,1,0:T(8,128)(2,1)S(1)}, bf16[2,32,16,128]{3,2,1,0:T(8,128)(2,1)S(1)}, u32[]{:S(2)}, u32[]{:S(2)}) collective-permute-start(bf16[2,32,16,128]{3,2,1,0:T(8,128)(2,1)S(1)} %maximum_select_fusion.4), channel_id=1, source_target_pairs={{0,448},{32,480},{64,0},{96,32},{128,64},{160,96},{192,128},{224,1... | collective-permute-start | bytes 786440 | tf_op jit(solution)/shard_map/ppermute | solution.py:77
  173.4 10.1 %collective-permute-start.15 = (bf16[2,32,16,128]{3,2,1,0:T(8,128)(2,1)S(1)}, bf16[2,32,16,128]{3,2,1,0:T(8,128)(2,1)S(1)}, u32[]{:S(2)}, u32[]{:S(2)}) collective-permute-start(bf16[2,32,16,128]{3,2,1,0:T(8,128)(2,1)S(1)} %collective-permute-done.14), channel_id=1, source_target_pairs={{0,64},{32,96},{64,128},{96,160},{128,192},{160,224},{192,256},{22... | collective-permute-start | bytes 786440 | tf_op jit(solution)/shard_map/ppermute | solution.py:74
  176.5 12.2 %collective-permute-start.18 = (bf16[2,32,16,128]{3,2,1,0:T(8,128)(2,1)S(1)}, bf16[2,32,16,128]{3,2,1,0:T(8,128)(2,1)S(1)}, u32[]{:S(2)}, u32[]{:S(2)}) collective-permute-start(bf16[2,32,16,128]{3,2,1,0:T(8,128)(2,1)S(1)} %collective-permute-done.17), channel_id=1, source_target_pairs={{0,448},{32,480},{64,0},{96,32},{128,64},{160,96},{192,128},{224,1... | collective-permute-start | bytes 786440 | tf_op jit(solution)/shard_map/ppermute | solution.py:77
  183.5 8.3 %collective-permute-start.16 = (bf16[2,32,16,128]{3,2,1,0:T(8,128)(2,1)S(1)}, bf16[2,32,16,128]{3,2,1,0:T(8,128)(2,1)S(1)}, u32[]{:S(2)}, u32[]{:S(2)}) collective-permute-start(bf16[2,32,16,128]{3,2,1,0:T(8,128)(2,1)S(1)} %collective-permute-done.15), channel_id=1, source_target_pairs={{0,64},{32,96},{64,128},{96,160},{128,192},{160,224},{192,256},{22... | collective-permute-start | bytes 786440 | tf_op jit(solution)/shard_map/ppermute | solution.py:74
  188.7 9.5 %collective-permute-start.19 = (bf16[2,32,16,128]{3,2,1,0:T(8,128)(2,1)S(1)}, bf16[2,32,16,128]{3,2,1,0:T(8,128)(2,1)S(1)}, u32[]{:S(2)}, u32[]{:S(2)}) collective-permute-start(bf16[2,32,16,128]{3,2,1,0:T(8,128)(2,1)S(1)} %collective-permute-done.18), channel_id=1, source_target_pairs={{0,448},{32,480},{64,0},{96,32},{128,64},{160,96},{192,128},{224,1... | collective-permute-start | bytes 786440 | tf_op jit(solution)/shard_map/ppermute | solution.py:77
  (4 other events, 25.1 us)
Sparse Core Ops, SparseCore 0:
  11.8 48.8 all-gather.2
  145.2 44.1 all-gather.4

commit v9 on v7

--- a/solution.py
+++ b/solution.py
@@ -1,7 +1,10 @@
 import jax
 import jax.numpy as jnp
 from jax import lax
-from jax.sharding import PartitionSpec as P
+import numpy as np
+from jax.sharding import Mesh, PartitionSpec as P
+
+ROW, COL = ("y", "xl"), ("z", "core")
 
 
 def layer_norm(value):
@@ -35,7 +38,7 @@
 
 def transpose_tiles(value, n):
     perm = [(r * n + c, c * n + r) for r in range(n) for c in range(n)]
-    return lax.ppermute(value, ("row", "col"), perm)
+    return lax.ppermute(value, ROW + COL, perm)
 
 
 def gather_a2a(value, axis_name, n, axis):
@@ -62,11 +65,21 @@
     )
 
 
+def gather_over_row(value):
+    me = lax.axis_index("xl")
+    swapped = lax.ppermute(value, "xl", [(0, 1), (1, 0)])
+    pair = jnp.where(me == 0, jnp.stack([value, swapped]), jnp.stack([swapped, value]))
+    ny = lax.psum(1, "y")
+    copies = jnp.broadcast_to(pair[None], (ny,) + pair.shape)
+    got = lax.all_to_all(copies, "y", 0, 0, tiled=False)
+    return got.reshape((2 * ny * value.shape[0],) + value.shape[1:])
+
+
 def on_device(n, pair, pair_mask, w_in, w_gate, w_out):
     valid = pair_mask.astype(jnp.float32)[..., None]
     left, right, gate = prepare(pair, valid, w_in[0], w_gate[0])
-    left_rows = lax.all_gather(jnp.swapaxes(left, 0, 1), "col", axis=0, tiled=True)
-    right_diag = gather_a2a(jnp.swapaxes(transpose_tiles(right, n), 0, 1), "row", n, 0)
+    left_rows = lax.all_gather(jnp.swapaxes(left, 0, 1), COL, axis=0, tiled=True)
+    right_diag = gather_over_row(jnp.swapaxes(transpose_tiles(right, n), 0, 1))
     partial_value = jnp.sum(
         left_rows[:, :, None].astype(jnp.float32) * right_diag[:, None].astype(jnp.float32),
         axis=0,
@@ -74,9 +87,9 @@
     tri = sum_over_ka(partial_value)
     middle = finish(pair, tri, gate, w_out[0])
     left, right, gate = prepare(middle, valid, w_in[1], w_gate[1])
-    right_cols = gather_a2a(right, "row", n, 0)
+    right_cols = gather_over_row(right)
     left_tile = join_over_ka(transpose_tiles(left, n))
-    left_diag = lax.all_gather(left_tile, "col", axis=0, tiled=True)
+    left_diag = lax.all_gather(left_tile, COL, axis=0, tiled=True)
     tri = jnp.sum(
         left_diag[:, :, None].astype(jnp.float32) * right_cols[:, None].astype(jnp.float32), axis=0
     )
@@ -86,11 +99,13 @@
 def solution(mesh):
     n = mesh.shape["row"]
     assert mesh.shape["col"] == n
-    placed = (P("row", ("col", "ka"), None), P("row", ("col", "ka")), P(), P(), P())
+    devices = np.asarray(mesh.devices).reshape(n // 2, 2, n // 2, 2, mesh.shape["ka"])
+    fine = Mesh(devices, ("y", "xl", "z", "core", "ka"))
+    placed = (P(ROW, COL + ("ka",), None), P(ROW, COL + ("ka",)), P(), P(), P())
     return jax.shard_map(
         lambda *a: on_device(n, *a),
-        mesh=mesh,
+        mesh=fine,
         in_specs=placed,
-        out_specs=P("row", ("col", "ka"), None),
+        out_specs=P(ROW, COL + ("ka",), None),
         check_vma=False,
     )

time: 223 us -> 240 us (1.076)
  waiting for transfers between devices: 102 us -> 123 us
  starting transfers between devices: 57.4 us -> 52.2 us
  local copies, waits for them, and re-layouts: 9.84 us -> 6.66 us
    all_to_all x2, waiting for transfers between devices: 66.1 us -> 98.3 us  [gather_over_row(): got = lax.all_to_all(copies, 'y', 0, 0, tiled=False)]
    all_gather x2, waiting for transfers between devices: 25.4 us -> 0.01 us  [the longest x1 0.01 us: on_device(): lax.all_gather(jnp.swapaxes(left, 0, 1), COL, axis=0, tiled=True)]
    ppermute x2 -> x4, waiting for transfers between devices: 5.43 us -> 17.2 us  [the longest x2 9.76 us: gather_over_row(): swapped = lax.ppermute(value, 'xl', [(0, 1), (1, 0)])]
    all_to_all x2, starting transfers between devices: 37.7 us -> 33.2 us  [gather_over_row(): got = lax.all_to_all(copies, 'y', 0, 0, tiled=False)]
    ppermute x2 -> x4, starting transfers between devices: 10.7 us -> 11 us  [the longest x2 7.21 us: transpose_tiles(): return lax.ppermute(value, ROW + COL, perm)]
  transfers between devices with their start and end apart: 8 -> 10, of which waited for: 7 -> 8; matrix products, arithmetic and copies ran while one was open for 5% -> 3% of each run, Pallas kernels for 0% -> 0%
where the time goes in v9:
time: 240 us; the launch traced here: 237 us
  waiting for transfers between devices  123 us (51%)
  starting transfers between devices  52.2 us (22%)
  other arithmetic  37.5 us (16%)
  between operations  13.8 us (6%)
  local copies, waits for them, and re-layouts  6.66 us (3%)
  matrix products  3.72 us (2%)
    all_to_all x2, waiting for transfers between devices, gather_over_row(): got = lax.all_to_all(copies, 'y', 0, 0, tiled=False)  98.3 us
    all_to_all x2, starting transfers between devices, gather_over_row(): got = lax.all_to_all(copies, 'y', 0, 0, tiled=False)  33.2 us
    reduce_sum x3, other arithmetic, layer_norm(): mean = jnp.mean(value, axis=-1, keepdims=True)  13.1 us
    reduce_sum x1, other arithmetic, on_device(): jnp.sum(left_rows[:, :, None].astype(jnp.float32) * right_diag[:, None].a...  11.3 us
    ppermute x2, waiting for transfers between devices, gather_over_row(): swapped = lax.ppermute(value, 'xl', [(0, 1), (1, 0)])  9.76 us
    ppermute x2, waiting for transfers between devices, transpose_tiles(): return lax.ppermute(value, ROW + COL, perm)  7.49 us
    ppermute x2, starting transfers between devices, transpose_tiles(): return lax.ppermute(value, ROW + COL, perm)  7.21 us
  transfers between devices with their start and end apart: 10, of which 8 were waited for; matrix products, arithmetic and copies ran while one was open for 3% of the time, Pallas kernels for 0%

profile of v9, /device:TPU:1, one launch (start us, length us, event | category | flops | bytes accessed | tf_op | source)
XLA Modules:
  0.0 237.1 jit_solution(14760433425050541161)
XLA Ops:
  11.7 4.5 %collective-permute-start = (bf16[32,16,128]{2,1,0:T(8,128)(2,1)S(1)}, bf16[32,16,128]{2,1,0:T(8,128)(2,1)S(1)}, u32[]{:S(2)}, u32[]{:S(2)}) collective-permute-start(bf16[32,16,128]{2,1,0:T(8,128)(2,1)S(1)} %get-tuple-element.10), channel_id=1, source_target_pairs={{0,0},{2,32},{4,64},{6,96},{8,128},{10,160},{12,192},{14,224},{16,... | collective-permute-start | bytes 393224 | tf_op jit(solution)/shard_map/ppermute | solution.py:41
  16.2 2.6 %collective-permute-done = bf16[32,16,128]{2,1,0:T(8,128)(2,1)S(1)} collective-permute-done((bf16[32,16,128]{2,1,0:T(8,128)(2,1)S(1)}, bf16[32,16,128]{2,1,0:T(8,128)(2,1)S(1)}, u32[]{:S(2)}, u32[]{:S(2)}) %collective-permute-start) | collective-permute-done | bytes 131104 | tf_op jit(solution)/shard_map/ppermute | solution.py:41
  18.8 1.9 collective-permute-start.1
  20.8 4.6 %collective-permute-done.1 = bf16[16,32,128]{2,0,1:T(8,128)(2,1)S(1)} collective-permute-done((bf16[16,32,128]{2,0,1:T(8,128)(2,1)S(1)}, bf16[16,32,128]{2,0,1:T(8,128)(2,1)S(1)}, u32[]{:S(2)}, u32[]{:S(2)}) %collective-permute-start.1) | collective-permute-done | bytes 131104 | tf_op jit(solution)/shard_map/ppermute | solution.py:70
  25.5 1.8 broadcast_in_dim.4
  27.2 21.7 %all-to-all-start = ((bf16[8,2,16,32,128]{4,3,2,1,0:T(8,128)(2,1)}), bf16[8,2,16,32,128]{4,3,2,1,0:T(8,128)(2,1)S(1)}, u32[]{:S(2)}, u32[]{:S(2)}) async-start(bf16[8,2,16,32,128]{4,3,2,1,0:T(8,128)(2,1)} %broadcast_in_dim.4), calls=%async_computation | async-start | bytes 4194304 | tf_op jit(solution)/shard_map/all_to_all | solution.py:74
  49.8 50.9 %all-to-all-done = bf16[8,2,16,32,128]{4,3,2,1,0:T(8,128)(2,1)S(1)} async-done(((bf16[8,2,16,32,128]{4,3,2,1,0:T(8,128)(2,1)}), bf16[8,2,16,32,128]{4,3,2,1,0:T(8,128)(2,1)S(1)}, u32[]{:S(2)}, u32[]{:S(2)}) %all-to-all-start) | async-done | bytes 2097184 | tf_op jit(solution)/shard_map/all_to_all | solution.py:74
  100.6 2.7 %bitcast_convert_fusion = f32[256,32,128]{2,1,0:T(8,128)} fusion(bf16[8,2,16,32,128]{4,3,2,1,0:T(8,128)(2,1)S(1)} %all-to-all-done), kind=kLoop, calls=%fused_computation.3 | loop fusion | flops 1048576 | bytes 6291456 | tf_op jit(solution)/shard_map/convert_element_type | solution.py:84
  103.3 3.0 %copy.13 = f32[256,32,128]{2,1,0:T(8,128)S(1)} copy(bf16[256,32,128]{2,0,1:T(8,128)(2,1)} %all-gather.3.cloned.1.call-done) | data formatting | bytes 6291456 | tf_op jit(solution)/shard_map/convert_element_type | solution.py:84
  106.3 11.3 %multiply_reduce_fusion.2 = f32[32,32,128]{2,1,0:T(8,128)S(1)} fusion(f32[256,32,128]{2,1,0:T(8,128)S(1)} %copy-done.1, f32[256,32,128]{2,1,0:T(8,128)S(1)} %copy.13), kind=kLoop, calls=%fused_computation.2 | loop fusion | flops 66977792 | bytes 8912896 | tf_op jit(solution)/shard_map/reduce_sum | solution.py:83
  117.7 4.1 %collective-permute-start.2 = (bf16[32,16,128]{2,1,0:T(8,128)(2,1)S(1)}, bf16[32,16,128]{2,1,0:T(8,128)(2,1)S(1)}, u32[]{:S(2)}, u32[]{:S(2)}) collective-permute-start(bf16[32,16,128]{2,1,0:T(8,128)(2,1)S(1)} %dynamic-slice_convert_fusion), channel_id=1, source_target_pairs={{0,1},{1,0},{2,3},{3,2},{4,5},{5,4},{6,7},{7,6},{8,9},{9,8},{10,11... | collective-permute-start | bytes 393224 | tf_op jit(solution)/shard_map/ppermute | solution.py:56
  122.2 3.6 %collective-permute-done.2 = bf16[32,16,128]{2,1,0:T(8,128)(2,1)S(1)} collective-permute-done((bf16[32,16,128]{2,1,0:T(8,128)(2,1)S(1)}, bf16[32,16,128]{2,1,0:T(8,128)(2,1)S(1)}, u32[]{:S(2)}, u32[]{:S(2)}) %collective-permute-start.2) | collective-permute-done | bytes 131104 | tf_op jit(solution)/shard_map/ppermute | solution.py:56
  127.5 2.7 %collective-permute-start.3 = (bf16[32,16,128]{2,1,0:T(8,128)(2,1)S(1)}, bf16[32,16,128]{2,1,0:T(8,128)(2,1)S(1)}, u32[]{:S(2)}, u32[]{:S(2)}) collective-permute-start(bf16[32,16,128]{2,1,0:T(8,128)(2,1)S(1)} %get-tuple-element.7), channel_id=1, source_target_pairs={{0,0},{2,32},{4,64},{6,96},{8,128},{10,160},{12,192},{14,224},{16,... | collective-permute-start | bytes 393224 | tf_op jit(solution)/shard_map/ppermute | solution.py:41
  130.2 4.9 %collective-permute-done.3 = bf16[32,16,128]{2,1,0:T(8,128)(2,1)S(1)} collective-permute-done((bf16[32,16,128]{2,1,0:T(8,128)(2,1)S(1)}, bf16[32,16,128]{2,1,0:T(8,128)(2,1)S(1)}, u32[]{:S(2)}, u32[]{:S(2)}) %collective-permute-start.3) | collective-permute-done | bytes 131104 | tf_op jit(solution)/shard_map/ppermute | solution.py:41
  135.1 3.8 %collective-permute-start.4 = (bf16[32,16,128]{2,1,0:T(8,128)(2,1)S(1)}, bf16[32,16,128]{2,1,0:T(8,128)(2,1)S(1)}, u32[]{:S(2)}, u32[]{:S(2)}) collective-permute-start(bf16[32,16,128]{2,1,0:T(8,128)(2,1)S(1)} %collective-permute-done.3), channel_id=1, source_target_pairs={{0,1},{1,0},{2,3},{3,2},{4,5},{5,4},{6,7},{7,6},{8,9},{9,8},{10,11... | collective-permute-start | bytes 393224 | tf_op jit(solution)/shard_map/ppermute | solution.py:62
  138.8 3.4 %collective-permute-done.4 = bf16[32,16,128]{2,1,0:T(8,128)(2,1)S(1)} collective-permute-done((bf16[32,16,128]{2,1,0:T(8,128)(2,1)S(1)}, bf16[32,16,128]{2,1,0:T(8,128)(2,1)S(1)}, u32[]{:S(2)}, u32[]{:S(2)}) %collective-permute-start.4) | collective-permute-done | bytes 131104 | tf_op jit(solution)/shard_map/ppermute | solution.py:62
  143.1 1.9 collective-permute-start.5
  145.0 5.1 %collective-permute-done.5 = bf16[32,16,128]{2,1,0:T(8,128)(2,1)S(1)} collective-permute-done((bf16[32,16,128]{2,1,0:T(8,128)(2,1)S(1)}, bf16[32,16,128]{2,1,0:T(8,128)(2,1)S(1)}, u32[]{:S(2)}, u32[]{:S(2)}) %collective-permute-start.5) | collective-permute-done | bytes 131104 | tf_op jit(solution)/shard_map/ppermute | solution.py:70
  150.2 1.7 broadcast_in_dim.5
  151.9 11.5 %all-to-all-start.1 = ((bf16[8,2,32,16,128]{4,3,2,1,0:T(8,128)(2,1)}), bf16[8,2,32,16,128]{4,3,2,1,0:T(8,128)(2,1)S(1)}, u32[]{:S(2)}, u32[]{:S(2)}) async-start(bf16[8,2,32,16,128]{4,3,2,1,0:T(8,128)(2,1)} %broadcast_in_dim.5), calls=%async_computation.1 | async-start | bytes 4194304 | tf_op jit(solution)/shard_map/all_to_all | solution.py:74
  163.7 47.5 %all-to-all-done.1 = bf16[8,2,32,16,128]{4,3,2,1,0:T(8,128)(2,1)S(1)} async-done(((bf16[8,2,32,16,128]{4,3,2,1,0:T(8,128)(2,1)}), bf16[8,2,32,16,128]{4,3,2,1,0:T(8,128)(2,1)S(1)}, u32[]{:S(2)}, u32[]{:S(2)}) %all-to-all-start.1) | async-done | bytes 2097184 | tf_op jit(solution)/shard_map/all_to_all | solution.py:74
  211.2 2.3 convert.3
  213.5 3.5 %convert_element_type.92 = f32[512,32,128]{2,1,0:T(8,128)S(1)} convert(bf16[512,32,128]{2,1,0:T(8,128)(2,1)} %all-gather.5.cloned.1.call-done) | non-fusion elementwise | flops 2097152 | bytes 12582912 | tf_op jit(solution)/shard_map/convert_element_type | solution.py:94
  217.0 12.0 %multiply_reduce_fusion = (f32[32,16]{1,0:T(8,128)S(1)}, f32[32,16,128]{2,1,0:T(8,128)S(1)}) fusion(f32[512,16,128]{2,1,0:T(8,128)S(1)} %copy-done, f32[512,32,128]{2,1,0:T(8,128)S(1)} %convert_element_type.92), kind=kLoop, calls=%fused_computation | loop fusion | flops 100597248 | bytes 12847104 | tf_op jit(solution)/shard_map/reduce_sum | solution.py:11
  (47 shorter events, 10.4 us)
Async XLA Ops:
  11.7 7.1 %collective-permute-start = (bf16[32,16,128]{2,1,0:T(8,128)(2,1)S(1)}, bf16[32,16,128]{2,1,0:T(8,128)(2,1)S(1)}, u32[]{:S(2)}, u32[]{:S(2)}) collective-permute-start(bf16[32,16,128]{2,1,0:T(8,128)(2,1)S(1)} %get-tuple-element.10), channel_id=1, source_target_pairs={{0,0},{2,32},{4,64},{6,96},{8,128},{10,160},{12,192},{14,224},{16,... | collective-permute-start | bytes 393224 | tf_op jit(solution)/shard_map/ppermute | solution.py:41
  18.8 6.5 %collective-permute-start.1 = (bf16[16,32,128]{2,0,1:T(8,128)(2,1)S(1)}, bf16[16,32,128]{2,0,1:T(8,128)(2,1)S(1)}, u32[]{:S(2)}, u32[]{:S(2)}) collective-permute-start(bf16[16,32,128]{2,0,1:T(8,128)(2,1)S(1)} %bitcast.41), channel_id=1, source_target_pairs={{0,32},{32,0},{1,33},{33,1},{2,34},{34,2},{3,35},{35,3},{4,36},{36... | collective-permute-start | bytes 393224 | tf_op jit(solution)/shard_map/ppermute | solution.py:70
  27.2 73.4 %all-to-all-start = ((bf16[8,2,16,32,128]{4,3,2,1,0:T(8,128)(2,1)}), bf16[8,2,16,32,128]{4,3,2,1,0:T(8,128)(2,1)S(1)}, u32[]{:S(2)}, u32[]{:S(2)}) async-start(bf16[8,2,16,32,128]{4,3,2,1,0:T(8,128)(2,1)} %broadcast_in_dim.4), calls=%async_computation | async-start | bytes 4194304 | tf_op jit(solution)/shard_map/all_to_all | solution.py:74
  49.0 54.3 %all-gather.3.cloned.1.call-start = ((), (), s32[]{:S(2)}) async-start(), calls=%async_computation.2 | async-start | bytes 2228224 | tf_op jit(solution)/shard_map/all_gather | solution.py:81
  49.7 163.8 %all-gather.5.cloned.1.call-start = ((), (), s32[]{:S(2)}) async-start(), calls=%async_computation.3 | async-start | bytes 4456448 | tf_op jit(solution)/shard_map/all_gather | solution.py:92
  103.3 3.0 %copy-start.1 = (f32[256,32,128]{2,1,0:T(8,128)S(1)}, f32[256,32,128]{2,1,0:T(8,128)}, u32[]{:S(2)}) copy-start(f32[256,32,128]{2,1,0:T(8,128)} %bitcast_convert_fusion) | copy-start | bytes 12582916
  106.3 15.6 %copy-start.2 = (bf16[32,16,128]{2,1,0:T(8,128)(2,1)S(1)}, bf16[32,16,128]{2,1,0:T(8,128)(2,1)}, u32[]{:S(2)}) copy-start(bf16[32,16,128]{2,1,0:T(8,128)(2,1)} %param.5) | copy-start | bytes 393220
  106.3 15.6 %copy-start.4 = (bf16[2,128,128]{2,1,0:T(8,128)(2,1)S(1)}, bf16[2,128,128]{2,1,0:T(8,128)(2,1)}, u32[]{:S(2)}) copy-start(bf16[2,128,128]{2,1,0:T(8,128)(2,1)} %param.8) | copy-start | bytes 196612
  106.3 19.9 %copy-start.5 = (bf16[2,128,128]{2,1,0:T(8,128)(2,1)S(1)}, bf16[2,128,128]{2,1,0:T(8,128)(2,1)}, u32[]{:S(2)}) copy-start(bf16[2,128,128]{2,1,0:T(8,128)(2,1)} %param.9) | copy-start | bytes 196612
  117.6 9.3 %copy-start.3 = (bf16[2,128,512]{2,1,0:T(8,128)(2,1)S(1)}, bf16[2,128,512]{2,1,0:T(8,128)(2,1)}, u32[]{:S(2)}) copy-start(bf16[2,128,512]{2,1,0:T(8,128)(2,1)} %param.7) | copy-start | bytes 786436
  117.7 8.1 %collective-permute-start.2 = (bf16[32,16,128]{2,1,0:T(8,128)(2,1)S(1)}, bf16[32,16,128]{2,1,0:T(8,128)(2,1)S(1)}, u32[]{:S(2)}, u32[]{:S(2)}) collective-permute-start(bf16[32,16,128]{2,1,0:T(8,128)(2,1)S(1)} %dynamic-slice_convert_fusion), channel_id=1, source_target_pairs={{0,1},{1,0},{2,3},{3,2},{4,5},{5,4},{6,7},{7,6},{8,9},{9,8},{10,11... | collective-permute-start | bytes 393224 | tf_op jit(solution)/shard_map/ppermute | solution.py:56
  127.5 7.6 %collective-permute-start.3 = (bf16[32,16,128]{2,1,0:T(8,128)(2,1)S(1)}, bf16[32,16,128]{2,1,0:T(8,128)(2,1)S(1)}, u32[]{:S(2)}, u32[]{:S(2)}) collective-permute-start(bf16[32,16,128]{2,1,0:T(8,128)(2,1)S(1)} %get-tuple-element.7), channel_id=1, source_target_pairs={{0,0},{2,32},{4,64},{6,96},{8,128},{10,160},{12,192},{14,224},{16,... | collective-permute-start | bytes 393224 | tf_op jit(solution)/shard_map/ppermute | solution.py:41
  135.1 7.2 %collective-permute-start.4 = (bf16[32,16,128]{2,1,0:T(8,128)(2,1)S(1)}, bf16[32,16,128]{2,1,0:T(8,128)(2,1)S(1)}, u32[]{:S(2)}, u32[]{:S(2)}) collective-permute-start(bf16[32,16,128]{2,1,0:T(8,128)(2,1)S(1)} %collective-permute-done.3), channel_id=1, source_target_pairs={{0,1},{1,0},{2,3},{3,2},{4,5},{5,4},{6,7},{7,6},{8,9},{9,8},{10,11... | collective-permute-start | bytes 393224 | tf_op jit(solution)/shard_map/ppermute | solution.py:62
  143.1 7.1 %collective-permute-start.5 = (bf16[32,16,128]{2,1,0:T(8,128)(2,1)S(1)}, bf16[32,16,128]{2,1,0:T(8,128)(2,1)S(1)}, u32[]{:S(2)}, u32[]{:S(2)}) collective-permute-start(bf16[32,16,128]{2,1,0:T(8,128)(2,1)S(1)} %get-tuple-element.8), channel_id=1, source_target_pairs={{0,32},{32,0},{1,33},{33,1},{2,34},{34,2},{3,35},{35,3},{4,36},{36... | collective-permute-start | bytes 393224 | tf_op jit(solution)/shard_map/ppermute | solution.py:70
  151.9 59.3 %all-to-all-start.1 = ((bf16[8,2,32,16,128]{4,3,2,1,0:T(8,128)(2,1)}), bf16[8,2,32,16,128]{4,3,2,1,0:T(8,128)(2,1)S(1)}, u32[]{:S(2)}, u32[]{:S(2)}) async-start(bf16[8,2,32,16,128]{4,3,2,1,0:T(8,128)(2,1)} %broadcast_in_dim.5), calls=%async_computation.1 | async-start | bytes 4194304 | tf_op jit(solution)/shard_map/all_to_all | solution.py:74
  213.5 3.5 %copy-start = (f32[512,16,128]{2,1,0:T(8,128)S(1)}, f32[512,16,128]{2,1,0:T(8,128)}, u32[]{:S(2)}) copy-start(f32[512,16,128]{2,1,0:T(8,128)} %convert.3) | copy-start | bytes 12582916
Sparse Core Ops, SparseCore 0:
  51.8 46.1 all-gather.2
  143.2 53.0 all-gather.4

commit v10 on v7

--- a/solution.py
+++ b/solution.py
@@ -67,11 +67,19 @@
     left, right, gate = prepare(pair, valid, w_in[0], w_gate[0])
     left_rows = lax.all_gather(jnp.swapaxes(left, 0, 1), "col", axis=0, tiled=True)
     right_diag = gather_a2a(jnp.swapaxes(transpose_tiles(right, n), 0, 1), "row", n, 0)
-    partial_value = jnp.sum(
-        left_rows[:, :, None].astype(jnp.float32) * right_diag[:, None].astype(jnp.float32),
-        axis=0,
+    half = right_diag.shape[1] // 2
+    me = lax.axis_index("ka")
+    theirs = lax.dynamic_slice_in_dim(right_diag, (1 - me) * half, half, axis=1)
+    mine = lax.dynamic_slice_in_dim(right_diag, me * half, half, axis=1)
+    sent = jnp.sum(
+        left_rows[:, :, None].astype(jnp.float32) * theirs[:, None].astype(jnp.float32), axis=0
+    ).astype(jnp.bfloat16)
+    sent, left_later, mine = lax.optimization_barrier((sent, left_rows, mine))
+    got = lax.ppermute(sent, "ka", [(0, 1), (1, 0)])
+    kept = jnp.sum(
+        left_later[:, :, None].astype(jnp.float32) * mine[:, None].astype(jnp.float32), axis=0
     )
-    tri = sum_over_ka(partial_value)
+    tri = kept + got.astype(jnp.float32)
     middle = finish(pair, tri, gate, w_out[0])
     left, right, gate = prepare(middle, valid, w_in[1], w_gate[1])
     right_cols = gather_a2a(right, "row", n, 0)

time: 223 us -> 222 us (level)
  waiting for transfers between devices: 102 us -> 99.3 us
    reduce_sum x1 -> x2, other arithmetic: 11.3 us -> 11.2 us  [the longest x1 5.63 us: on_device(): jnp.sum(left_rows[:, :, None].astype(jnp.float32) * theirs[:, None].astyp...]
  transfers between devices with their start and end apart: 8 -> 8, of which waited for: 7 -> 6; matrix products, arithmetic and copies ran while one was open for 5% -> 8% of each run, Pallas kernels for 0% -> 0%
where the time goes in v10:
time: 222 us; the launch traced here: 220 us
  waiting for transfers between devices  99.3 us (45%)
  starting transfers between devices  56.8 us (26%)
  other arithmetic  35.1 us (16%)
  between operations  13.8 us (6%)
  local copies, waits for them, and re-layouts  11.5 us (5%)
  matrix products  3.73 us (2%)
    all_to_all x2, waiting for transfers between devices, gather_a2a(): got = lax.all_to_all(copies, axis_name, 0, 0, tiled=False)  66.6 us
    all_to_all x2, starting transfers between devices, gather_a2a(): got = lax.all_to_all(copies, axis_name, 0, 0, tiled=False)  38.4 us
    all_gather x1, waiting for transfers between devices, on_device(): lax.all_gather(jnp.swapaxes(left, 0, 1), 'col', axis=0, tiled=True)  25 us
    reduce_sum x3, other arithmetic, layer_norm(): mean = jnp.mean(value, axis=-1, keepdims=True)  13.1 us
    ppermute x2, starting transfers between devices, transpose_tiles(): return lax.ppermute(value, ('row', 'col'), perm)  8.58 us
    reduce_sum x1, other arithmetic, on_device(): jnp.sum(left_rows[:, :, None].astype(jnp.float32) * theirs[:, None].astyp...  5.63 us
    reduce_sum x1, other arithmetic, on_device(): jnp.sum(left_later[:, :, None].astype(jnp.float32) * mine[:, None].astype...  5.62 us
    ppermute x2, waiting for transfers between devices, transpose_tiles(): return lax.ppermute(value, ('row', 'col'), perm)  5.27 us
  transfers between devices with their start and end apart: 8, of which 6 were waited for; matrix products, arithmetic and copies ran while one was open for 8% of the time, Pallas kernels for 0%

profile of v10, /device:TPU:1, one launch (start us, length us, event | category | flops | bytes accessed | tf_op | source)
XLA Modules:
  0.0 220.1 jit_solution(18404984934848869823)
XLA Ops:
  7.6 1.1 fusion.13
  9.5 1.3 fusion.37
  11.7 4.5 %collective-permute-start = (bf16[32,16,128]{2,1,0:T(8,128)(2,1)S(1)}, bf16[32,16,128]{2,1,0:T(8,128)(2,1)S(1)}, u32[]{:S(2)}, u32[]{:S(2)}) collective-permute-start(bf16[32,16,128]{2,1,0:T(8,128)(2,1)S(1)} %get-tuple-element.18), channel_id=1, source_target_pairs={{0,0},{2,32},{4,64},{6,96},{8,128},{10,160},{12,192},{14,224},{16,... | collective-permute-start | bytes 393224 | tf_op jit(solution)/shard_map/ppermute | solution.py:38
  16.2 2.6 %collective-permute-done = bf16[32,16,128]{2,1,0:T(8,128)(2,1)S(1)} collective-permute-done((bf16[32,16,128]{2,1,0:T(8,128)(2,1)S(1)}, bf16[32,16,128]{2,1,0:T(8,128)(2,1)S(1)}, u32[]{:S(2)}, u32[]{:S(2)}) %collective-permute-start) | collective-permute-done | bytes 131104 | tf_op jit(solution)/shard_map/ppermute | solution.py:38
  18.9 1.8 broadcast_in_dim.4
  20.6 21.2 %all-to-all-start = ((bf16[16,16,32,128]{3,2,1,0:T(8,128)(2,1)}), bf16[16,16,32,128]{3,2,1,0:T(8,128)(2,1)S(1)}, u32[]{:S(2)}, u32[]{:S(2)}) async-start(bf16[16,16,32,128]{3,2,1,0:T(8,128)(2,1)} %broadcast_in_dim.4), calls=%async_computation | async-start | bytes 4194304 | tf_op jit(solution)/shard_map/all_to_all | solution.py:43
  42.3 25.0 %all-gather.3.cloned.1.call-done = bf16[256,32,128]{2,0,1:T(8,128)(2,1)} async-done(((bf16[16,32,128]{2,0,1:T(8,128)(2,1)}), bf16[256,32,128]{2,0,1:T(8,128)(2,1)}) %all-gather.3.cloned.1.call-update) | async-done | bytes 2097168 | tf_op jit(solution)/shard_map/all_gather | solution.py:68
  67.3 4.7 %copy.15 = f32[256,32,128]{2,1,0:T(8,128)} copy(bf16[256,32,128]{2,0,1:T(8,128)(2,1)} %all-gather.3.cloned.1.call-done) | data formatting | bytes 6291456 | tf_op jit(solution)/shard_map/convert_element_type | solution.py:75
  72.1 18.3 %all-to-all-done = bf16[16,16,32,128]{3,2,1,0:T(8,128)(2,1)S(1)} async-done(((bf16[16,16,32,128]{3,2,1,0:T(8,128)(2,1)}), bf16[16,16,32,128]{3,2,1,0:T(8,128)(2,1)S(1)}, u32[]{:S(2)}, u32[]{:S(2)}) %all-to-all-start) | async-done | bytes 2097184 | tf_op jit(solution)/shard_map/all_to_all | solution.py:43
  90.6 1.9 copy-done
  92.5 5.6 %multiply_reduce_fusion.3 = bf16[32,16,128]{2,1,0:T(8,128)(2,1)S(1)} fusion(f32[256,16,128]{2,1,0:T(8,128)S(1)} %get-tuple-element.14, f32[256,32,128]{2,1,0:T(8,128)S(1)} %copy-done), kind=kLoop, calls=%fused_computation.3 | loop fusion | flops 33488896 | bytes 6422528 | tf_op jit(solution)/shard_map/reduce_sum | solution.py:74
  98.2 1.2 copy.17
  99.6 5.0 %collective-permute-start.1 = (bf16[32,16,128]{2,1,0:T(8,128)(2,1)S(1)}, bf16[32,16,128]{2,1,0:T(8,128)(2,1)S(1)}, u32[]{:S(2)}, u32[]{:S(2)}) collective-permute-start(bf16[32,16,128]{2,1,0:T(8,128)(2,1)S(1)} %multiply_reduce_fusion.3), channel_id=1, source_target_pairs={{0,1},{1,0},{2,3},{3,2},{4,5},{5,4},{6,7},{7,6},{8,9},{9,8},{10,11... | collective-permute-start | bytes 393224 | tf_op jit(solution)/shard_map/ppermute | solution.py:78
  104.6 5.6 %multiply_reduce_fusion.2 = f32[32,16,128]{2,1,0:T(8,128)S(1)} fusion(f32[256,16,128]{2,1,0:T(8,128)S(1)} %convert_element_type.87, f32[256,32,128]{2,1,0:T(8,128)S(1)} %copy.17), kind=kLoop, calls=%fused_computation.2 | loop fusion | flops 33488896 | bytes 6553600 | tf_op jit(solution)/shard_map/reduce_sum | solution.py:79
  111.9 4.1 %collective-permute-start.2 = (bf16[32,16,128]{2,1,0:T(8,128)(2,1)S(1)}, bf16[32,16,128]{2,1,0:T(8,128)(2,1)S(1)}, u32[]{:S(2)}, u32[]{:S(2)}) collective-permute-start(bf16[32,16,128]{2,1,0:T(8,128)(2,1)S(1)} %get-tuple-element.15), channel_id=1, source_target_pairs={{0,0},{2,32},{4,64},{6,96},{8,128},{10,160},{12,192},{14,224},{16,... | collective-permute-start | bytes 393224 | tf_op jit(solution)/shard_map/ppermute | solution.py:38
  116.0 2.7 %collective-permute-done.2 = bf16[32,16,128]{2,1,0:T(8,128)(2,1)S(1)} collective-permute-done((bf16[32,16,128]{2,1,0:T(8,128)(2,1)S(1)}, bf16[32,16,128]{2,1,0:T(8,128)(2,1)S(1)}, u32[]{:S(2)}, u32[]{:S(2)}) %collective-permute-start.2) | collective-permute-done | bytes 131104 | tf_op jit(solution)/shard_map/ppermute | solution.py:38
  118.6 4.8 %collective-permute-start.3 = (bf16[32,16,128]{2,1,0:T(8,128)(2,1)S(1)}, bf16[32,16,128]{2,1,0:T(8,128)(2,1)S(1)}, u32[]{:S(2)}, u32[]{:S(2)}) collective-permute-start(bf16[32,16,128]{2,1,0:T(8,128)(2,1)S(1)} %collective-permute-done.2), channel_id=1, source_target_pairs={{0,1},{1,0},{2,3},{3,2},{4,5},{5,4},{6,7},{7,6},{8,9},{9,8},{10,11... | collective-permute-start | bytes 393224 | tf_op jit(solution)/shard_map/ppermute | solution.py:59
  123.5 2.4 %collective-permute-done.3 = bf16[32,16,128]{2,1,0:T(8,128)(2,1)S(1)} collective-permute-done((bf16[32,16,128]{2,1,0:T(8,128)(2,1)S(1)}, bf16[32,16,128]{2,1,0:T(8,128)(2,1)S(1)}, u32[]{:S(2)}, u32[]{:S(2)}) %collective-permute-start.3) | collective-permute-done | bytes 131104 | tf_op jit(solution)/shard_map/ppermute | solution.py:59
  126.7 1.7 broadcast_in_dim.5
  128.4 17.1 %all-to-all-start.1 = ((bf16[16,32,16,128]{3,2,1,0:T(8,128)(2,1)}), bf16[16,32,16,128]{3,2,1,0:T(8,128)(2,1)S(1)}, u32[]{:S(2)}, u32[]{:S(2)}) async-start(bf16[16,32,16,128]{3,2,1,0:T(8,128)(2,1)} %broadcast_in_dim.5), calls=%async_computation.1 | async-start | bytes 4194304 | tf_op jit(solution)/shard_map/all_to_all | solution.py:43
  145.9 48.3 %all-to-all-done.1 = bf16[16,32,16,128]{3,2,1,0:T(8,128)(2,1)S(1)} async-done(((bf16[16,32,16,128]{3,2,1,0:T(8,128)(2,1)}), bf16[16,32,16,128]{3,2,1,0:T(8,128)(2,1)S(1)}, u32[]{:S(2)}, u32[]{:S(2)}) %all-to-all-start.1) | async-done | bytes 2097184 | tf_op jit(solution)/shard_map/all_to_all | solution.py:43
  194.2 2.3 %convert.1 = f32[512,16,128]{2,1,0:T(8,128)} convert(bf16[512,16,128]{2,1,0:T(8,128)(2,1)S(1)} %bitcast.32) | non-fusion elementwise | flops 1048576 | bytes 6291456 | tf_op jit(solution)/shard_map/convert_element_type | solution.py:89
  196.5 3.5 %convert_element_type.94 = f32[512,32,128]{2,1,0:T(8,128)S(1)} convert(bf16[512,32,128]{2,1,0:T(8,128)(2,1)} %all-gather.5.cloned.1.call-done) | non-fusion elementwise | flops 2097152 | bytes 12582912 | tf_op jit(solution)/shard_map/convert_element_type | solution.py:89
  200.1 12.0 %multiply_reduce_fusion = (f32[32,16]{1,0:T(8,128)S(1)}, f32[32,16,128]{2,1,0:T(8,128)S(1)}) fusion(f32[512,16,128]{2,1,0:T(8,128)S(1)} %copy-done.1, f32[512,32,128]{2,1,0:T(8,128)S(1)} %convert_element_type.94), kind=kLoop, calls=%fused_computation | loop fusion | flops 100597248 | bytes 12847104 | tf_op jit(solution)/shard_map/reduce_sum | solution.py:8
  (45 shorter events, 7.6 us)
Async XLA Ops:
  6.5 60.8 %all-gather.3.cloned.1.call-start = ((), (), s32[]{:S(2)}) async-start(), calls=%async_computation.2 | async-start | bytes 2228224 | tf_op jit(solution)/shard_map/all_gather | solution.py:68
  10.9 31.1 %copy-start.3 = (bf16[32,16,128]{2,1,0:T(8,128)(2,1)S(1)}, bf16[32,16,128]{2,1,0:T(8,128)(2,1)}, u32[]{:S(2)}) copy-start(bf16[32,16,128]{2,1,0:T(8,128)(2,1)} %param.5) | copy-start | bytes 393220
  10.9 31.1 %copy-start.5 = (bf16[2,128,128]{2,1,0:T(8,128)(2,1)S(1)}, bf16[2,128,128]{2,1,0:T(8,128)(2,1)}, u32[]{:S(2)}) copy-start(bf16[2,128,128]{2,1,0:T(8,128)(2,1)} %param.8) | copy-start | bytes 196612
  11.7 7.1 %collective-permute-start = (bf16[32,16,128]{2,1,0:T(8,128)(2,1)S(1)}, bf16[32,16,128]{2,1,0:T(8,128)(2,1)S(1)}, u32[]{:S(2)}, u32[]{:S(2)}) collective-permute-start(bf16[32,16,128]{2,1,0:T(8,128)(2,1)S(1)} %get-tuple-element.18), channel_id=1, source_target_pairs={{0,0},{2,32},{4,64},{6,96},{8,128},{10,160},{12,192},{14,224},{16,... | collective-permute-start | bytes 393224 | tf_op jit(solution)/shard_map/ppermute | solution.py:38
  20.6 69.7 %all-to-all-start = ((bf16[16,16,32,128]{3,2,1,0:T(8,128)(2,1)}), bf16[16,16,32,128]{3,2,1,0:T(8,128)(2,1)S(1)}, u32[]{:S(2)}, u32[]{:S(2)}) async-start(bf16[16,16,32,128]{3,2,1,0:T(8,128)(2,1)} %broadcast_in_dim.4), calls=%async_computation | async-start | bytes 4194304 | tf_op jit(solution)/shard_map/all_to_all | solution.py:43
  41.9 154.7 %all-gather.5.cloned.1.call-start = ((), (), s32[]{:S(2)}) async-start(), calls=%async_computation.3 | async-start | bytes 4456448 | tf_op jit(solution)/shard_map/all_gather | solution.py:87
  90.3 2.2 copy-start
  90.6 7.5 %copy-start.2 = (bf16[256,32,128]{2,0,1:T(8,128)(2,1)S(1)}, bf16[256,32,128]{2,0,1:T(8,128)(2,1)}, u32[]{:S(2)}) copy-start(bf16[256,32,128]{2,0,1:T(8,128)(2,1)} %all-gather.3.cloned.1.call-done) | copy-start | bytes 6291460
  99.6 11.1 %copy-start.6 = (bf16[2,128,128]{2,1,0:T(8,128)(2,1)S(1)}, bf16[2,128,128]{2,1,0:T(8,128)(2,1)}, u32[]{:S(2)}) copy-start(bf16[2,128,128]{2,1,0:T(8,128)(2,1)} %param.9) | copy-start | bytes 196612
  99.6 11.8 %copy-start.4 = (bf16[2,128,512]{2,1,0:T(8,128)(2,1)S(1)}, bf16[2,128,512]{2,1,0:T(8,128)(2,1)}, u32[]{:S(2)}) copy-start(bf16[2,128,512]{2,1,0:T(8,128)(2,1)} %param.7) | copy-start | bytes 786436
  99.6 10.6 %collective-permute-start.1 = (bf16[32,16,128]{2,1,0:T(8,128)(2,1)S(1)}, bf16[32,16,128]{2,1,0:T(8,128)(2,1)S(1)}, u32[]{:S(2)}, u32[]{:S(2)}) collective-permute-start(bf16[32,16,128]{2,1,0:T(8,128)(2,1)S(1)} %multiply_reduce_fusion.3), channel_id=1, source_target_pairs={{0,1},{1,0},{2,3},{3,2},{4,5},{5,4},{6,7},{7,6},{8,9},{9,8},{10,11... | collective-permute-start | bytes 393224 | tf_op jit(solution)/shard_map/ppermute | solution.py:78
  111.9 6.8 %collective-permute-start.2 = (bf16[32,16,128]{2,1,0:T(8,128)(2,1)S(1)}, bf16[32,16,128]{2,1,0:T(8,128)(2,1)S(1)}, u32[]{:S(2)}, u32[]{:S(2)}) collective-permute-start(bf16[32,16,128]{2,1,0:T(8,128)(2,1)S(1)} %get-tuple-element.15), channel_id=1, source_target_pairs={{0,0},{2,32},{4,64},{6,96},{8,128},{10,160},{12,192},{14,224},{16,... | collective-permute-start | bytes 393224 | tf_op jit(solution)/shard_map/ppermute | solution.py:38
  118.6 7.2 %collective-permute-start.3 = (bf16[32,16,128]{2,1,0:T(8,128)(2,1)S(1)}, bf16[32,16,128]{2,1,0:T(8,128)(2,1)S(1)}, u32[]{:S(2)}, u32[]{:S(2)}) collective-permute-start(bf16[32,16,128]{2,1,0:T(8,128)(2,1)S(1)} %collective-permute-done.2), channel_id=1, source_target_pairs={{0,1},{1,0},{2,3},{3,2},{4,5},{5,4},{6,7},{7,6},{8,9},{9,8},{10,11... | collective-permute-start | bytes 393224 | tf_op jit(solution)/shard_map/ppermute | solution.py:59
  128.4 65.8 %all-to-all-start.1 = ((bf16[16,32,16,128]{3,2,1,0:T(8,128)(2,1)}), bf16[16,32,16,128]{3,2,1,0:T(8,128)(2,1)S(1)}, u32[]{:S(2)}, u32[]{:S(2)}) async-start(bf16[16,32,16,128]{3,2,1,0:T(8,128)(2,1)} %broadcast_in_dim.5), calls=%async_computation.1 | async-start | bytes 4194304 | tf_op jit(solution)/shard_map/all_to_all | solution.py:43
  196.5 3.5 %copy-start.1 = (f32[512,16,128]{2,1,0:T(8,128)S(1)}, f32[512,16,128]{2,1,0:T(8,128)}, u32[]{:S(2)}) copy-start(f32[512,16,128]{2,1,0:T(8,128)} %convert.1) | copy-start | bytes 12582916
Sparse Core Ops, SparseCore 0:
  16.4 50.9 all-gather.2
  126.8 57.7 all-gather.4

commit v11 on v10

--- a/solution.py
+++ b/solution.py
@@ -71,23 +71,19 @@
     me = lax.axis_index("ka")
     theirs = lax.dynamic_slice_in_dim(right_diag, (1 - me) * half, half, axis=1)
     mine = lax.dynamic_slice_in_dim(right_diag, me * half, half, axis=1)
-    sent = jnp.sum(
-        left_rows[:, :, None].astype(jnp.float32) * theirs[:, None].astype(jnp.float32), axis=0
-    ).astype(jnp.bfloat16)
+    sent = jnp.sum(left_rows[:, :, None] * theirs[:, None], axis=0, dtype=jnp.float32).astype(
+        jnp.bfloat16
+    )
     sent, left_later, mine = lax.optimization_barrier((sent, left_rows, mine))
     got = lax.ppermute(sent, "ka", [(0, 1), (1, 0)])
-    kept = jnp.sum(
-        left_later[:, :, None].astype(jnp.float32) * mine[:, None].astype(jnp.float32), axis=0
-    )
+    kept = jnp.sum(left_later[:, :, None] * mine[:, None], axis=0, dtype=jnp.float32)
     tri = kept + got.astype(jnp.float32)
     middle = finish(pair, tri, gate, w_out[0])
     left, right, gate = prepare(middle, valid, w_in[1], w_gate[1])
     right_cols = gather_a2a(right, "row", n, 0)
     left_tile = join_over_ka(transpose_tiles(left, n))
     left_diag = lax.all_gather(left_tile, "col", axis=0, tiled=True)
-    tri = jnp.sum(
-        left_diag[:, :, None].astype(jnp.float32) * right_cols[:, None].astype(jnp.float32), axis=0
-    )
+    tri = jnp.sum(left_diag[:, :, None] * right_cols[:, None], axis=0, dtype=jnp.float32)
     return finish(middle, tri, gate, w_out[1])
 
 

time: 222 us -> 221 us (level)
    convert_element_type x3 -> x0, other arithmetic: 5.98 us -> none  [the longest x1 3.52 us: on_device(): left_diag[:, :, None].astype(jnp.float32)]
    convert_element_type x2 -> x0, local copies, waits for them, and re-layouts: 5.95 us -> none  [the longest x1 4.73 us: on_device(): left_rows[:, :, None].astype(jnp.float32)]
    all_gather x0 -> x1, local copies, waits for them, and re-layouts: none -> 4.27 us  [on_device(): lax.all_gather(jnp.swapaxes(left, 0, 1), 'col', axis=0, tiled=True)]
    reduce_sum x3, other arithmetic: 13.1 us -> 16.5 us  [layer_norm(): mean = jnp.mean(value, axis=-1, keepdims=True)]
    reduce_sum x2, other arithmetic: 11.2 us -> 14.5 us  [the longest x1 7.24 us: on_device(): jnp.sum(left_rows[:, :, None] * theirs[:, None], axis=0, dtype=jnp.float32)]
  transfers between devices with their start and end apart: 8 -> 8, of which waited for: 6 -> 6; matrix products, arithmetic and copies ran while one was open for 8% -> 7% of each run, Pallas kernels for 0% -> 0%
where the time goes in v11:
time: 221 us; the launch traced here: 220 us
  waiting for transfers between devices  99.8 us (45%)
  starting transfers between devices  56.6 us (26%)
  other arithmetic  35.4 us (16%)
  between operations  13.7 us (6%)
  local copies, waits for them, and re-layouts  10.8 us (5%)
  matrix products  3.73 us (2%)
    all_to_all x2, waiting for transfers between devices, gather_a2a(): got = lax.all_to_all(copies, axis_name, 0, 0, tiled=False)  67 us
    all_to_all x2, starting transfers between devices, gather_a2a(): got = lax.all_to_all(copies, axis_name, 0, 0, tiled=False)  38.4 us
    all_gather x1, waiting for transfers between devices, on_device(): lax.all_gather(jnp.swapaxes(left, 0, 1), 'col', axis=0, tiled=True)  25.1 us
    reduce_sum x3, other arithmetic, layer_norm(): mean = jnp.mean(value, axis=-1, keepdims=True)  16.5 us
    ppermute x2, starting transfers between devices, transpose_tiles(): return lax.ppermute(value, ('row', 'col'), perm)  8.58 us
    reduce_sum x1, other arithmetic, on_device(): jnp.sum(left_rows[:, :, None] * theirs[:, None], axis=0, dtype=jnp.float32)  7.24 us
    reduce_sum x1, other arithmetic, on_device(): jnp.sum(left_later[:, :, None] * mine[:, None], axis=0, dtype=jnp.float32)  7.24 us
    ppermute x2, waiting for transfers between devices, transpose_tiles(): return lax.ppermute(value, ('row', 'col'), perm)  5.28 us
  transfers between devices with their start and end apart: 8, of which 6 were waited for; matrix products, arithmetic and copies ran while one was open for 7% of the time, Pallas kernels for 0%

profile of v11, /device:TPU:1, one launch (start us, length us, event | category | flops | bytes accessed | tf_op | source)
XLA Modules:
  0.0 220.1 jit_solution(6546879355600309622)
XLA Ops:
  6.5 1.0 convert_reduce_fusion.3
  7.6 1.1 fusion.13
  9.5 1.3 fusion.37
  11.7 4.5 %collective-permute-start = (bf16[32,16,128]{2,1,0:T(8,128)(2,1)S(1)}, bf16[32,16,128]{2,1,0:T(8,128)(2,1)S(1)}, u32[]{:S(2)}, u32[]{:S(2)}) collective-permute-start(bf16[32,16,128]{2,1,0:T(8,128)(2,1)S(1)} %get-tuple-element.18), channel_id=1, source_target_pairs={{0,0},{2,32},{4,64},{6,96},{8,128},{10,160},{12,192},{14,224},{16,... | collective-permute-start | bytes 393224 | tf_op jit(solution)/shard_map/ppermute | solution.py:38
  16.2 2.6 %collective-permute-done = bf16[32,16,128]{2,1,0:T(8,128)(2,1)S(1)} collective-permute-done((bf16[32,16,128]{2,1,0:T(8,128)(2,1)S(1)}, bf16[32,16,128]{2,1,0:T(8,128)(2,1)S(1)}, u32[]{:S(2)}, u32[]{:S(2)}) %collective-permute-start) | collective-permute-done | bytes 131104 | tf_op jit(solution)/shard_map/ppermute | solution.py:38
  18.9 1.7 broadcast_in_dim.4
  20.6 21.2 %all-to-all-start = ((bf16[16,16,32,128]{3,2,1,0:T(8,128)(2,1)}), bf16[16,16,32,128]{3,2,1,0:T(8,128)(2,1)S(1)}, u32[]{:S(2)}, u32[]{:S(2)}) async-start(bf16[16,16,32,128]{3,2,1,0:T(8,128)(2,1)} %broadcast_in_dim.4), calls=%async_computation | async-start | bytes 4194304 | tf_op jit(solution)/shard_map/all_to_all | solution.py:43
  42.2 25.1 %all-gather.3.cloned.1.call-done = bf16[256,32,128]{2,0,1:T(8,128)(2,1)} async-done(((bf16[16,32,128]{2,0,1:T(8,128)(2,1)}), bf16[256,32,128]{2,0,1:T(8,128)(2,1)}) %all-gather.3.cloned.1.call-update) | async-done | bytes 2097168 | tf_op jit(solution)/shard_map/all_gather | solution.py:68
  67.3 4.3 %copy.15 = bf16[256,32,128]{2,1,0:T(8,128)(2,1)} copy(bf16[256,32,128]{2,0,1:T(8,128)(2,1)} %all-gather.3.cloned.1.call-done) | data formatting | bytes 4194304 | tf_op jit(solution)/shard_map/all_gather | solution.py:68
  71.6 18.7 %all-to-all-done = bf16[16,16,32,128]{3,2,1,0:T(8,128)(2,1)S(1)} async-done(((bf16[16,16,32,128]{3,2,1,0:T(8,128)(2,1)}), bf16[16,16,32,128]{3,2,1,0:T(8,128)(2,1)S(1)}, u32[]{:S(2)}, u32[]{:S(2)}) %all-to-all-start) | async-done | bytes 2097184 | tf_op jit(solution)/shard_map/all_to_all | solution.py:43
  90.7 1.2 copy-done.1
  91.9 7.2 %multiply_reduce_fusion = bf16[32,16,128]{2,1,0:T(8,128)(2,1)S(1)} fusion(bf16[256,16,128]{2,1,0:T(8,128)(2,1)S(1)} %get-tuple-element.14, bf16[256,32,128]{2,1,0:T(8,128)(2,1)S(1)} %copy-done.1), kind=kLoop, calls=%fused_computation.3 | loop fusion | flops 33488896 | bytes 3276800 | tf_op jit(solution)/shard_map/reduce_sum | solution.py:74
  99.2 1.4 copy.17
  100.5 4.8 %collective-permute-start.1 = (bf16[32,16,128]{2,1,0:T(8,128)(2,1)S(1)}, bf16[32,16,128]{2,1,0:T(8,128)(2,1)S(1)}, u32[]{:S(2)}, u32[]{:S(2)}) collective-permute-start(bf16[32,16,128]{2,1,0:T(8,128)(2,1)S(1)} %multiply_reduce_fusion), channel_id=1, source_target_pairs={{0,1},{1,0},{2,3},{3,2},{4,5},{5,4},{6,7},{7,6},{8,9},{9,8},{10,11... | collective-permute-start | bytes 393224 | tf_op jit(solution)/shard_map/ppermute | solution.py:78
  105.4 7.2 %convert_reduce_fusion.2 = f32[32,16,128]{2,1,0:T(8,128)S(1)} fusion(bf16[256,16,128]{2,1,0:T(8,128)(2,1)S(1)} %get-tuple-element.9, bf16[256,32,128]{2,1,0:T(8,128)(2,1)S(1)} %copy.17), kind=kLoop, calls=%fused_computation.2 | loop fusion | flops 50266112 | bytes 3407872 | tf_op jit(solution)/shard_map/reduce_sum | solution.py:79
  114.3 4.1 %collective-permute-start.2 = (bf16[32,16,128]{2,1,0:T(8,128)(2,1)S(1)}, bf16[32,16,128]{2,1,0:T(8,128)(2,1)S(1)}, u32[]{:S(2)}, u32[]{:S(2)}) collective-permute-start(bf16[32,16,128]{2,1,0:T(8,128)(2,1)S(1)} %get-tuple-element.15), channel_id=1, source_target_pairs={{0,0},{2,32},{4,64},{6,96},{8,128},{10,160},{12,192},{14,224},{16,... | collective-permute-start | bytes 393224 | tf_op jit(solution)/shard_map/ppermute | solution.py:38
  118.4 2.7 %collective-permute-done.2 = bf16[32,16,128]{2,1,0:T(8,128)(2,1)S(1)} collective-permute-done((bf16[32,16,128]{2,1,0:T(8,128)(2,1)S(1)}, bf16[32,16,128]{2,1,0:T(8,128)(2,1)S(1)}, u32[]{:S(2)}, u32[]{:S(2)}) %collective-permute-start.2) | collective-permute-done | bytes 131104 | tf_op jit(solution)/shard_map/ppermute | solution.py:38
  121.1 4.8 %collective-permute-start.3 = (bf16[32,16,128]{2,1,0:T(8,128)(2,1)S(1)}, bf16[32,16,128]{2,1,0:T(8,128)(2,1)S(1)}, u32[]{:S(2)}, u32[]{:S(2)}) collective-permute-start(bf16[32,16,128]{2,1,0:T(8,128)(2,1)S(1)} %collective-permute-done.2), channel_id=1, source_target_pairs={{0,1},{1,0},{2,3},{3,2},{4,5},{5,4},{6,7},{7,6},{8,9},{9,8},{10,11... | collective-permute-start | bytes 393224 | tf_op jit(solution)/shard_map/ppermute | solution.py:59
  125.9 2.4 %collective-permute-done.3 = bf16[32,16,128]{2,1,0:T(8,128)(2,1)S(1)} collective-permute-done((bf16[32,16,128]{2,1,0:T(8,128)(2,1)S(1)}, bf16[32,16,128]{2,1,0:T(8,128)(2,1)S(1)}, u32[]{:S(2)}, u32[]{:S(2)}) %collective-permute-start.3) | collective-permute-done | bytes 131104 | tf_op jit(solution)/shard_map/ppermute | solution.py:59
  129.1 1.7 broadcast_in_dim.5
  130.9 17.1 %all-to-all-start.1 = ((bf16[16,32,16,128]{3,2,1,0:T(8,128)(2,1)}), bf16[16,32,16,128]{3,2,1,0:T(8,128)(2,1)S(1)}, u32[]{:S(2)}, u32[]{:S(2)}) async-start(bf16[16,32,16,128]{3,2,1,0:T(8,128)(2,1)} %broadcast_in_dim.5), calls=%async_computation.1 | async-start | bytes 4194304 | tf_op jit(solution)/shard_map/all_to_all | solution.py:43
  148.4 48.3 %all-to-all-done.1 = bf16[16,32,16,128]{3,2,1,0:T(8,128)(2,1)S(1)} async-done(((bf16[16,32,16,128]{3,2,1,0:T(8,128)(2,1)}), bf16[16,32,16,128]{3,2,1,0:T(8,128)(2,1)S(1)}, u32[]{:S(2)}, u32[]{:S(2)}) %all-to-all-start.1) | async-done | bytes 2097184 | tf_op jit(solution)/shard_map/all_to_all | solution.py:43
  196.7 15.3 %convert_reduce_fusion = (f32[32,16]{1,0:T(8,128)S(1)}, f32[32,16,128]{2,1,0:T(8,128)S(1)}) fusion(bf16[512,16,128]{2,1,0:T(8,128)(2,1)S(1)} %bitcast.31, bf16[512,32,128]{2,1,0:T(8,128)(2,1)} %all-gather.5.cloned.1.call-done), kind=kLoop, calls=%fused_computation | loop fusion | flops 134151680 | bytes 6555648 | tf_op jit(solution)/shard_map/reduce_sum | solution.py:8
  212.3 1.0 fusion.10
  (40 shorter events, 5.5 us)
Async XLA Ops:
  6.5 60.8 %all-gather.3.cloned.1.call-start = ((), (), s32[]{:S(2)}) async-start(), calls=%async_computation.2 | async-start | bytes 2228224 | tf_op jit(solution)/shard_map/all_gather | solution.py:68
  10.9 31.0 %copy-start.2 = (bf16[32,16,128]{2,1,0:T(8,128)(2,1)S(1)}, bf16[32,16,128]{2,1,0:T(8,128)(2,1)}, u32[]{:S(2)}) copy-start(bf16[32,16,128]{2,1,0:T(8,128)(2,1)} %param.5) | copy-start | bytes 393220
  10.9 31.0 %copy-start.4 = (bf16[2,128,128]{2,1,0:T(8,128)(2,1)S(1)}, bf16[2,128,128]{2,1,0:T(8,128)(2,1)}, u32[]{:S(2)}) copy-start(bf16[2,128,128]{2,1,0:T(8,128)(2,1)} %param.8) | copy-start | bytes 196612
  11.7 7.1 %collective-permute-start = (bf16[32,16,128]{2,1,0:T(8,128)(2,1)S(1)}, bf16[32,16,128]{2,1,0:T(8,128)(2,1)S(1)}, u32[]{:S(2)}, u32[]{:S(2)}) collective-permute-start(bf16[32,16,128]{2,1,0:T(8,128)(2,1)S(1)} %get-tuple-element.18), channel_id=1, source_target_pairs={{0,0},{2,32},{4,64},{6,96},{8,128},{10,160},{12,192},{14,224},{16,... | collective-permute-start | bytes 393224 | tf_op jit(solution)/shard_map/ppermute | solution.py:38
  20.6 69.7 %all-to-all-start = ((bf16[16,16,32,128]{3,2,1,0:T(8,128)(2,1)}), bf16[16,16,32,128]{3,2,1,0:T(8,128)(2,1)S(1)}, u32[]{:S(2)}, u32[]{:S(2)}) async-start(bf16[16,16,32,128]{3,2,1,0:T(8,128)(2,1)} %broadcast_in_dim.4), calls=%async_computation | async-start | bytes 4194304 | tf_op jit(solution)/shard_map/all_to_all | solution.py:43
  41.8 154.8 %all-gather.5.cloned.1.call-start = ((), (), s32[]{:S(2)}) async-start(), calls=%async_computation.3 | async-start | bytes 4456448 | tf_op jit(solution)/shard_map/all_gather | solution.py:85
  90.3 1.6 copy-start.1
  90.3 8.8 %copy-start = (bf16[256,32,128]{2,0,1:T(8,128)(2,1)S(1)}, bf16[256,32,128]{2,0,1:T(8,128)(2,1)}, u32[]{:S(2)}) copy-start(bf16[256,32,128]{2,0,1:T(8,128)(2,1)} %all-gather.3.cloned.1.call-done) | copy-start | bytes 6291460
  99.1 13.9 %copy-start.5 = (bf16[2,128,128]{2,1,0:T(8,128)(2,1)S(1)}, bf16[2,128,128]{2,1,0:T(8,128)(2,1)}, u32[]{:S(2)}) copy-start(bf16[2,128,128]{2,1,0:T(8,128)(2,1)} %param.9) | copy-start | bytes 196612
  99.1 14.6 %copy-start.3 = (bf16[2,128,512]{2,1,0:T(8,128)(2,1)S(1)}, bf16[2,128,512]{2,1,0:T(8,128)(2,1)}, u32[]{:S(2)}) copy-start(bf16[2,128,512]{2,1,0:T(8,128)(2,1)} %param.7) | copy-start | bytes 786436
  100.5 12.1 %collective-permute-start.1 = (bf16[32,16,128]{2,1,0:T(8,128)(2,1)S(1)}, bf16[32,16,128]{2,1,0:T(8,128)(2,1)S(1)}, u32[]{:S(2)}, u32[]{:S(2)}) collective-permute-start(bf16[32,16,128]{2,1,0:T(8,128)(2,1)S(1)} %multiply_reduce_fusion), channel_id=1, source_target_pairs={{0,1},{1,0},{2,3},{3,2},{4,5},{5,4},{6,7},{7,6},{8,9},{9,8},{10,11... | collective-permute-start | bytes 393224 | tf_op jit(solution)/shard_map/ppermute | solution.py:78
  114.3 6.8 %collective-permute-start.2 = (bf16[32,16,128]{2,1,0:T(8,128)(2,1)S(1)}, bf16[32,16,128]{2,1,0:T(8,128)(2,1)S(1)}, u32[]{:S(2)}, u32[]{:S(2)}) collective-permute-start(bf16[32,16,128]{2,1,0:T(8,128)(2,1)S(1)} %get-tuple-element.15), channel_id=1, source_target_pairs={{0,0},{2,32},{4,64},{6,96},{8,128},{10,160},{12,192},{14,224},{16,... | collective-permute-start | bytes 393224 | tf_op jit(solution)/shard_map/ppermute | solution.py:38
  121.1 7.2 %collective-permute-start.3 = (bf16[32,16,128]{2,1,0:T(8,128)(2,1)S(1)}, bf16[32,16,128]{2,1,0:T(8,128)(2,1)S(1)}, u32[]{:S(2)}, u32[]{:S(2)}) collective-permute-start(bf16[32,16,128]{2,1,0:T(8,128)(2,1)S(1)} %collective-permute-done.2), channel_id=1, source_target_pairs={{0,1},{1,0},{2,3},{3,2},{4,5},{5,4},{6,7},{7,6},{8,9},{9,8},{10,11... | collective-permute-start | bytes 393224 | tf_op jit(solution)/shard_map/ppermute | solution.py:59
  130.9 65.8 %all-to-all-start.1 = ((bf16[16,32,16,128]{3,2,1,0:T(8,128)(2,1)}), bf16[16,32,16,128]{3,2,1,0:T(8,128)(2,1)S(1)}, u32[]{:S(2)}, u32[]{:S(2)}) async-start(bf16[16,32,16,128]{3,2,1,0:T(8,128)(2,1)} %broadcast_in_dim.5), calls=%async_computation.1 | async-start | bytes 4194304 | tf_op jit(solution)/shard_map/all_to_all | solution.py:43
Sparse Core Ops, SparseCore 0:
  16.4 50.9 all-gather.2
  129.2 57.7 all-gather.4

commit v12 on v6

--- a/solution.py
+++ b/solution.py
@@ -65,12 +65,34 @@
 def on_device(n, pair, pair_mask, w_in, w_gate, w_out):
     valid = pair_mask.astype(jnp.float32)[..., None]
     left, right, gate = prepare(pair, valid, w_in[0], w_gate[0])
-    left_rows = lax.all_gather(left, "col", axis=1, tiled=True)
-    right_diag = gather_a2a(transpose_tiles(right, n), "row", n, 1)
-    partial_value = jnp.einsum(
-        "ikc,jkc->ijc", left_rows, right_diag, preferred_element_type=jnp.float32
+    few = 2
+    left_t = jnp.swapaxes(left, 0, 1)
+    right_t = jnp.swapaxes(transpose_tiles(right, n), 0, 1)
+    width = left_t.shape[0]
+    left_all = lax.all_gather(left_t, "col", axis=0, tiled=False)
+    right_few = lax.all_gather(right_t[:few], "row", axis=0, tiled=True)
+    right_rest = gather_a2a(right_t[few:], "row", n, 0)
+    left_few = left_all[:, :few].reshape((n * few,) + left_t.shape[1:])
+    left_rest = left_all[:, few:].reshape((n * (width - few),) + left_t.shape[1:])
+    half = right_t.shape[1] // 2
+    me = lax.axis_index("ka")
+
+    def part_sum(lhs, rhs, start):
+        cut = lax.dynamic_slice_in_dim(rhs, start, half, axis=1)
+        return jnp.sum(
+            lhs[:, :, None].astype(jnp.float32) * cut[:, None].astype(jnp.float32), axis=0
+        )
+
+    sent = (
+        part_sum(left_few, right_few, (1 - me) * half)
+        + part_sum(left_rest, right_rest, (1 - me) * half)
+    ).astype(jnp.bfloat16)
+    sent, left_few, left_rest, right_few, right_rest = lax.optimization_barrier(
+        (sent, left_few, left_rest, right_few, right_rest)
     )
-    tri = sum_over_ka(partial_value)
+    got = lax.ppermute(sent, "ka", [(0, 1), (1, 0)])
+    kept = part_sum(left_few, right_few, me * half) + part_sum(left_rest, right_rest, me * half)
+    tri = kept + got.astype(jnp.float32)
     middle = finish(pair, tri, gate, w_out[0])
     left, right, gate = prepare(middle, valid, w_in[1], w_gate[1])
     right_cols = gather_a2a(right, "row", n, 0)

time: 233 us -> 247 us (1.060)
  the two profiles are of different devices: /device:TPU:1 before, /device:TPU:4 now
where the time goes in v12:
time: 247 us
  blocking collectives  69.9 us (28%)
  starting transfers between devices  59.8 us (24%)
  waiting for transfers between devices  52 us (21%)
  other arithmetic  38.3 us (16%)
  between operations  13.9 us (6%)
  local copies, waits for them, and re-layouts  9.44 us (4%)
  matrix products  3.72 us (2%)
    all_gather x1, blocking collectives, on_device(): right_few = lax.all_gather(right_t[:few], 'row', axis=0, tiled=True)  69.9 us
    all_to_all x2, starting transfers between devices, gather_a2a(): got = lax.all_to_all(copies, axis_name, 0, 0, tiled=False)  51.2 us
    all_to_all x2, waiting for transfers between devices, gather_a2a(): got = lax.all_to_all(copies, axis_name, 0, 0, tiled=False)  48.2 us
    reduce_sum x3, other arithmetic, layer_norm(): mean = jnp.mean(value, axis=-1, keepdims=True)  13.1 us
    reduce_sum x4, other arithmetic, part_sum(): jnp.sum(lhs[:, :, None].astype(jnp.float32) * cut[:, None].astype(jnp.flo...  12 us
    ppermute x1, starting transfers between devices, join_over_ka(): got = lax.ppermute(value, 'ka', [(0, 1), (1, 0)])  5 us
  transfers between devices with their start and end apart: 8, of which 3 were waited for; matrix products, arithmetic and copies ran while one was open for 6% of the time, Pallas kernels for 0%

profile of v12, /device:TPU:4, one launch (start us, length us, event | category | flops | bytes accessed | tf_op | source)
XLA Modules:
  0.0 247.0 jit_solution(12047649266961668535)
XLA Ops:
  6.5 1.0 convert_reduce_fusion
  7.6 1.1 fusion.13
  9.5 1.3 fusion.37
  12.5 1.6 broadcast_in_dim.4
  14.1 26.6 %all-to-all-start = ((bf16[16,14,32,128]{3,2,1,0:T(8,128)(2,1)}), bf16[16,14,32,128]{3,2,1,0:T(8,128)(2,1)S(1)}, u32[]{:S(2)}, u32[]{:S(2)}) async-start(bf16[16,14,32,128]{3,2,1,0:T(8,128)(2,1)} %broadcast_in_dim.4), calls=%async_computation | async-start | bytes 3670016 | tf_op jit(solution)/shard_map/all_to_all | solution.py:43
  41.2 69.9 %all_gather.14 = bf16[32,32,128]{2,1,0:T(8,128)(2,1)S(1)} all-gather(bf16[2,32,128]{2,1,0:T(8,128)(2,1)S(1)} %copy.29), channel_id=1, replica_groups=mesh['row'=16,'col'=16,'ka'=2] {'row'}, dimensions={0}, use_global_device_ids=true | all-gather | bytes 278528 | tf_op jit(solution)/shard_map/all_gather | solution.py:73
  111.1 1.4 dynamic-slice_convert_fusion.1
  112.5 2.6 %slice.78 = bf16[16,14,32,128]{3,1,0,2:T(8,128)(2,1)S(1)} slice(bf16[16,16,32,128]{3,1,0,2:T(8,128)(2,1)} %bitcast.40), slice={[0:16], [2:16], [0:32], [0:128]} | slice | bytes 3670016 | tf_op jit(solution)/shard_map/slice | solution.py:76
  115.1 1.4 slice.74
  116.5 1.2 copy.33
  119.1 4.9 %multiply_reduce_fusion.3 = f32[32,16,128]{2,1,0:T(8,128)S(1)} fusion(f32[224,16,128]{2,1,0:T(8,128)S(1)} %copy-done.1, f32[224,32,128]{2,1,0:T(8,128)S(1)} %bitcast_convert_fusion), kind=kLoop, calls=%fused_computation.3 | loop fusion | flops 29294592 | bytes 5767168 | tf_op jit(solution)/shard_map/reduce_sum | solution.py:82
  124.1 1.1 multiply_reduce_fusion.5
  126.0 2.2 collective-permute-start.1
  128.3 4.9 %multiply_reduce_fusion.2 = f32[32,16,128]{2,1,0:T(8,128)S(1)} fusion(f32[224,16,128]{2,1,0:T(8,128)S(1)} %dynamic-slice_convert_fusion, f32[224,32,128]{2,1,0:T(8,128)S(1)} %convert_element_type.114), kind=kLoop, calls=%fused_computation.2 | loop fusion | flops 29294592 | bytes 5767168 | tf_op jit(solution)/shard_map/reduce_sum | solution.py:82
  133.2 1.1 multiply_reduce_fusion.4
  136.9 5.0 %collective-permute-start.3 = (bf16[32,16,128]{2,1,0:T(8,128)(2,1)S(1)}, bf16[32,16,128]{2,1,0:T(8,128)(2,1)S(1)}, u32[]{:S(2)}, u32[]{:S(2)}) collective-permute-start(bf16[32,16,128]{2,1,0:T(8,128)(2,1)S(1)} %collective-permute-done.2), channel_id=1, source_target_pairs={{0,1},{1,0},{2,3},{3,2},{4,5},{5,4},{6,7},{7,6},{8,9},{9,8},{10,11... | collective-permute-start | bytes 393224 | tf_op jit(solution)/shard_map/ppermute | solution.py:59
  141.9 3.5 %collective-permute-done.3 = bf16[32,16,128]{2,1,0:T(8,128)(2,1)S(1)} collective-permute-done((bf16[32,16,128]{2,1,0:T(8,128)(2,1)S(1)}, bf16[32,16,128]{2,1,0:T(8,128)(2,1)S(1)}, u32[]{:S(2)}, u32[]{:S(2)}) %collective-permute-start.3) | collective-permute-done | bytes 131104 | tf_op jit(solution)/shard_map/ppermute | solution.py:59
  146.2 1.7 broadcast_in_dim.5
  148.0 24.5 %all-to-all-start.1 = ((bf16[16,32,16,128]{3,2,1,0:T(8,128)(2,1)}), bf16[16,32,16,128]{3,2,1,0:T(8,128)(2,1)S(1)}, u32[]{:S(2)}, u32[]{:S(2)}) async-start(bf16[16,32,16,128]{3,2,1,0:T(8,128)(2,1)} %broadcast_in_dim.5), calls=%async_computation.1 | async-start | bytes 4194304 | tf_op jit(solution)/shard_map/all_to_all | solution.py:43
  172.8 48.2 %all-to-all-done.1 = bf16[16,32,16,128]{3,2,1,0:T(8,128)(2,1)S(1)} async-done(((bf16[16,32,16,128]{3,2,1,0:T(8,128)(2,1)}), bf16[16,32,16,128]{3,2,1,0:T(8,128)(2,1)S(1)}, u32[]{:S(2)}, u32[]{:S(2)}) %all-to-all-start.1) | async-done | bytes 2097184 | tf_op jit(solution)/shard_map/all_to_all | solution.py:43
  221.1 2.3 convert.1
  223.4 3.5 %convert_element_type.122 = f32[512,32,128]{2,1,0:T(8,128)S(1)} convert(bf16[512,32,128]{2,1,0:T(8,128)(2,1)} %all-gather.4.cloned.1.call-done) | non-fusion elementwise | flops 2097152 | bytes 12582912 | tf_op jit(solution)/shard_map/convert_element_type | solution.py:102
  226.9 12.0 %multiply_reduce_fusion = (f32[32,16]{1,0:T(8,128)S(1)}, f32[32,16,128]{2,1,0:T(8,128)S(1)}) fusion(f32[512,16,128]{2,1,0:T(8,128)S(1)} %copy-done, f32[512,32,128]{2,1,0:T(8,128)S(1)} %convert_element_type.122), kind=kLoop, calls=%fused_computation | loop fusion | flops 100597248 | bytes 12847104 | tf_op jit(solution)/shard_map/reduce_sum | solution.py:8
  239.2 1.0 fusion.10
  (57 shorter events, 9.0 us)
Async XLA Ops:
  6.5 105.9 %all-gather.6.cloned.1.call-start = ((), (), s32[]{:S(2)}) async-start(), calls=%async_computation.3 | async-start | bytes 2228224 | tf_op jit(solution)/shard_map/all_gather | solution.py:72
  10.9 29.9 %copy-start.2 = (bf16[32,16,128]{2,1,0:T(8,128)(2,1)S(1)}, bf16[32,16,128]{2,1,0:T(8,128)(2,1)}, u32[]{:S(2)}) copy-start(bf16[32,16,128]{2,1,0:T(8,128)(2,1)} %param.5) | copy-start | bytes 393220
  10.9 29.9 %copy-start.4 = (bf16[2,128,128]{2,1,0:T(8,128)(2,1)S(1)}, bf16[2,128,128]{2,1,0:T(8,128)(2,1)}, u32[]{:S(2)}) copy-start(bf16[2,128,128]{2,1,0:T(8,128)(2,1)} %param.8) | copy-start | bytes 196612
  11.8 0.7 collective-permute-start
  14.1 97.0 %all-to-all-start = ((bf16[16,14,32,128]{3,2,1,0:T(8,128)(2,1)}), bf16[16,14,32,128]{3,2,1,0:T(8,128)(2,1)S(1)}, u32[]{:S(2)}, u32[]{:S(2)}) async-start(bf16[16,14,32,128]{3,2,1,0:T(8,128)(2,1)} %broadcast_in_dim.4), calls=%async_computation | async-start | bytes 3670016 | tf_op jit(solution)/shard_map/all_to_all | solution.py:43
  40.8 182.6 %all-gather.4.cloned.1.call-start = ((), (), s32[]{:S(2)}) async-start(), calls=%async_computation.2 | async-start | bytes 4456448 | tf_op jit(solution)/shard_map/all_gather | solution.py:100
  117.6 1.5 copy-start.1
  126.0 9.0 %copy-start.5 = (bf16[2,128,128]{2,1,0:T(8,128)(2,1)S(1)}, bf16[2,128,128]{2,1,0:T(8,128)(2,1)}, u32[]{:S(2)}) copy-start(bf16[2,128,128]{2,1,0:T(8,128)(2,1)} %param.9) | copy-start | bytes 196612
  126.0 9.6 %copy-start.3 = (bf16[2,128,512]{2,1,0:T(8,128)(2,1)S(1)}, bf16[2,128,512]{2,1,0:T(8,128)(2,1)}, u32[]{:S(2)}) copy-start(bf16[2,128,512]{2,1,0:T(8,128)(2,1)} %param.7) | copy-start | bytes 786436
  126.0 8.5 %collective-permute-start.1 = (bf16[32,16,128]{2,1,0:T(8,128)(2,1)S(1)}, bf16[32,16,128]{2,1,0:T(8,128)(2,1)S(1)}, u32[]{:S(2)}, u32[]{:S(2)}) collective-permute-start(bf16[32,16,128]{2,1,0:T(8,128)(2,1)S(1)} %add_convert_fusion), channel_id=1, source_target_pairs={{0,1},{1,0},{2,3},{3,2},{4,5},{5,4},{6,7},{7,6},{8,9},{9,8},{10,11... | collective-permute-start | bytes 393224 | tf_op jit(solution)/shard_map/ppermute | solution.py:93
  136.2 0.7 collective-permute-start.2
  136.9 8.5 %collective-permute-start.3 = (bf16[32,16,128]{2,1,0:T(8,128)(2,1)S(1)}, bf16[32,16,128]{2,1,0:T(8,128)(2,1)S(1)}, u32[]{:S(2)}, u32[]{:S(2)}) collective-permute-start(bf16[32,16,128]{2,1,0:T(8,128)(2,1)S(1)} %collective-permute-done.2), channel_id=1, source_target_pairs={{0,1},{1,0},{2,3},{3,2},{4,5},{5,4},{6,7},{7,6},{8,9},{9,8},{10,11... | collective-permute-start | bytes 393224 | tf_op jit(solution)/shard_map/ppermute | solution.py:59
  148.0 73.1 %all-to-all-start.1 = ((bf16[16,32,16,128]{3,2,1,0:T(8,128)(2,1)}), bf16[16,32,16,128]{3,2,1,0:T(8,128)(2,1)S(1)}, u32[]{:S(2)}, u32[]{:S(2)}) async-start(bf16[16,32,16,128]{3,2,1,0:T(8,128)(2,1)} %broadcast_in_dim.5), calls=%async_computation.1 | async-start | bytes 4194304 | tf_op jit(solution)/shard_map/all_to_all | solution.py:43
  223.4 3.5 %copy-start = (f32[512,16,128]{2,1,0:T(8,128)S(1)}, f32[512,16,128]{2,1,0:T(8,128)}, u32[]{:S(2)}) copy-start(f32[512,16,128]{2,1,0:T(8,128)} %convert.1) | copy-start | bytes 12582916
Sparse Core Ops, SparseCore 0:
  11.9 51.8 all-gather.5
  146.4 62.1 all-gather.3

commit v13 on v10

--- a/solution.py
+++ b/solution.py
@@ -85,9 +85,7 @@
     right_cols = gather_a2a(right, "row", n, 0)
     left_tile = join_over_ka(transpose_tiles(left, n))
     left_diag = lax.all_gather(left_tile, "col", axis=0, tiled=True)
-    tri = jnp.sum(
-        left_diag[:, :, None].astype(jnp.float32) * right_cols[:, None].astype(jnp.float32), axis=0
-    )
+    tri = jnp.sum(left_diag[:, :, None] * right_cols[:, None], axis=0, dtype=jnp.float32)
     return finish(middle, tri, gate, w_out[1])
 
 

time: 222 us -> 219 us (0.986)
  other arithmetic: 35.1 us -> 32.7 us
    convert_element_type x2 -> x0, other arithmetic: 5.82 us -> none  [the longest x1 3.52 us: on_device(): left_diag[:, :, None].astype(jnp.float32)]
    reduce_sum x3, other arithmetic: 13.1 us -> 16.5 us  [layer_norm(): mean = jnp.mean(value, axis=-1, keepdims=True)]
  transfers between devices with their start and end apart: 8 -> 8, of which waited for: 6 -> 6; matrix products, arithmetic and copies ran while one was open for 8% -> 7% of each run, Pallas kernels for 0% -> 0%
where the time goes in v13:
time: 219 us; the launch traced here: 218 us
  waiting for transfers between devices  99.3 us (45%)
  starting transfers between devices  56.8 us (26%)
  other arithmetic  32.7 us (15%)
  between operations  13.7 us (6%)
  local copies, waits for them, and re-layouts  11.5 us (5%)
  matrix products  3.73 us (2%)
    all_to_all x2, waiting for transfers between devices, gather_a2a(): got = lax.all_to_all(copies, axis_name, 0, 0, tiled=False)  66.6 us
    all_to_all x2, starting transfers between devices, gather_a2a(): got = lax.all_to_all(copies, axis_name, 0, 0, tiled=False)  38.4 us
    all_gather x1, waiting for transfers between devices, on_device(): lax.all_gather(jnp.swapaxes(left, 0, 1), 'col', axis=0, tiled=True)  25 us
    reduce_sum x3, other arithmetic, layer_norm(): mean = jnp.mean(value, axis=-1, keepdims=True)  16.5 us
    ppermute x2, starting transfers between devices, transpose_tiles(): return lax.ppermute(value, ('row', 'col'), perm)  8.58 us
    reduce_sum x1, other arithmetic, on_device(): jnp.sum(left_rows[:, :, None].astype(jnp.float32) * theirs[:, None].astyp...  5.63 us
    reduce_sum x1, other arithmetic, on_device(): jnp.sum(left_later[:, :, None].astype(jnp.float32) * mine[:, None].astype...  5.62 us
    ppermute x2, waiting for transfers between devices, transpose_tiles(): return lax.ppermute(value, ('row', 'col'), perm)  5.27 us
  transfers between devices with their start and end apart: 8, of which 6 were waited for; matrix products, arithmetic and copies ran while one was open for 7% of the time, Pallas kernels for 0%

profile of v13, /device:TPU:1, one launch (start us, length us, event | category | flops | bytes accessed | tf_op | source)
XLA Modules:
  0.0 217.7 jit_solution(2915067116465360204)
XLA Ops:
  6.5 1.0 convert_reduce_fusion.2
  7.6 1.1 fusion.13
  9.5 1.3 fusion.37
  11.7 4.5 %collective-permute-start = (bf16[32,16,128]{2,1,0:T(8,128)(2,1)S(1)}, bf16[32,16,128]{2,1,0:T(8,128)(2,1)S(1)}, u32[]{:S(2)}, u32[]{:S(2)}) collective-permute-start(bf16[32,16,128]{2,1,0:T(8,128)(2,1)S(1)} %get-tuple-element.18), channel_id=1, source_target_pairs={{0,0},{2,32},{4,64},{6,96},{8,128},{10,160},{12,192},{14,224},{16,... | collective-permute-start | bytes 393224 | tf_op jit(solution)/shard_map/ppermute | solution.py:38
  16.2 2.6 %collective-permute-done = bf16[32,16,128]{2,1,0:T(8,128)(2,1)S(1)} collective-permute-done((bf16[32,16,128]{2,1,0:T(8,128)(2,1)S(1)}, bf16[32,16,128]{2,1,0:T(8,128)(2,1)S(1)}, u32[]{:S(2)}, u32[]{:S(2)}) %collective-permute-start) | collective-permute-done | bytes 131104 | tf_op jit(solution)/shard_map/ppermute | solution.py:38
  18.9 1.8 broadcast_in_dim.4
  20.6 21.2 %all-to-all-start = ((bf16[16,16,32,128]{3,2,1,0:T(8,128)(2,1)}), bf16[16,16,32,128]{3,2,1,0:T(8,128)(2,1)S(1)}, u32[]{:S(2)}, u32[]{:S(2)}) async-start(bf16[16,16,32,128]{3,2,1,0:T(8,128)(2,1)} %broadcast_in_dim.4), calls=%async_computation | async-start | bytes 4194304 | tf_op jit(solution)/shard_map/all_to_all | solution.py:43
  42.3 25.0 %all-gather.3.cloned.1.call-done = bf16[256,32,128]{2,0,1:T(8,128)(2,1)} async-done(((bf16[16,32,128]{2,0,1:T(8,128)(2,1)}), bf16[256,32,128]{2,0,1:T(8,128)(2,1)}) %all-gather.3.cloned.1.call-update) | async-done | bytes 2097168 | tf_op jit(solution)/shard_map/all_gather | solution.py:68
  67.3 4.7 %copy.15 = f32[256,32,128]{2,1,0:T(8,128)} copy(bf16[256,32,128]{2,0,1:T(8,128)(2,1)} %all-gather.3.cloned.1.call-done) | data formatting | bytes 6291456 | tf_op jit(solution)/shard_map/convert_element_type | solution.py:75
  72.1 18.3 %all-to-all-done = bf16[16,16,32,128]{3,2,1,0:T(8,128)(2,1)S(1)} async-done(((bf16[16,16,32,128]{3,2,1,0:T(8,128)(2,1)}), bf16[16,16,32,128]{3,2,1,0:T(8,128)(2,1)S(1)}, u32[]{:S(2)}, u32[]{:S(2)}) %all-to-all-start) | async-done | bytes 2097184 | tf_op jit(solution)/shard_map/all_to_all | solution.py:43
  90.6 1.9 copy-done
  92.5 5.6 %multiply_reduce_fusion.1 = bf16[32,16,128]{2,1,0:T(8,128)(2,1)S(1)} fusion(f32[256,16,128]{2,1,0:T(8,128)S(1)} %get-tuple-element.14, f32[256,32,128]{2,1,0:T(8,128)S(1)} %copy-done), kind=kLoop, calls=%fused_computation.3 | loop fusion | flops 33488896 | bytes 6422528 | tf_op jit(solution)/shard_map/reduce_sum | solution.py:74
  98.2 1.2 copy.17
  99.6 5.0 %collective-permute-start.1 = (bf16[32,16,128]{2,1,0:T(8,128)(2,1)S(1)}, bf16[32,16,128]{2,1,0:T(8,128)(2,1)S(1)}, u32[]{:S(2)}, u32[]{:S(2)}) collective-permute-start(bf16[32,16,128]{2,1,0:T(8,128)(2,1)S(1)} %multiply_reduce_fusion.1), channel_id=1, source_target_pairs={{0,1},{1,0},{2,3},{3,2},{4,5},{5,4},{6,7},{7,6},{8,9},{9,8},{10,11... | collective-permute-start | bytes 393224 | tf_op jit(solution)/shard_map/ppermute | solution.py:78
  104.6 5.6 %multiply_reduce_fusion = f32[32,16,128]{2,1,0:T(8,128)S(1)} fusion(f32[256,16,128]{2,1,0:T(8,128)S(1)} %convert_element_type.75, f32[256,32,128]{2,1,0:T(8,128)S(1)} %copy.17), kind=kLoop, calls=%fused_computation.2 | loop fusion | flops 33488896 | bytes 6553600 | tf_op jit(solution)/shard_map/reduce_sum | solution.py:79
  111.9 4.1 %collective-permute-start.2 = (bf16[32,16,128]{2,1,0:T(8,128)(2,1)S(1)}, bf16[32,16,128]{2,1,0:T(8,128)(2,1)S(1)}, u32[]{:S(2)}, u32[]{:S(2)}) collective-permute-start(bf16[32,16,128]{2,1,0:T(8,128)(2,1)S(1)} %get-tuple-element.15), channel_id=1, source_target_pairs={{0,0},{2,32},{4,64},{6,96},{8,128},{10,160},{12,192},{14,224},{16,... | collective-permute-start | bytes 393224 | tf_op jit(solution)/shard_map/ppermute | solution.py:38
  116.0 2.7 %collective-permute-done.2 = bf16[32,16,128]{2,1,0:T(8,128)(2,1)S(1)} collective-permute-done((bf16[32,16,128]{2,1,0:T(8,128)(2,1)S(1)}, bf16[32,16,128]{2,1,0:T(8,128)(2,1)S(1)}, u32[]{:S(2)}, u32[]{:S(2)}) %collective-permute-start.2) | collective-permute-done | bytes 131104 | tf_op jit(solution)/shard_map/ppermute | solution.py:38
  118.6 4.8 %collective-permute-start.3 = (bf16[32,16,128]{2,1,0:T(8,128)(2,1)S(1)}, bf16[32,16,128]{2,1,0:T(8,128)(2,1)S(1)}, u32[]{:S(2)}, u32[]{:S(2)}) collective-permute-start(bf16[32,16,128]{2,1,0:T(8,128)(2,1)S(1)} %collective-permute-done.2), channel_id=1, source_target_pairs={{0,1},{1,0},{2,3},{3,2},{4,5},{5,4},{6,7},{7,6},{8,9},{9,8},{10,11... | collective-permute-start | bytes 393224 | tf_op jit(solution)/shard_map/ppermute | solution.py:59
  123.5 2.4 %collective-permute-done.3 = bf16[32,16,128]{2,1,0:T(8,128)(2,1)S(1)} collective-permute-done((bf16[32,16,128]{2,1,0:T(8,128)(2,1)S(1)}, bf16[32,16,128]{2,1,0:T(8,128)(2,1)S(1)}, u32[]{:S(2)}, u32[]{:S(2)}) %collective-permute-start.3) | collective-permute-done | bytes 131104 | tf_op jit(solution)/shard_map/ppermute | solution.py:59
  126.7 1.7 broadcast_in_dim.5
  128.4 17.1 %all-to-all-start.1 = ((bf16[16,32,16,128]{3,2,1,0:T(8,128)(2,1)}), bf16[16,32,16,128]{3,2,1,0:T(8,128)(2,1)S(1)}, u32[]{:S(2)}, u32[]{:S(2)}) async-start(bf16[16,32,16,128]{3,2,1,0:T(8,128)(2,1)} %broadcast_in_dim.5), calls=%async_computation.1 | async-start | bytes 4194304 | tf_op jit(solution)/shard_map/all_to_all | solution.py:43
  145.9 48.3 %all-to-all-done.1 = bf16[16,32,16,128]{3,2,1,0:T(8,128)(2,1)S(1)} async-done(((bf16[16,32,16,128]{3,2,1,0:T(8,128)(2,1)}), bf16[16,32,16,128]{3,2,1,0:T(8,128)(2,1)S(1)}, u32[]{:S(2)}, u32[]{:S(2)}) %all-to-all-start.1) | async-done | bytes 2097184 | tf_op jit(solution)/shard_map/all_to_all | solution.py:43
  194.2 15.3 %convert_reduce_fusion = (f32[32,16]{1,0:T(8,128)S(1)}, f32[32,16,128]{2,1,0:T(8,128)S(1)}) fusion(bf16[512,16,128]{2,1,0:T(8,128)(2,1)S(1)} %bitcast.31, bf16[512,32,128]{2,1,0:T(8,128)(2,1)} %all-gather.5.cloned.1.call-done), kind=kLoop, calls=%fused_computation | loop fusion | flops 134151680 | bytes 6555648 | tf_op jit(solution)/shard_map/reduce_sum | solution.py:8
  209.9 1.0 fusion.10
  (41 shorter events, 5.5 us)
Async XLA Ops:
  6.5 60.8 %all-gather.3.cloned.1.call-start = ((), (), s32[]{:S(2)}) async-start(), calls=%async_computation.2 | async-start | bytes 2228224 | tf_op jit(solution)/shard_map/all_gather | solution.py:68
  10.9 31.1 %copy-start.2 = (bf16[32,16,128]{2,1,0:T(8,128)(2,1)S(1)}, bf16[32,16,128]{2,1,0:T(8,128)(2,1)}, u32[]{:S(2)}) copy-start(bf16[32,16,128]{2,1,0:T(8,128)(2,1)} %param.5) | copy-start | bytes 393220
  10.9 31.1 %copy-start.4 = (bf16[2,128,128]{2,1,0:T(8,128)(2,1)S(1)}, bf16[2,128,128]{2,1,0:T(8,128)(2,1)}, u32[]{:S(2)}) copy-start(bf16[2,128,128]{2,1,0:T(8,128)(2,1)} %param.8) | copy-start | bytes 196612
  11.7 7.1 %collective-permute-start = (bf16[32,16,128]{2,1,0:T(8,128)(2,1)S(1)}, bf16[32,16,128]{2,1,0:T(8,128)(2,1)S(1)}, u32[]{:S(2)}, u32[]{:S(2)}) collective-permute-start(bf16[32,16,128]{2,1,0:T(8,128)(2,1)S(1)} %get-tuple-element.18), channel_id=1, source_target_pairs={{0,0},{2,32},{4,64},{6,96},{8,128},{10,160},{12,192},{14,224},{16,... | collective-permute-start | bytes 393224 | tf_op jit(solution)/shard_map/ppermute | solution.py:38
  20.6 69.7 %all-to-all-start = ((bf16[16,16,32,128]{3,2,1,0:T(8,128)(2,1)}), bf16[16,16,32,128]{3,2,1,0:T(8,128)(2,1)S(1)}, u32[]{:S(2)}, u32[]{:S(2)}) async-start(bf16[16,16,32,128]{3,2,1,0:T(8,128)(2,1)} %broadcast_in_dim.4), calls=%async_computation | async-start | bytes 4194304 | tf_op jit(solution)/shard_map/all_to_all | solution.py:43
  41.9 152.4 %all-gather.5.cloned.1.call-start = ((), (), s32[]{:S(2)}) async-start(), calls=%async_computation.3 | async-start | bytes 4456448 | tf_op jit(solution)/shard_map/all_gather | solution.py:87
  90.3 2.2 %copy-start = (f32[256,32,128]{2,1,0:T(8,128)S(1)}, f32[256,32,128]{2,1,0:T(8,128)}, u32[]{:S(2)}) copy-start(f32[256,32,128]{2,1,0:T(8,128)} %copy.15) | copy-start | bytes 12582916
  90.6 7.5 %copy-start.1 = (bf16[256,32,128]{2,0,1:T(8,128)(2,1)S(1)}, bf16[256,32,128]{2,0,1:T(8,128)(2,1)}, u32[]{:S(2)}) copy-start(bf16[256,32,128]{2,0,1:T(8,128)(2,1)} %all-gather.3.cloned.1.call-done) | copy-start | bytes 6291460
  99.6 11.1 %copy-start.5 = (bf16[2,128,128]{2,1,0:T(8,128)(2,1)S(1)}, bf16[2,128,128]{2,1,0:T(8,128)(2,1)}, u32[]{:S(2)}) copy-start(bf16[2,128,128]{2,1,0:T(8,128)(2,1)} %param.9) | copy-start | bytes 196612
  99.6 11.8 %copy-start.3 = (bf16[2,128,512]{2,1,0:T(8,128)(2,1)S(1)}, bf16[2,128,512]{2,1,0:T(8,128)(2,1)}, u32[]{:S(2)}) copy-start(bf16[2,128,512]{2,1,0:T(8,128)(2,1)} %param.7) | copy-start | bytes 786436
  99.6 10.6 %collective-permute-start.1 = (bf16[32,16,128]{2,1,0:T(8,128)(2,1)S(1)}, bf16[32,16,128]{2,1,0:T(8,128)(2,1)S(1)}, u32[]{:S(2)}, u32[]{:S(2)}) collective-permute-start(bf16[32,16,128]{2,1,0:T(8,128)(2,1)S(1)} %multiply_reduce_fusion.1), channel_id=1, source_target_pairs={{0,1},{1,0},{2,3},{3,2},{4,5},{5,4},{6,7},{7,6},{8,9},{9,8},{10,11... | collective-permute-start | bytes 393224 | tf_op jit(solution)/shard_map/ppermute | solution.py:78
  111.9 6.8 %collective-permute-start.2 = (bf16[32,16,128]{2,1,0:T(8,128)(2,1)S(1)}, bf16[32,16,128]{2,1,0:T(8,128)(2,1)S(1)}, u32[]{:S(2)}, u32[]{:S(2)}) collective-permute-start(bf16[32,16,128]{2,1,0:T(8,128)(2,1)S(1)} %get-tuple-element.15), channel_id=1, source_target_pairs={{0,0},{2,32},{4,64},{6,96},{8,128},{10,160},{12,192},{14,224},{16,... | collective-permute-start | bytes 393224 | tf_op jit(solution)/shard_map/ppermute | solution.py:38
  118.6 7.2 %collective-permute-start.3 = (bf16[32,16,128]{2,1,0:T(8,128)(2,1)S(1)}, bf16[32,16,128]{2,1,0:T(8,128)(2,1)S(1)}, u32[]{:S(2)}, u32[]{:S(2)}) collective-permute-start(bf16[32,16,128]{2,1,0:T(8,128)(2,1)S(1)} %collective-permute-done.2), channel_id=1, source_target_pairs={{0,1},{1,0},{2,3},{3,2},{4,5},{5,4},{6,7},{7,6},{8,9},{9,8},{10,11... | collective-permute-start | bytes 393224 | tf_op jit(solution)/shard_map/ppermute | solution.py:59
  128.4 65.8 %all-to-all-start.1 = ((bf16[16,32,16,128]{3,2,1,0:T(8,128)(2,1)}), bf16[16,32,16,128]{3,2,1,0:T(8,128)(2,1)S(1)}, u32[]{:S(2)}, u32[]{:S(2)}) async-start(bf16[16,32,16,128]{3,2,1,0:T(8,128)(2,1)} %broadcast_in_dim.5), calls=%async_computation.1 | async-start | bytes 4194304 | tf_op jit(solution)/shard_map/all_to_all | solution.py:43
Sparse Core Ops, SparseCore 0:
  16.4 50.9 all-gather.2
  126.8 57.7 all-gather.4

commit v14 on v13

--- a/solution.py
+++ b/solution.py
@@ -62,6 +62,21 @@
     )
 
 
+def transposed_tile(value, n):
+    me = lax.axis_index("ka")
+    own = transpose_tiles(value, n)
+    perm = [
+        ((c * n + r) * 2 + 1 - k, (r * n + c) * 2 + k)
+        for r in range(n)
+        for c in range(n)
+        for k in range(2)
+    ]
+    other = lax.ppermute(value, ("row", "col", "ka"), perm)
+    return jnp.where(
+        me == 0, jnp.concatenate([own, other], axis=1), jnp.concatenate([other, own], axis=1)
+    )
+
+
 def on_device(n, pair, pair_mask, w_in, w_gate, w_out):
     valid = pair_mask.astype(jnp.float32)[..., None]
     left, right, gate = prepare(pair, valid, w_in[0], w_gate[0])
@@ -83,7 +98,7 @@
     middle = finish(pair, tri, gate, w_out[0])
     left, right, gate = prepare(middle, valid, w_in[1], w_gate[1])
     right_cols = gather_a2a(right, "row", n, 0)
-    left_tile = join_over_ka(transpose_tiles(left, n))
+    left_tile = transposed_tile(left, n)
     left_diag = lax.all_gather(left_tile, "col", axis=0, tiled=True)
     tri = jnp.sum(left_diag[:, :, None] * right_cols[:, None], axis=0, dtype=jnp.float32)
     return finish(middle, tri, gate, w_out[1])

time: 219 us -> 222 us (1.014)
  starting transfers between devices: 56.8 us -> 60.2 us
    all_to_all x2, starting transfers between devices: 38.4 us -> 44 us  [gather_a2a(): got = lax.all_to_all(copies, axis_name, 0, 0, tiled=False)]
    ppermute x1, waiting for transfers between devices: 2.4 us -> 5.64 us  [transposed_tile(): other = lax.ppermute(value, ('row', 'col', 'ka'), perm)]
    ppermute x2, waiting for transfers between devices: 5.27 us -> 2.63 us  [transpose_tiles(): return lax.ppermute(value, ('row', 'col'), perm)]
  transfers between devices with their start and end apart: 8 -> 8, of which waited for: 6 -> 5; matrix products, arithmetic and copies ran while one was open for 7% -> 7% of each run, Pallas kernels for 0% -> 0%
where the time goes in v14:
time: 222 us
  waiting for transfers between devices  100 us (45%)
  starting transfers between devices  60.2 us (27%)
  other arithmetic  32.7 us (15%)
  between operations  13.7 us (6%)
  local copies, waits for them, and re-layouts  11.5 us (5%)
  matrix products  3.73 us (2%)
    all_to_all x2, waiting for transfers between devices, gather_a2a(): got = lax.all_to_all(copies, axis_name, 0, 0, tiled=False)  66.7 us
    all_to_all x2, starting transfers between devices, gather_a2a(): got = lax.all_to_all(copies, axis_name, 0, 0, tiled=False)  44 us
    all_gather x1, waiting for transfers between devices, on_device(): lax.all_gather(jnp.swapaxes(left, 0, 1), 'col', axis=0, tiled=True)  25 us
    reduce_sum x3, other arithmetic, layer_norm(): mean = jnp.mean(value, axis=-1, keepdims=True)  16.5 us
    ppermute x2, starting transfers between devices, transpose_tiles(): return lax.ppermute(value, ('row', 'col'), perm)  8.58 us
    ppermute x1, waiting for transfers between devices, transposed_tile(): other = lax.ppermute(value, ('row', 'col', 'ka'), perm)  5.64 us
    reduce_sum x1, other arithmetic, on_device(): jnp.sum(left_rows[:, :, None].astype(jnp.float32) * theirs[:, None].astyp...  5.63 us
    reduce_sum x1, other arithmetic, on_device(): jnp.sum(left_later[:, :, None].astype(jnp.float32) * mine[:, None].astype...  5.62 us
  transfers between devices with their start and end apart: 8, of which 5 were waited for; matrix products, arithmetic and copies ran while one was open for 7% of the time, Pallas kernels for 0%

profile of v14, /device:TPU:1, one launch (start us, length us, event | category | flops | bytes accessed | tf_op | source)
XLA Modules:
  0.0 221.8 jit_solution(8474699214631152854)
XLA Ops:
  6.5 1.0 convert_reduce_fusion.2
  7.6 1.1 fusion.13
  9.5 1.3 fusion.37
  11.7 4.5 %collective-permute-start = (bf16[32,16,128]{2,1,0:T(8,128)(2,1)S(1)}, bf16[32,16,128]{2,1,0:T(8,128)(2,1)S(1)}, u32[]{:S(2)}, u32[]{:S(2)}) collective-permute-start(bf16[32,16,128]{2,1,0:T(8,128)(2,1)S(1)} %get-tuple-element.18), channel_id=1, source_target_pairs={{0,0},{2,32},{4,64},{6,96},{8,128},{10,160},{12,192},{14,224},{16,... | collective-permute-start | bytes 393224 | tf_op jit(solution)/shard_map/ppermute | solution.py:38
  16.2 2.6 %collective-permute-done = bf16[32,16,128]{2,1,0:T(8,128)(2,1)S(1)} collective-permute-done((bf16[32,16,128]{2,1,0:T(8,128)(2,1)S(1)}, bf16[32,16,128]{2,1,0:T(8,128)(2,1)S(1)}, u32[]{:S(2)}, u32[]{:S(2)}) %collective-permute-start) | collective-permute-done | bytes 131104 | tf_op jit(solution)/shard_map/ppermute | solution.py:38
  18.9 1.8 broadcast_in_dim.4
  20.6 21.2 %all-to-all-start = ((bf16[16,16,32,128]{3,2,1,0:T(8,128)(2,1)}), bf16[16,16,32,128]{3,2,1,0:T(8,128)(2,1)S(1)}, u32[]{:S(2)}, u32[]{:S(2)}) async-start(bf16[16,16,32,128]{3,2,1,0:T(8,128)(2,1)} %broadcast_in_dim.4), calls=%async_computation | async-start | bytes 4194304 | tf_op jit(solution)/shard_map/all_to_all | solution.py:43
  42.3 25.0 %all-gather.3.cloned.1.call-done = bf16[256,32,128]{2,0,1:T(8,128)(2,1)} async-done(((bf16[16,32,128]{2,0,1:T(8,128)(2,1)}), bf16[256,32,128]{2,0,1:T(8,128)(2,1)}) %all-gather.3.cloned.1.call-update) | async-done | bytes 2097168 | tf_op jit(solution)/shard_map/all_gather | solution.py:83
  67.3 4.7 %copy.15 = f32[256,32,128]{2,1,0:T(8,128)} copy(bf16[256,32,128]{2,0,1:T(8,128)(2,1)} %all-gather.3.cloned.1.call-done) | data formatting | bytes 6291456 | tf_op jit(solution)/shard_map/convert_element_type | solution.py:90
  72.1 18.3 %all-to-all-done = bf16[16,16,32,128]{3,2,1,0:T(8,128)(2,1)S(1)} async-done(((bf16[16,16,32,128]{3,2,1,0:T(8,128)(2,1)}), bf16[16,16,32,128]{3,2,1,0:T(8,128)(2,1)S(1)}, u32[]{:S(2)}, u32[]{:S(2)}) %all-to-all-start) | async-done | bytes 2097184 | tf_op jit(solution)/shard_map/all_to_all | solution.py:43
  90.6 1.9 copy-done
  92.5 5.6 %multiply_reduce_fusion.1 = bf16[32,16,128]{2,1,0:T(8,128)(2,1)S(1)} fusion(f32[256,16,128]{2,1,0:T(8,128)S(1)} %get-tuple-element.14, f32[256,32,128]{2,1,0:T(8,128)S(1)} %copy-done), kind=kLoop, calls=%fused_computation.3 | loop fusion | flops 33488896 | bytes 6422528 | tf_op jit(solution)/shard_map/reduce_sum | solution.py:89
  98.2 1.2 copy.17
  99.6 5.0 %collective-permute-start.1 = (bf16[32,16,128]{2,1,0:T(8,128)(2,1)S(1)}, bf16[32,16,128]{2,1,0:T(8,128)(2,1)S(1)}, u32[]{:S(2)}, u32[]{:S(2)}) collective-permute-start(bf16[32,16,128]{2,1,0:T(8,128)(2,1)S(1)} %multiply_reduce_fusion.1), channel_id=1, source_target_pairs={{0,1},{1,0},{2,3},{3,2},{4,5},{5,4},{6,7},{7,6},{8,9},{9,8},{10,11... | collective-permute-start | bytes 393224 | tf_op jit(solution)/shard_map/ppermute | solution.py:93
  104.6 5.6 %multiply_reduce_fusion = f32[32,16,128]{2,1,0:T(8,128)S(1)} fusion(f32[256,16,128]{2,1,0:T(8,128)S(1)} %convert_element_type.75, f32[256,32,128]{2,1,0:T(8,128)S(1)} %copy.17), kind=kLoop, calls=%fused_computation.2 | loop fusion | flops 33488896 | bytes 6553600 | tf_op jit(solution)/shard_map/reduce_sum | solution.py:94
  111.9 4.1 %collective-permute-start.2 = (bf16[32,16,128]{2,1,0:T(8,128)(2,1)S(1)}, bf16[32,16,128]{2,1,0:T(8,128)(2,1)S(1)}, u32[]{:S(2)}, u32[]{:S(2)}) collective-permute-start(bf16[32,16,128]{2,1,0:T(8,128)(2,1)S(1)} %get-tuple-element.15), channel_id=1, source_target_pairs={{0,0},{2,32},{4,64},{6,96},{8,128},{10,160},{12,192},{14,224},{16,... | collective-permute-start | bytes 393224 | tf_op jit(solution)/shard_map/ppermute | solution.py:38
  116.0 2.6 %collective-permute-start.3 = (bf16[32,16,128]{2,1,0:T(8,128)(2,1)S(1)}, bf16[32,16,128]{2,1,0:T(8,128)(2,1)S(1)}, u32[]{:S(2)}, u32[]{:S(2)}) collective-permute-start(bf16[32,16,128]{2,1,0:T(8,128)(2,1)S(1)} %get-tuple-element.15), channel_id=1, source_target_pairs={{1,0},{0,1},{33,2},{32,3},{65,4},{64,5},{97,6},{96,7},{129,8},{128... | collective-permute-start | bytes 393224 | tf_op jit(solution)/shard_map/ppermute | solution.py:74
  118.6 5.6 %collective-permute-done.3 = bf16[32,16,128]{2,1,0:T(8,128)(2,1)S(1)} collective-permute-done((bf16[32,16,128]{2,1,0:T(8,128)(2,1)S(1)}, bf16[32,16,128]{2,1,0:T(8,128)(2,1)S(1)}, u32[]{:S(2)}, u32[]{:S(2)}) %collective-permute-start.3) | collective-permute-done | bytes 131104 | tf_op jit(solution)/shard_map/ppermute | solution.py:74
  124.3 0.8 maximum_select_fusion
  125.1 1.7 broadcast_in_dim.5
  126.9 22.8 %all-to-all-start.1 = ((bf16[16,32,16,128]{3,2,1,0:T(8,128)(2,1)}), bf16[16,32,16,128]{3,2,1,0:T(8,128)(2,1)S(1)}, u32[]{:S(2)}, u32[]{:S(2)}) async-start(bf16[16,32,16,128]{3,2,1,0:T(8,128)(2,1)} %broadcast_in_dim.5), calls=%async_computation.1 | async-start | bytes 4194304 | tf_op jit(solution)/shard_map/all_to_all | solution.py:43
  150.0 48.4 %all-to-all-done.1 = bf16[16,32,16,128]{3,2,1,0:T(8,128)(2,1)S(1)} async-done(((bf16[16,32,16,128]{3,2,1,0:T(8,128)(2,1)}), bf16[16,32,16,128]{3,2,1,0:T(8,128)(2,1)S(1)}, u32[]{:S(2)}, u32[]{:S(2)}) %all-to-all-start.1) | async-done | bytes 2097184 | tf_op jit(solution)/shard_map/all_to_all | solution.py:43
  198.4 15.3 %convert_reduce_fusion = (f32[32,16]{1,0:T(8,128)S(1)}, f32[32,16,128]{2,1,0:T(8,128)S(1)}) fusion(bf16[512,16,128]{2,1,0:T(8,128)(2,1)S(1)} %bitcast.31, bf16[512,32,128]{2,1,0:T(8,128)(2,1)} %all-gather.5.cloned.1.call-done), kind=kLoop, calls=%fused_computation | loop fusion | flops 134151680 | bytes 6555648 | tf_op jit(solution)/shard_map/reduce_sum | solution.py:8
  214.0 1.0 fusion.10
  (41 shorter events, 4.7 us)
Async XLA Ops:
  6.5 60.8 %all-gather.3.cloned.1.call-start = ((), (), s32[]{:S(2)}) async-start(), calls=%async_computation.2 | async-start | bytes 2228224 | tf_op jit(solution)/shard_map/all_gather | solution.py:83
  10.9 31.1 %copy-start.2 = (bf16[32,16,128]{2,1,0:T(8,128)(2,1)S(1)}, bf16[32,16,128]{2,1,0:T(8,128)(2,1)}, u32[]{:S(2)}) copy-start(bf16[32,16,128]{2,1,0:T(8,128)(2,1)} %param.5) | copy-start | bytes 393220
  10.9 31.1 %copy-start.4 = (bf16[2,128,128]{2,1,0:T(8,128)(2,1)S(1)}, bf16[2,128,128]{2,1,0:T(8,128)(2,1)}, u32[]{:S(2)}) copy-start(bf16[2,128,128]{2,1,0:T(8,128)(2,1)} %param.8) | copy-start | bytes 196612
  11.7 7.1 %collective-permute-start = (bf16[32,16,128]{2,1,0:T(8,128)(2,1)S(1)}, bf16[32,16,128]{2,1,0:T(8,128)(2,1)S(1)}, u32[]{:S(2)}, u32[]{:S(2)}) collective-permute-start(bf16[32,16,128]{2,1,0:T(8,128)(2,1)S(1)} %get-tuple-element.18), channel_id=1, source_target_pairs={{0,0},{2,32},{4,64},{6,96},{8,128},{10,160},{12,192},{14,224},{16,... | collective-permute-start | bytes 393224 | tf_op jit(solution)/shard_map/ppermute | solution.py:38
  20.6 69.7 %all-to-all-start = ((bf16[16,16,32,128]{3,2,1,0:T(8,128)(2,1)}), bf16[16,16,32,128]{3,2,1,0:T(8,128)(2,1)S(1)}, u32[]{:S(2)}, u32[]{:S(2)}) async-start(bf16[16,16,32,128]{3,2,1,0:T(8,128)(2,1)} %broadcast_in_dim.4), calls=%async_computation | async-start | bytes 4194304 | tf_op jit(solution)/shard_map/all_to_all | solution.py:43
  41.9 156.5 %all-gather.5.cloned.1.call-start = ((), (), s32[]{:S(2)}) async-start(), calls=%async_computation.3 | async-start | bytes 4456448 | tf_op jit(solution)/shard_map/all_gather | solution.py:102
  90.3 2.2 copy-start
  90.6 7.5 %copy-start.1 = (bf16[256,32,128]{2,0,1:T(8,128)(2,1)S(1)}, bf16[256,32,128]{2,0,1:T(8,128)(2,1)}, u32[]{:S(2)}) copy-start(bf16[256,32,128]{2,0,1:T(8,128)(2,1)} %all-gather.3.cloned.1.call-done) | copy-start | bytes 6291460
  99.6 11.1 %copy-start.5 = (bf16[2,128,128]{2,1,0:T(8,128)(2,1)S(1)}, bf16[2,128,128]{2,1,0:T(8,128)(2,1)}, u32[]{:S(2)}) copy-start(bf16[2,128,128]{2,1,0:T(8,128)(2,1)} %param.9) | copy-start | bytes 196612
  99.6 11.8 %copy-start.3 = (bf16[2,128,512]{2,1,0:T(8,128)(2,1)S(1)}, bf16[2,128,512]{2,1,0:T(8,128)(2,1)}, u32[]{:S(2)}) copy-start(bf16[2,128,512]{2,1,0:T(8,128)(2,1)} %param.7) | copy-start | bytes 786436
  99.6 10.6 %collective-permute-start.1 = (bf16[32,16,128]{2,1,0:T(8,128)(2,1)S(1)}, bf16[32,16,128]{2,1,0:T(8,128)(2,1)S(1)}, u32[]{:S(2)}, u32[]{:S(2)}) collective-permute-start(bf16[32,16,128]{2,1,0:T(8,128)(2,1)S(1)} %multiply_reduce_fusion.1), channel_id=1, source_target_pairs={{0,1},{1,0},{2,3},{3,2},{4,5},{5,4},{6,7},{7,6},{8,9},{9,8},{10,11... | collective-permute-start | bytes 393224 | tf_op jit(solution)/shard_map/ppermute | solution.py:93
  111.9 6.8 %collective-permute-start.2 = (bf16[32,16,128]{2,1,0:T(8,128)(2,1)S(1)}, bf16[32,16,128]{2,1,0:T(8,128)(2,1)S(1)}, u32[]{:S(2)}, u32[]{:S(2)}) collective-permute-start(bf16[32,16,128]{2,1,0:T(8,128)(2,1)S(1)} %get-tuple-element.15), channel_id=1, source_target_pairs={{0,0},{2,32},{4,64},{6,96},{8,128},{10,160},{12,192},{14,224},{16,... | collective-permute-start | bytes 393224 | tf_op jit(solution)/shard_map/ppermute | solution.py:38
  116.0 8.3 %collective-permute-start.3 = (bf16[32,16,128]{2,1,0:T(8,128)(2,1)S(1)}, bf16[32,16,128]{2,1,0:T(8,128)(2,1)S(1)}, u32[]{:S(2)}, u32[]{:S(2)}) collective-permute-start(bf16[32,16,128]{2,1,0:T(8,128)(2,1)S(1)} %get-tuple-element.15), channel_id=1, source_target_pairs={{1,0},{0,1},{33,2},{32,3},{65,4},{64,5},{97,6},{96,7},{129,8},{128... | collective-permute-start | bytes 393224 | tf_op jit(solution)/shard_map/ppermute | solution.py:74
  126.9 71.5 %all-to-all-start.1 = ((bf16[16,32,16,128]{3,2,1,0:T(8,128)(2,1)}), bf16[16,32,16,128]{3,2,1,0:T(8,128)(2,1)S(1)}, u32[]{:S(2)}, u32[]{:S(2)}) async-start(bf16[16,32,16,128]{3,2,1,0:T(8,128)(2,1)} %broadcast_in_dim.5), calls=%async_computation.1 | async-start | bytes 4194304 | tf_op jit(solution)/shard_map/all_to_all | solution.py:43
Sparse Core Ops, SparseCore 0:
  16.4 50.9 all-gather.2
  125.3 63.1 all-gather.4
